TPU v7x, 32 devices: a whole 2x2x4 slice. The times are simulated.
32 devices in a mesh: expert: 16 (over z, y, x), shard: 2 (over core).
Axes of the slice: x: 2, y: 2, z: 4, core: 2. Of those that a mesh axis runs over, the one named last changes fastest.
Arguments:
- tokens_in: bfloat16 [4096, 2048], P(('expert', 'shard'))
- cotangent: bfloat16 [4096, 2048], P(('expert', 'shard')), may hold values from -6 to 6
- expert_ids: int32 [4096, 6], P(('expert', 'shard')), may hold values from 0 to 15, all different within a row; in each aligned block of 128 rows (0 to 127, 128 to 255, ...) at most 64 rows name the same one
- attention_gain: bfloat16 [2048], P(('expert', 'shard')), may hold values from 0.5 to 1.5
- query_weight: bfloat16 [2048, 3072], P(('expert', 'shard')), may hold values from -0.25 to 0.25
- latent_down: bfloat16 [2048, 576], P(('expert', 'shard')), may hold values from -0.125 to 0.125
- latent_gain: bfloat16 [512], P(('expert', 'shard')), may hold values from 0.5 to 1.5
- latent_up: bfloat16 [512, 4096], P(('expert', 'shard')), may hold values from -0.25 to 0.25
- output_weight: bfloat16 [2048, 2048], P(None, ('expert', 'shard')), may hold values from -0.375 to 0.375
- feedforward_gain: bfloat16 [2048], P(('expert', 'shard')), may hold values from 0.5 to 1.5
- router_weight: bfloat16 [2048, 16], P(('expert', 'shard')), may hold values from -0.0625 to 0.0625
- shared_inner: bfloat16 [2, 2048, 2816], P(None, ('expert', 'shard')), may hold values from -0.125 to 0.125
- shared_outer: bfloat16 [2816, 2048], P(None, ('expert', 'shard')), may hold values from -0.109375 to 0.109375
- expert_inner: bfloat16 [16, 2, 2048, 1408], P('expert', None, None, 'shard'), may hold values from -0.125 to 0.125
- expert_outer: bfloat16 [16, 1408, 2048], P('expert', 'shard'), may hold values from -3.5 to 3.5
Outputs:
- layer_output: bfloat16 [4096, 2048], P(('expert', 'shard'))
- input_gradient: bfloat16 [4096, 2048], P(('expert', 'shard'))
- attention_gain_delta: float32 [2048], P(('expert', 'shard'))
- query_delta: float32 [2048, 3072], P(('expert', 'shard'))
- latent_down_delta: float32 [2048, 576], P(('expert', 'shard'))
- latent_gain_delta: float32 [512], P(('expert', 'shard'))
- latent_up_delta: float32 [512, 4096], P(('expert', 'shard'))
- output_delta: float32 [2048, 2048], P(None, ('expert', 'shard'))
- feedforward_gain_delta: float32 [2048], P(('expert', 'shard'))
- router_delta: float32 [2048, 16], P(('expert', 'shard'))
- shared_inner_delta: float32 [2, 2048, 2816], P(None, ('expert', 'shard'))
- shared_outer_delta: float32 [2816, 2048], P(None, ('expert', 'shard'))
- expert_inner_delta: float32 [16, 2, 2048, 1408], P('expert', None, None, 'shard')
- expert_outer_delta: float32 [16, 1408, 2048], P('expert', 'shard')
- statistics: float32 [3], replicated
Inputs may be any that keep to these rules, and one draw needn't show every extreme that they name: `expert_ids`: each row names 6 different experts. In each aligned block of 128 rows (the rows of one device) no expert is named by more than 64 rows, a bound that some block reaches.
All inputs are finite; a program needn't handle non-finite values.
Results may differ from a plain program's by a relative error of at most 0.02.
Values may be sent and summed in bfloat16 or wider, within the bound.
No kernel may reach another device: no remote copies, remote signals or barrier semaphores. Data moves between devices by JAX's collectives and lax.ppermute only.
A program may use at most 448 MiB of HBM per device.

v0:
```python
import jax
import jax.numpy as jnp
from jax import lax
from jax.sharding import PartitionSpec as P

D = 2048
H = 16
DN = 128
DR = 64
DV = 128
KVR = 512
TOPK = 6
CL = 64


EPSILON = 1e-06
THETA = 10000.0


def passed_along(value, axis, steps):
    count = lax.axis_size(axis)
    first, last = (max(0, -steps), min(count, count - steps))
    return lax.ppermute(value, axis, [(source, source + steps) for source in range(first, last)])


def matmul(left_side, right_side):
    return jnp.dot(left_side, right_side, preferred_element_type=jnp.float32)


def norm_rows(values, gain_vector):
    return (
        values
        * lax.rsqrt(jnp.mean(values * values, axis=-1, keepdims=True) + EPSILON)
        * gain_vector
    )


def rotate(values, cosine_table, sine_table):
    middle = values.shape[-1] // 2
    first_half = values[..., :middle]
    second_half = values[..., middle:]
    return jnp.concatenate(
        [
            first_half * cosine_table - second_half * sine_table,
            second_half * cosine_table + first_half * sine_table,
        ],
        axis=-1,
    )


def angles(positions):
    inverse = THETA ** (-jnp.arange(DR // 2, dtype=jnp.float32) * 2.0 / DR)
    phases = positions.astype(jnp.float32)[:, None] * inverse[None, :]
    return (jnp.cos(phases), jnp.sin(phases))


def gated(inner_out):
    return jax.nn.silu(inner_out[..., 0, :]) * inner_out[..., 1, :]


def masked_scores(queries, key_rows, rotary_rows, visible):
    factor = (DN + DR) ** (-0.5)
    plain_part = jnp.einsum(
        "qhd,khd->hqk", queries[..., :DN], key_rows[..., :DN], preferred_element_type=jnp.float32
    )
    rotary_part = jnp.einsum(
        "qhr,kr->hqk", queries[..., DN:], rotary_rows, preferred_element_type=jnp.float32
    )
    return jnp.where(visible[None], (plain_part + rotary_part) * factor, -1e30)


def gather_attention(
    attention_gain, query_weight, latent_down, latent_gain, latent_up, output_weight
):
    return (
        lax.all_gather(attention_gain, ("expert", "shard"), axis=0, tiled=True),
        lax.all_gather(query_weight, ("expert", "shard"), axis=0, tiled=True),
        lax.all_gather(latent_down, ("expert", "shard"), axis=0, tiled=True),
        lax.all_gather(latent_gain, ("expert", "shard"), axis=0, tiled=True),
        lax.all_gather(latent_up, ("expert", "shard"), axis=0, tiled=True),
        lax.all_gather(output_weight, ("expert", "shard"), axis=1, tiled=True),
    )


def gather_feedforward(feedforward_gain, router_weight, shared_inner, shared_outer):
    return (
        lax.all_gather(feedforward_gain, ("expert", "shard"), axis=0, tiled=True),
        lax.all_gather(router_weight, ("expert", "shard"), axis=0, tiled=True),
        lax.all_gather(shared_inner, ("expert", "shard"), axis=1, tiled=True),
        lax.all_gather(shared_outer, ("expert", "shard"), axis=1, tiled=True),
    )


def shards(
    tokens_in,
    cotangent,
    expert_ids,
    attention_gain,
    query_weight,
    latent_down,
    latent_gain,
    latent_up,
    output_weight,
    feedforward_gain,
    router_weight,
    shared_inner,
    shared_outer,
    expert_inner,
    expert_outer,
):
    tok_rows = tokens_in.shape[0]
    experts_all = lax.axis_size("expert")
    slot_cap = tok_rows * TOPK * 4 // (3 * experts_all)
    factor = (DN + DR) ** (-0.5)
    side_index = lax.axis_index("shard")
    ordinal = jnp.arange(tok_rows, dtype=jnp.int32)
    positions = jnp.where(side_index == 0, ordinal, tok_rows + ordinal % CL)
    cosine_table, sine_table = angles(positions)
    query_place = ordinal[:, None]
    key_place = ordinal[None, :]
    causal = key_place <= query_place
    same_block = query_place // CL == key_place // CL
    local_mask = jnp.where(side_index == 0, causal, causal & same_block)
    remote_mask = jnp.broadcast_to(side_index == 1, (tok_rows, tok_rows))
    visible = jnp.concatenate([remote_mask, local_mask], axis=1)
    gain_one, query_full, down_full, gain_latent, up_full, output_full = gather_attention(
        attention_gain, query_weight, latent_down, latent_gain, latent_up, output_weight
    )
    tokens_float = tokens_in.astype(jnp.float32)
    gain_one_float = gain_one.astype(jnp.float32)
    normed_one = norm_rows(tokens_float, gain_one_float).astype(jnp.bfloat16)
    query_raw = matmul(normed_one, query_full).reshape(tok_rows, H, DN + DR)
    queries = jnp.concatenate(
        [
            query_raw[..., :DN],
            rotate(query_raw[..., DN:], cosine_table[:, None, :], sine_table[:, None, :]),
        ],
        axis=-1,
    ).astype(jnp.bfloat16)
    down_out = matmul(normed_one, down_full)
    latent_raw = down_out[:, :KVR]
    gain_latent_float = gain_latent.astype(jnp.float32)
    latents = norm_rows(latent_raw, gain_latent_float).astype(jnp.bfloat16)
    key_rotary = rotate(down_out[:, KVR:], cosine_table, sine_table).astype(jnp.bfloat16)
    expanded = matmul(latents, up_full).astype(jnp.bfloat16).reshape(tok_rows, H, DN + DV)
    remote_expanded, remote_rotary = passed_along((expanded, key_rotary), "shard", 1)
    key_rows = jnp.concatenate([remote_expanded, expanded], axis=0)
    rotary_rows = jnp.concatenate([remote_rotary, key_rotary], axis=0)
    scores = masked_scores(queries, key_rows, rotary_rows, visible)
    score_max = jnp.max(scores, axis=-1, keepdims=True)
    log_total = score_max + jnp.log(jnp.sum(jnp.exp(scores - score_max), axis=-1, keepdims=True))
    weights_low = jnp.exp(scores - log_total).astype(jnp.bfloat16)
    mixed_heads = (
        jnp.einsum(
            "hqk,khd->qhd", weights_low, key_rows[..., DN:], preferred_element_type=jnp.float32
        )
        .astype(jnp.bfloat16)
        .reshape(tok_rows, H * DV)
    )
    attention_out = matmul(mixed_heads, output_full)
    residual = tokens_float + attention_out
    gain_two, router_full, shared_in_full, shared_out_full = gather_feedforward(
        feedforward_gain, router_weight, shared_inner, shared_outer
    )
    gain_two_float = gain_two.astype(jnp.float32)
    normed_two = norm_rows(residual, gain_two_float).astype(jnp.bfloat16)
    logits = matmul(normed_two, router_full)
    route_probs = jax.nn.softmax(logits, axis=-1)
    gate_values = jnp.take_along_axis(route_probs, expert_ids, axis=1)
    flat_experts = expert_ids.reshape(-1)
    expert_match = (
        flat_experts[:, None] == jnp.arange(experts_all, dtype=jnp.int32)[None, :]
    ).astype(jnp.int32)
    slot_rank = jnp.sum((jnp.cumsum(expert_match, axis=0) - expert_match) * expert_match, axis=1)
    pair_count = tok_rows * TOPK
    slot_of = flat_experts * slot_cap + slot_rank
    slot_pair = (
        jnp.full((experts_all * slot_cap,), pair_count, jnp.int32)
        .at[slot_of]
        .set(jnp.arange(pair_count, dtype=jnp.int32))
    )
    slot_token = slot_pair // TOPK
    padded_rows = jnp.concatenate([normed_two, jnp.zeros((1, D), jnp.bfloat16)], axis=0)
    send_rows = jnp.take(padded_rows, slot_token, axis=0).reshape(experts_all, slot_cap, D)
    arrived = lax.all_to_all(send_rows, "expert", split_axis=0, concat_axis=0, tiled=True).reshape(
        -1, D
    )
    inner_full, outer_full = (
        lax.all_gather(expert_inner, "shard", axis=3, tiled=True),
        lax.all_gather(expert_outer, "shard", axis=1, tiled=True),
    )
    inner_matrix = inner_full[0]
    outer_matrix = outer_full[0]
    expert_pre = jnp.einsum(
        "rd,gdf->rgf", arrived, inner_matrix, preferred_element_type=jnp.float32
    )
    expert_hidden = gated(expert_pre).astype(jnp.bfloat16)
    expert_result = (
        matmul(expert_hidden, outer_matrix).astype(jnp.bfloat16).reshape(experts_all, slot_cap, D)
    )
    returned = lax.all_to_all(
        expert_result, "expert", split_axis=0, concat_axis=0, tiled=True
    ).reshape(-1, D)
    picked = jnp.take(returned, slot_of, axis=0).reshape(tok_rows, TOPK, D).astype(jnp.float32)
    routed = jnp.sum(gate_values[..., None] * picked, axis=1)
    shared_pre = jnp.einsum(
        "td,gdf->tgf", normed_two, shared_in_full, preferred_element_type=jnp.float32
    )
    shared_hidden = gated(shared_pre).astype(jnp.bfloat16)
    shared_result = matmul(shared_hidden, shared_out_full)
    feedforward = routed + shared_result
    layer_output = (residual + feedforward).astype(jnp.bfloat16)
    square_sums = lax.psum(
        (
            jnp.sum(residual * residual),
            jnp.sum(attention_out * attention_out),
            jnp.sum(feedforward * feedforward),
        ),
        ("expert", "shard"),
    )
    statistics = jnp.sqrt(
        jnp.stack(square_sums) / (tok_rows * D * experts_all * lax.axis_size("shard"))
    )
    held_ffn = lax.optimization_barrier(
        (feedforward_gain, router_weight, shared_inner, shared_outer, layer_output)
    )
    gain_two, router_full, shared_in_full, shared_out_full = gather_feedforward(
        held_ffn[0], held_ffn[1], held_ffn[2], held_ffn[3]
    )
    delta_out = cotangent.astype(jnp.float32)
    delta_shared_outer = jnp.einsum(
        "tf,td->fd", shared_hidden, cotangent, preferred_element_type=jnp.float32
    )
    delta_shared_hidden = jnp.einsum(
        "td,fd->tf", cotangent, shared_out_full, preferred_element_type=jnp.float32
    )
    unused_shared, shared_back = jax.vjp(gated, shared_pre)
    delta_shared_pre = shared_back(delta_shared_hidden)[0].astype(jnp.bfloat16)
    delta_shared_inner = jnp.einsum(
        "td,tgf->gdf", normed_two, delta_shared_pre, preferred_element_type=jnp.float32
    )
    delta_normed = jnp.einsum(
        "tgf,gdf->td", delta_shared_pre, shared_in_full, preferred_element_type=jnp.float32
    )
    delta_gates = jnp.sum(delta_out[:, None, :] * picked, axis=-1)
    padded_gates = jnp.concatenate([gate_values.reshape(-1), jnp.zeros((1,), jnp.float32)])
    slot_gate = jnp.take(padded_gates, slot_pair, axis=0)
    padded_delta = jnp.concatenate([delta_out, jnp.zeros((1, D), jnp.float32)], axis=0)
    send_delta = (
        (jnp.take(padded_delta, slot_token, axis=0) * slot_gate[:, None])
        .astype(jnp.bfloat16)
        .reshape(experts_all, slot_cap, D)
    )
    delta_arrived = lax.all_to_all(
        send_delta, "expert", split_axis=0, concat_axis=0, tiled=True
    ).reshape(-1, D)
    delta_outer_matrix = jnp.einsum(
        "rf,rd->fd", expert_hidden, delta_arrived, preferred_element_type=jnp.float32
    )
    delta_expert_hidden = jnp.einsum(
        "rd,fd->rf", delta_arrived, outer_matrix, preferred_element_type=jnp.float32
    )
    unused_expert, expert_back = jax.vjp(gated, expert_pre)
    delta_expert_pre = expert_back(delta_expert_hidden)[0].astype(jnp.bfloat16)
    delta_inner_matrix = jnp.einsum(
        "rd,rgf->gdf", arrived, delta_expert_pre, preferred_element_type=jnp.float32
    )
    delta_rows = (
        jnp.einsum(
            "rgf,gdf->rd", delta_expert_pre, inner_matrix, preferred_element_type=jnp.float32
        )
        .astype(jnp.bfloat16)
        .reshape(experts_all, slot_cap, D)
    )
    delta_expert_inner, delta_expert_outer = (
        lax.psum_scatter(
            delta_inner_matrix[None].astype(jnp.bfloat16), "shard", scatter_dimension=3, tiled=True
        ).astype(jnp.float32),
        lax.psum_scatter(
            delta_outer_matrix[None].astype(jnp.bfloat16), "shard", scatter_dimension=1, tiled=True
        ).astype(jnp.float32),
    )
    delta_returned = lax.all_to_all(
        delta_rows, "expert", split_axis=0, concat_axis=0, tiled=True
    ).reshape(-1, D)
    delta_normed = delta_normed + jnp.sum(
        jnp.take(delta_returned, slot_of, axis=0).reshape(tok_rows, TOPK, D).astype(jnp.float32),
        axis=1,
    )
    match_float = expert_match.reshape(tok_rows, TOPK, experts_all).astype(jnp.float32)
    delta_probs = jnp.einsum("tk,tke->te", delta_gates, match_float)
    delta_logits = (
        route_probs * (delta_probs - jnp.sum(route_probs * delta_probs, axis=-1, keepdims=True))
    ).astype(jnp.bfloat16)
    delta_router = jnp.einsum(
        "td,te->de", normed_two, delta_logits, preferred_element_type=jnp.float32
    )
    delta_normed = delta_normed + jnp.einsum(
        "te,de->td", delta_logits, router_full, preferred_element_type=jnp.float32
    )
    unused_second, second_back = jax.vjp(norm_rows, residual, gain_two_float)
    delta_residual_norm, delta_gain_two = second_back(delta_normed)
    delta_residual = delta_out + delta_residual_norm
    delta_ffn_set = (
        lax.psum_scatter(delta_gain_two, ("expert", "shard"), scatter_dimension=0, tiled=True),
        lax.psum_scatter(delta_router, ("expert", "shard"), scatter_dimension=0, tiled=True),
        lax.psum_scatter(delta_shared_inner, ("expert", "shard"), scatter_dimension=1, tiled=True),
        lax.psum_scatter(delta_shared_outer, ("expert", "shard"), scatter_dimension=1, tiled=True),
    )
    held_attention = lax.optimization_barrier(
        (
            attention_gain,
            query_weight,
            latent_down,
            latent_gain,
            latent_up,
            output_weight,
            delta_residual,
        )
    )
    gain_one, query_full, down_full, gain_latent, up_full, output_full = gather_attention(
        held_attention[0],
        held_attention[1],
        held_attention[2],
        held_attention[3],
        held_attention[4],
        held_attention[5],
    )
    delta_attention = delta_residual.astype(jnp.bfloat16)
    delta_output_weight = jnp.einsum(
        "tc,td->cd", mixed_heads, delta_attention, preferred_element_type=jnp.float32
    )
    delta_mixed = (
        jnp.einsum("td,cd->tc", delta_attention, output_full, preferred_element_type=jnp.float32)
        .astype(jnp.bfloat16)
        .reshape(tok_rows, H, DV)
    )
    scores_again = masked_scores(queries, key_rows, rotary_rows, visible)
    weights_again = jnp.exp(scores_again - log_total)
    delta_weights = jnp.einsum(
        "qhd,khd->hqk", delta_mixed, key_rows[..., DN:], preferred_element_type=jnp.float32
    )
    delta_scores = (
        weights_again
        * (delta_weights - jnp.sum(weights_again * delta_weights, axis=-1, keepdims=True))
    ).astype(jnp.bfloat16)
    delta_values = jnp.einsum(
        "hqk,qhd->khd",
        weights_again.astype(jnp.bfloat16),
        delta_mixed,
        preferred_element_type=jnp.float32,
    )
    delta_query_plain = (
        jnp.einsum(
            "hqk,khd->qhd", delta_scores, key_rows[..., :DN], preferred_element_type=jnp.float32
        )
        * factor
    )
    delta_query_rotary = (
        jnp.einsum("hqk,kr->qhr", delta_scores, rotary_rows, preferred_element_type=jnp.float32)
        * factor
    )
    delta_key_plain = (
        jnp.einsum(
            "hqk,qhd->khd", delta_scores, queries[..., :DN], preferred_element_type=jnp.float32
        )
        * factor
    )
    delta_key_rotary = (
        jnp.einsum(
            "hqk,qhr->kr", delta_scores, queries[..., DN:], preferred_element_type=jnp.float32
        )
        * factor
    )
    delta_key_rows = jnp.concatenate([delta_key_plain, delta_values], axis=-1)
    back_rows, back_rotary = (
        passed_along(delta_key_rows[:tok_rows].astype(jnp.bfloat16), "shard", -1).astype(
            jnp.float32
        ),
        passed_along(delta_key_rotary[:tok_rows].astype(jnp.bfloat16), "shard", -1).astype(
            jnp.float32
        ),
    )
    delta_expanded = (
        (delta_key_rows[tok_rows:] + back_rows)
        .astype(jnp.bfloat16)
        .reshape(tok_rows, H * (DN + DV))
    )
    delta_rotary_total = delta_key_rotary[tok_rows:] + back_rotary
    delta_latent_up = jnp.einsum(
        "tl,tc->lc", latents, delta_expanded, preferred_element_type=jnp.float32
    )
    delta_latents = jnp.einsum(
        "tc,lc->tl", delta_expanded, up_full, preferred_element_type=jnp.float32
    )
    unused_latent, latent_back = jax.vjp(norm_rows, latent_raw, gain_latent_float)
    delta_latent_raw, delta_gain_latent = latent_back(delta_latents)
    delta_down_out = jnp.concatenate(
        [delta_latent_raw, rotate(delta_rotary_total, cosine_table, -sine_table)], axis=-1
    ).astype(jnp.bfloat16)
    delta_latent_down = jnp.einsum(
        "td,tc->dc", normed_one, delta_down_out, preferred_element_type=jnp.float32
    )
    delta_query_raw = (
        jnp.concatenate(
            [
                delta_query_plain,
                rotate(delta_query_rotary, cosine_table[:, None, :], -sine_table[:, None, :]),
            ],
            axis=-1,
        )
        .astype(jnp.bfloat16)
        .reshape(tok_rows, H * (DN + DR))
    )
    delta_query_weight = jnp.einsum(
        "td,tc->dc", normed_one, delta_query_raw, preferred_element_type=jnp.float32
    )
    delta_normed_one = jnp.einsum(
        "tc,dc->td", delta_query_raw, query_full, preferred_element_type=jnp.float32
    ) + jnp.einsum("tc,dc->td", delta_down_out, down_full, preferred_element_type=jnp.float32)
    unused_first, first_back = jax.vjp(norm_rows, tokens_float, gain_one_float)
    delta_tokens_norm, delta_gain_one = first_back(delta_normed_one)
    input_gradient = (delta_residual + delta_tokens_norm).astype(jnp.bfloat16)
    delta_attention_set = (
        lax.psum_scatter(delta_gain_one, ("expert", "shard"), scatter_dimension=0, tiled=True),
        lax.psum_scatter(delta_query_weight, ("expert", "shard"), scatter_dimension=0, tiled=True),
        lax.psum_scatter(delta_latent_down, ("expert", "shard"), scatter_dimension=0, tiled=True),
        lax.psum_scatter(delta_gain_latent, ("expert", "shard"), scatter_dimension=0, tiled=True),
        lax.psum_scatter(delta_latent_up, ("expert", "shard"), scatter_dimension=0, tiled=True),
        lax.psum_scatter(delta_output_weight, ("expert", "shard"), scatter_dimension=1, tiled=True),
    )
    return (
        layer_output,
        input_gradient,
        delta_attention_set[0],
        delta_attention_set[1],
        delta_attention_set[2],
        delta_attention_set[3],
        delta_attention_set[4],
        delta_attention_set[5],
        delta_ffn_set[0],
        delta_ffn_set[1],
        delta_ffn_set[2],
        delta_ffn_set[3],
        delta_expert_inner,
        delta_expert_outer,
        statistics,
    )


def solution(mesh):
    return jax.shard_map(
        shards,
        mesh=mesh,
        in_specs=(
            P(("expert", "shard"), None),
            P(("expert", "shard"), None),
            P(("expert", "shard"), None),
            P(("expert", "shard")),
            P(("expert", "shard"), None),
            P(("expert", "shard"), None),
            P(("expert", "shard")),
            P(("expert", "shard"), None),
            P(None, ("expert", "shard")),
            P(("expert", "shard")),
            P(("expert", "shard"), None),
            P(None, ("expert", "shard"), None),
            P(None, ("expert", "shard")),
            P("expert", None, None, "shard"),
            P("expert", "shard", None),
        ),
        out_specs=(
            P(("expert", "shard"), None),
            P(("expert", "shard"), None),
            P(("expert", "shard")),
            P(("expert", "shard"), None),
            P(("expert", "shard"), None),
            P(("expert", "shard")),
            P(("expert", "shard"), None),
            P(None, ("expert", "shard")),
            P(("expert", "shard")),
            P(("expert", "shard"), None),
            P(None, ("expert", "shard"), None),
            P(None, ("expert", "shard")),
            P("expert", None, None, "shard"),
            P("expert", "shard", None),
            P(),
        ),
        check_vma=False,
    )
```

profile of v0, /device:TPU:0, one launch (start us, length us, event | category | flops | bytes accessed | tf_op | source)
XLA Modules:
  0.0 3416.7 jit_solution(499371561323982927)
XLA Ops:
  10.0 11.7 copy.124
  24.3 42.6 %all-reduce.15 = (bf16[2048]{0:T(1024)(128)(2,1)S(1)}, bf16[512]{0:T(512)(128)(2,1)S(1)}, bf16[2048]{0:T(1024)(128)(2,1)S(1)}) all-reduce(bf16[2048]{0:T(1024)(128)(2,1)S(1)} %dynamic-update-slice, bf16[512]{0:T(512)(128)(2,1)S(1)} %dynamic-update-slice.1, ...), channel_id=1, replica_groups=mesh['expert'=16,'shard'=2] {'expert','shard'}, use_global_device_ids=true, to_apply=%add.7 | all-reduce | flops 4608 | bytes 18432
  76.1 58.9 %all-gather.19.cloned.1.call-done = bf16[512,4096]{1,0:T(8,128)(2,1)} async-done(((bf16[16,4096]{1,0:T(8,128)(2,1)}), bf16[512,4096]{1,0:T(8,128)(2,1)}) %all-gather.19.cloned.1.call-update) | async-done | bytes 4194320 | tf_op jit(solution)/shard_map/all_gather | solution.py:80
  147.3 84.5 %all-gather.21.cloned.1.call-done = bf16[2048,3072]{1,0:T(8,128)(2,1)} async-done(((bf16[64,3072]{1,0:T(8,128)(2,1)}), bf16[2048,3072]{1,0:T(8,128)(2,1)}) %all-gather.21.cloned.1.call-update) | async-done | bytes 12582928 | tf_op jit(solution)/shard_map/all_gather | solution.py:77
  231.8 8.1 fusion.117
  243.4 66.8 %all-gather.23.cloned.1.call-done = bf16[2048,2048]{0,1:T(8,128)(2,1)} async-done(((bf16[2048,64]{0,1:T(8,128)(2,1)}), bf16[2048,2048]{0,1:T(8,128)(2,1)}) %all-gather.23.cloned.1.call-update) | async-done | bytes 8388624 | tf_op jit(solution)/shard_map/all_gather | solution.py:81
  310.2 7.0 multiply_reduce_fusion.8
  318.3 6.0 gather_fusion
  324.3 5.0 broadcast_select_fusion
  329.3 5.7 all-to-all-start
  335.1 29.0 copy.125
  364.1 85.7 %all-to-all-done = bf16[16,64,2048]{2,1,0:T(8,128)(2,1)} async-done(((bf16[16,64,2048]{2,1,0:T(8,128)(2,1)}), bf16[16,64,2048]{2,1,0:T(8,128)(2,1)}, u32[]{:S(2)}, u32[]{:S(2)}) %all-to-all-start) | async-done | bytes 4194336 | tf_op jit(solution)/shard_map/all_to_all | solution.py:185
  449.8 17.2 fusion.2
  474.0 10.8 fusion.19
  484.9 33.1 all-to-all-start.1
  518.3 130.4 %all-gather = bf16[32,64,16]{1,2,0:T(8,128)(2,1)S(1)} all-gather(bf16[1,64,16]{1,2,0:T(8,128)(2,1)S(1)} %bitcast.240), channel_id=1, replica_groups=mesh['expert'=16,'shard'=2] {'expert','shard'}, dimensions={0}, use_global_device_ids=true | all-gather | bytes 67584 | tf_op jit(solution)/shard_map/all_gather | solution.py:88
  649.0 6.8 gather_fusion.1
  660.1 8.2 mul.511
  668.7 9.1 gather_fusion.4
  682.2 5.1 gather_fusion.3
  692.5 5.2 multiply_convert_fusion
  697.7 17.0 all-to-all-start.2
  715.5 102.9 %all-to-all-done.2 = bf16[16,64,2048]{2,1,0:T(8,128)(2,1)} async-done(((bf16[16,64,2048]{2,1,0:T(8,128)(2,1)}), bf16[16,64,2048]{2,1,0:T(8,128)(2,1)}, u32[]{:S(2)}, u32[]{:S(2)}) %all-to-all-start.2) | async-done | bytes 4194336 | tf_op jit(solution)/shard_map/all_to_all | solution.py:254
  818.3 17.3 fusion.12
  835.6 19.3 bitcast_convert_fusion
  854.9 43.6 %all-to-all-start.3 = ((bf16[16,64,2048]{2,1,0:T(8,128)(2,1)}), bf16[16,64,2048]{2,1,0:T(8,128)(2,1)}, u32[]{:S(2)}, u32[]{:S(2)}) async-start(bf16[16,64,2048]{2,1,0:T(8,128)(2,1)} %bitcast.235), calls=%async_computation.3 | async-start | bytes 8388608 | tf_op jit(solution)/shard_map/all_to_all | solution.py:283
  898.8 9.4 fusion.55
  911.1 62.1 %all-to-all-done.3 = bf16[16,64,2048]{2,1,0:T(8,128)(2,1)} async-done(((bf16[16,64,2048]{2,1,0:T(8,128)(2,1)}), bf16[16,64,2048]{2,1,0:T(8,128)(2,1)}, u32[]{:S(2)}, u32[]{:S(2)}) %all-to-all-start.3) | async-done | bytes 4194336 | tf_op jit(solution)/shard_map/all_to_all | solution.py:283
  973.2 9.8 gather_fusion.5
  983.0 7.4 select_convert_fusion
  990.3 7.8 reshape.437
  998.2 6.7 multiply_reduce_fusion
  1005.0 9.5 multiply_reduce_fusion.3
  1015.5 7.8 reshape.438
  1023.3 7.1 reduce_sum.196
  1030.4 54.7 %all-gather.1 = bf16[32,64,16]{1,2,0:T(8,128)(2,1)S(1)} all-gather(bf16[1,64,16]{1,2,0:T(8,128)(2,1)S(1)} %bitcast.241), channel_id=1, replica_groups=mesh['expert'=16,'shard'=2] {'expert','shard'}, dimensions={0}, use_global_device_ids=true | all-gather | bytes 67584 | tf_op jit(solution)/shard_map/all_gather | solution.py:88
  1085.4 34.3 %all-gather.33.cloned.1.call-done = bf16[2816,2048]{0,1:T(8,128)(2,1)} async-done(((bf16[2816,64]{0,1:T(8,128)(2,1)}), bf16[2816,2048]{0,1:T(8,128)(2,1)}) %all-gather.33.cloned.1.call-update) | async-done | bytes 11534352 | tf_op jit(solution)/shard_map/all_gather | solution.py:90
  1119.6 8.3 multiply_bitcast_fusion.1
  1128.0 136.8 %all-gather.35.cloned.1.call-done = bf16[2,2048,2816]{2,1,0:T(8,128)(2,1)} async-done(((bf16[2,64,2816]{2,1,0:T(8,128)(2,1)}), bf16[2,2048,2816]{2,1,0:T(8,128)(2,1)}) %all-gather.35.cloned.1.call-update) | async-done | bytes 23068688 | tf_op jit(solution)/shard_map/all_gather | solution.py:89
  1264.8 13.3 fusion.24
  1284.1 10.5 fusion.4
  1294.8 19.9 convert_bitcast_fusion
  1314.8 20.8 convolution_bitcast_fusion
  1335.6 67.0 %copy.136 = f32[2,2048,2816]{2,0,1:T(2,128)} copy(f32[2,2048,2816]{1,2,0:T(8,128)} %convolution_bitcast_fusion) | data formatting | bytes 92274688 | tf_op jit(solution)/shard_map/td,tgf->gdf/transpose | solution.py:239
  1403.8 9.5 fusion.127
  1413.7 5.6 convolution_convert_fusion.2
  1440.6 9.2 fusion.63
  1449.8 5.8 fusion.113
  1458.8 10.3 fusion.115
  1469.1 88.8 %reduce-scatter.25.cloned.1.call-done = f32[64,16]{1,0:T(8,128)} async-done(((f32[2048,16]{1,0:T(8,128)}), f32[64,16]{1,0:T(8,128)}) %reduce-scatter.25.cloned.1.call-update) | async-done | bytes 4112
  1559.4 10.2 reduce-scatter.23.cloned.1.call-done
  1569.6 5.1 convert_element_type.202
  1574.7 17.7 reduce-scatter.21.cloned.1.call-done
  1592.4 8.7 convert_element_type.199
  1601.1 669.4 %all-reduce.18.cloned.1.call-done = f32[2,2048,2816]{2,0,1:T(2,128)} async-done(((f32[2,2048,2816]{2,0,1:T(2,128)}), f32[2,2048,2816]{2,0,1:T(2,128)}) %all-reduce.18.cloned.1.call-update) | async-done | bytes 46137360
  2273.1 94.1 %all-gather.39.cloned.1.call-done = bf16[2048,3072]{1,0:T(8,128)(2,1)} async-done(((bf16[64,3072]{1,0:T(8,128)(2,1)}), bf16[2048,3072]{1,0:T(8,128)(2,1)}) %all-gather.39.cloned.1.call-update) | async-done | bytes 12582928 | tf_op jit(solution)/shard_map/all_gather | solution.py:77
  2367.2 8.9 fusion.126
  2376.2 50.0 %all-gather.43.cloned.1.call-done = bf16[2048,576]{1,0:T(8,128)(2,1)} async-done(((bf16[64,576]{1,0:T(8,128)(2,1)}), bf16[2048,576]{1,0:T(8,128)(2,1)}) %all-gather.43.cloned.1.call-update) | async-done | bytes 2359312 | tf_op jit(solution)/shard_map/all_gather | solution.py:78
  2430.0 48.4 %all-reduce.14 = (f32[2048]{0:T(1024)S(1)}, f32[512]{0:T(512)S(1)}, f32[2048]{0:T(1024)S(1)}, f32[1]{0:T(128)}, f32[1]{0:T(128)}, /*index=5*/f32[1]{0:T(128)}) all-reduce(f32[2048]{0:T(1024)S(1)} %get-tuple-element.92, f32[512]{0:T(512)S(1)} %copy-done.62, ...), channel_id=2, replica_groups=mesh['expert'=16,'shard'=2] {'expert','shard'}, use_global_device_ids=true, to_apply=%region_20.22.clone | all-reduce | flops 4611 | bytes 36888
  2485.1 190.0 %reduce-scatter.19.cloned.1.call-done = f32[2816,64]{0,1:T(8,128)} async-done(((f32[2816,2048]{0,1:T(8,128)}), f32[2816,64]{0,1:T(8,128)}) %reduce-scatter.19.cloned.1.call-update) | async-done | bytes 720912 | tf_op jit(solution)/shard_map/reduce_scatter | solution.py:308
  2675.1 152.4 %reduce-scatter.13.cloned.1.call-done = f32[64,576]{1,0:T(8,128)} async-done(((f32[2048,576]{1,0:T(8,128)}), f32[64,576]{1,0:T(8,128)}) %reduce-scatter.13.cloned.1.call-update) | async-done | bytes 147472 | tf_op jit(solution)/shard_map/reduce_scatter | solution.py:427
  2827.5 181.7 %reduce-scatter.17.cloned.1.call-done = f32[2048,64]{0,1:T(8,128)} async-done(((f32[2048,2048]{0,1:T(8,128)}), f32[2048,64]{0,1:T(8,128)}) %reduce-scatter.17.cloned.1.call-update) | async-done | bytes 524304 | tf_op jit(solution)/shard_map/reduce_scatter | solution.py:430
  3009.2 154.5 %reduce-scatter.15.cloned.1.call-done = f32[16,4096]{1,0:T(8,128)} async-done(((f32[512,4096]{1,0:T(8,128)}), f32[16,4096]{1,0:T(8,128)}) %reduce-scatter.15.cloned.1.call-update) | async-done | bytes 262160 | tf_op jit(solution)/shard_map/reduce_scatter | solution.py:429
  3163.7 246.0 %reduce-scatter.11.cloned.1.call-done = f32[64,3072]{1,0:T(8,128)} async-done(((f32[2048,3072]{1,0:T(8,128)}), f32[64,3072]{1,0:T(8,128)}) %reduce-scatter.11.cloned.1.call-update) | async-done | bytes 786448 | tf_op jit(solution)/shard_map/reduce_scatter | solution.py:426
  (328 shorter events, 104.0 us)
Async XLA Ops:
  7.2 65.9 %all-gather.17.cloned.1.call-start = ((), (), s32[]{:S(2)}) async-start(), calls=%async_computation.12 | async-start | bytes 2703360 | tf_op jit(solution)/shard_map/all_gather | solution.py:78
  7.9 127.0 %all-gather.19.cloned.1.call-start = ((), (), s32[]{:S(2)}) async-start(), calls=%async_computation.13 | async-start | bytes 4325376 | tf_op jit(solution)/shard_map/all_gather | solution.py:80
  8.7 223.1 %all-gather.21.cloned.1.call-start = ((), (), s32[]{:S(2)}) async-start(), calls=%async_computation.14 | async-start | bytes 12976128 | tf_op jit(solution)/shard_map/all_gather | solution.py:77
  9.4 300.8 %all-gather.23.cloned.1.call-start = ((), (), s32[]{:S(2)}) async-start(), calls=%async_computation.15 | async-start | bytes 8650752 | tf_op jit(solution)/shard_map/all_gather | solution.py:81
  10.0 325.1 %all-gather.25.cloned.1.call-start = ((), (), s32[]{:S(2)}) async-start(), calls=%async_computation.16 | async-start | bytes 17301504 | tf_op jit(solution)/shard_map/all_gather | solution.py:189
  21.8 51.0 %copy-start.2 = (bf16[128,2048]{1,0:T(8,128)(2,1)S(1)}, bf16[128,2048]{1,0:T(8,128)(2,1)}, u32[]{:S(2)}) copy-start(bf16[128,2048]{1,0:T(8,128)(2,1)} %param.17) | copy-start | bytes 1572868
  21.8 452.2 %all-gather.27.cloned.1.call-start = ((), (), s32[]{:S(2)}) async-start(), calls=%async_computation.17 | async-start | bytes 8650752 | tf_op jit(solution)/shard_map/all_gather | solution.py:190
  22.4 876.4 %all-gather.29.cloned.1.call-start = ((), (), s32[]{:S(2)}) async-start(), calls=%async_computation.18 | async-start | bytes 23789568 | tf_op jit(solution)/shard_map/all_gather | solution.py:89
  67.0 71.0 %copy-start.44 = (f32[512]{0:T(512)}, f32[512]{0:T(512)S(1)}, u32[]{:S(2)}) copy-start(f32[512]{0:T(512)S(1)} %convert_element_type.159) | copy-start | bytes 6148
  67.0 164.8 %copy-start.32 = (f32[2048]{0:T(1024)}, f32[2048]{0:T(1024)S(1)}, u32[]{:S(2)}) copy-start(f32[2048]{0:T(1024)S(1)} %convert_element_type.157) | copy-start | bytes 24580
  73.0 158.8 %copy-start.51 = (f32[128]{0:T(128)}, f32[128]{0:T(128)S(1)}, u32[]{:S(2)}) copy-start(f32[128]{0:T(128)S(1)} %fusion.101) | copy-start | bytes 1540
  76.0 68.6 %copy-start.21 = (f32[128,576]{0,1:T(8,128)}, f32[128,576]{0,1:T(8,128)S(1)}, u32[]{:S(2)}) copy-start(f32[128,576]{0,1:T(8,128)S(1)} %fusion.119) | copy-start | bytes 884740
  76.0 66.2 %copy-start.69 = (f32[128]{0:T(128)}, f32[128]{0:T(128)S(1)}, u32[]{:S(2)}) copy-start(f32[128]{0:T(128)S(1)} %multiply_reduce_fusion.11) | copy-start | bytes 1540
  76.1 66.2 %copy-start.58 = (f32[128]{0:T(128)}, f32[128]{0:T(128)S(1)}, u32[]{:S(2)}) copy-start(f32[128]{0:T(128)S(1)} %fusion.102) | copy-start | bytes 1540
  139.1 5.5 collective-permute-start
  142.2 174.9 %copy-start.38 = (f32[2048]{0:T(1024)}, f32[2048]{0:T(1024)S(1)}, u32[]{:S(2)}) copy-start(f32[2048]{0:T(1024)S(1)} %convert_element_type.166) | copy-start | bytes 24580
  142.5 97.4 %copy-start.63 = (f32[128]{0:T(128)}, f32[128]{0:T(128)S(1)}, u32[]{:S(2)}) copy-start(f32[128]{0:T(128)S(1)} %fusion.100) | copy-start | bytes 1540
  142.7 97.2 %copy-start.36 = (f32[128,32]{0,1:T(8,128)}, f32[128,32]{0,1:T(8,128)S(1)}, u32[]{:S(2)}) copy-start(f32[128,32]{0,1:T(8,128)S(1)} %get-tuple-element.133) | copy-start | bytes 49156
  142.7 97.3 %copy-start.40 = (bf16[128,32]{0,1:T(8,128)(2,1)}, bf16[128,32]{0,1:T(8,128)(2,1)S(1)}, u32[]{:S(2)}) copy-start(bf16[128,32]{0,1:T(8,128)(2,1)S(1)} %get-tuple-element.123) | copy-start | bytes 24580
  142.7 97.3 %copy-start.42 = (bf16[128,32]{0,1:T(8,128)(2,1)}, bf16[128,32]{0,1:T(8,128)(2,1)S(1)}, u32[]{:S(2)}) copy-start(bf16[128,32]{0,1:T(8,128)(2,1)S(1)} %get-tuple-element.124) | copy-start | bytes 24580
  143.1 96.9 %collective-permute-start.1 = (bf16[128,64]{0,1:T(8,128)(2,1)S(1)}, bf16[128,64]{0,1:T(8,128)(2,1)S(1)}, u32[]{:S(2)}, u32[]{:S(2)}) collective-permute-start(bf16[128,64]{0,1:T(8,128)(2,1)S(1)} %pad_maximum_fusion.8), channel_id=1, source_target_pairs={{0,1},{2,3},{4,5},{6,7},{8,9},{10,11},{12,13},{14,15},{16,17},{18,... | collective-permute-start | bytes 49160 | tf_op jit(solution)/shard_map/ppermute | solution.py:23
  147.3 94.7 %copy-start.11 = (bf16[256,16,256]{2,0,1:T(8,128)(2,1)}, bf16[256,16,256]{2,0,1:T(8,128)(2,1)S(1)}, u32[]{:S(2)}) copy-start(bf16[256,16,256]{2,0,1:T(8,128)(2,1)S(1)} %constant_dynamic-update-slice_fusion) | copy-start | bytes 6291460
  242.6 74.6 %copy-start.34 = (f32[16,128]{1,0:T(8,128)}, f32[16,128]{1,0:T(8,128)S(1)}, u32[]{:S(2)}) copy-start(f32[16,128]{1,0:T(8,128)S(1)} %log_add_fusion) | copy-start | bytes 24580
  243.4 73.8 %copy-start.26 = (bf16[16,128,128]{2,1,0:T(8,128)(2,1)}, bf16[16,128,128]{2,1,0:T(8,128)(2,1)S(1)}, u32[]{:S(2)}) copy-start(bf16[16,128,128]{2,1,0:T(8,128)(2,1)S(1)} %convolution_convert_fusion.3) | copy-start | bytes 1572868
  317.2 7.2 copy-start.71
  317.2 7.1 copy-start.60
  318.3 350.1 %copy-start.9 = (bf16[128,2048]{1,0:T(8,128)(2,1)}, bf16[128,2048]{1,0:T(8,128)(2,1)S(1)}, u32[]{:S(2)}) copy-start(bf16[128,2048]{1,0:T(8,128)(2,1)S(1)} %multiply_convert_fusion.4) | copy-start | bytes 1572868
  329.3 120.4 %all-to-all-start = ((bf16[16,64,2048]{2,1,0:T(8,128)(2,1)}), bf16[16,64,2048]{2,1,0:T(8,128)(2,1)}, u32[]{:S(2)}, u32[]{:S(2)}) async-start(bf16[16,64,2048]{2,1,0:T(8,128)(2,1)} %broadcast_select_fusion), calls=%async_computation | async-start | bytes 8388608 | tf_op jit(solution)/shard_map/all_to_all | solution.py:185
  484.9 33.4 copy-start.56
  484.9 164.0 %copy-start.16 = (bf16[128,2048]{1,0:T(8,128)(2,1)S(1)}, bf16[128,2048]{1,0:T(8,128)(2,1)}, u32[]{:S(2)}) copy-start(bf16[128,2048]{1,0:T(8,128)(2,1)} %param.18) | copy-start | bytes 1572868
  484.9 183.8 %all-to-all-start.1 = ((bf16[16,64,2048]{2,1,0:T(8,128)(2,1)}), bf16[16,64,2048]{2,1,0:T(8,128)(2,1)}, u32[]{:S(2)}, u32[]{:S(2)}) async-start(bf16[16,64,2048]{2,1,0:T(8,128)(2,1)} %bitcast.234), calls=%async_computation.1 | async-start | bytes 8388608 | tf_op jit(solution)/shard_map/all_to_all | solution.py:201
  697.7 120.6 %all-to-all-start.2 = ((bf16[16,64,2048]{2,1,0:T(8,128)(2,1)}), bf16[16,64,2048]{2,1,0:T(8,128)(2,1)}, u32[]{:S(2)}, u32[]{:S(2)}) async-start(bf16[16,64,2048]{2,1,0:T(8,128)(2,1)} %multiply_convert_fusion), calls=%async_computation.2 | async-start | bytes 8388608 | tf_op jit(solution)/shard_map/all_to_all | solution.py:254
  714.7 290.2 %all-gather.31.cloned.1.call-start = ((), (), s32[]{:S(2)}) async-start(), calls=%async_computation.19 | async-start | bytes 11894784 | tf_op jit(solution)/shard_map/all_gather | solution.py:90
  854.9 118.3 %all-to-all-start.3 = ((bf16[16,64,2048]{2,1,0:T(8,128)(2,1)}), bf16[16,64,2048]{2,1,0:T(8,128)(2,1)}, u32[]{:S(2)}, u32[]{:S(2)}) async-start(bf16[16,64,2048]{2,1,0:T(8,128)(2,1)} %bitcast.235), calls=%async_computation.3 | async-start | bytes 8388608 | tf_op jit(solution)/shard_map/all_to_all | solution.py:283
  898.5 221.1 %all-gather.33.cloned.1.call-start = ((), (), s32[]{:S(2)}) async-start(), calls=%async_computation.20 | async-start | bytes 11894784 | tf_op jit(solution)/shard_map/all_gather | solution.py:90
  1014.5 250.3 %all-gather.35.cloned.1.call-start = ((), (), s32[]{:S(2)}) async-start(), calls=%async_computation.21 | async-start | bytes 23789568 | tf_op jit(solution)/shard_map/all_gather | solution.py:89
  1015.0 398.6 %all-gather.37.cloned.1.call-start = ((), (), s32[]{:S(2)}) async-start(), calls=%async_computation.22 | async-start | bytes 8650752 | tf_op jit(solution)/shard_map/all_gather | solution.py:81
  1023.3 7.1 copy-start.57
  1023.3 96.3 %copy-start.17 = (bf16[128,2048]{1,0:T(8,128)(2,1)S(1)}, bf16[128,2048]{1,0:T(8,128)(2,1)}, u32[]{:S(2)}) copy-start(bf16[128,2048]{1,0:T(8,128)(2,1)} %param.18) | copy-start | bytes 1572868
  1128.0 150.1 %copy-start.23 = (f32[128,1,2816]{2,0,1:T(8,128)}, f32[128,1,2816]{2,0,1:T(8,128)S(1)}, u32[]{:S(2)}) copy-start(f32[128,1,2816]{2,0,1:T(8,128)S(1)} %get-tuple-element.114) | copy-start | bytes 4325380
  1264.8 13.3 copy-start.39
  1264.8 13.3 copy-start.61
  1264.8 15.8 copy-start.72
  1282.0 131.7 %copy-start.7 = (f32[128,2048]{1,0:T(8,128)}, f32[128,2048]{1,0:T(8,128)S(1)}, u32[]{:S(2)}) copy-start(f32[128,2048]{1,0:T(8,128)S(1)} %fusion.44) | copy-start | bytes 3145732
  1282.0 149.3 %all-gather.41.cloned.1.call-start = ((), (), s32[]{:S(2)}) async-start(), calls=%async_computation.24 | async-start | bytes 4325376 | tf_op jit(solution)/shard_map/all_gather | solution.py:80
  1282.6 275.4 %reduce-scatter.25.cloned.1.call-start = ((), (), s32[]{:S(2)}) async-start(), calls=%async_computation.33 | async-start | bytes 1081344
  1284.0 285.6 %reduce-scatter.23.cloned.1.call-start = ((), (), s32[]{:S(2)}) async-start(), calls=%async_computation.32 | async-start | bytes 8650752 | tf_op jit(solution)/shard_map/reduce_scatter | solution.py:279
  1294.5 297.9 %reduce-scatter.21.cloned.1.call-start = ((), (), s32[]{:S(2)}) async-start(), calls=%async_computation.31 | async-start | bytes 17301504 | tf_op jit(solution)/shard_map/reduce_scatter | solution.py:276
  1314.7 955.8 %all-reduce.18.cloned.1.call-start = ((), (), s32[]{:S(2)}) async-start(), calls=%async_computation.34 | async-start | bytes 92274688
  1402.6 964.6 %all-gather.39.cloned.1.call-start = ((), (), s32[]{:S(2)}) async-start(), calls=%async_computation.23 | async-start | bytes 12976128 | tf_op jit(solution)/shard_map/all_gather | solution.py:77
  1403.2 1023.0 %all-gather.43.cloned.1.call-start = ((), (), s32[]{:S(2)}) async-start(), calls=%async_computation.25 | async-start | bytes 2703360 | tf_op jit(solution)/shard_map/all_gather | solution.py:78
  1403.8 1271.3 %reduce-scatter.19.cloned.1.call-start = ((), (), s32[]{:S(2)}) async-start(), calls=%async_computation.30 | async-start | bytes 23789568 | tf_op jit(solution)/shard_map/reduce_scatter | solution.py:308
  1413.4 7.3 copy-start.1
  1413.4 7.3 copy-start.35
  1413.4 1414.1 %reduce-scatter.13.cloned.1.call-start = ((), (), s32[]{:S(2)}) async-start(), calls=%async_computation.27 | async-start | bytes 5406720 | tf_op jit(solution)/shard_map/reduce_scatter | solution.py:427
  1425.3 5.7 collective-permute-start.2
  1427.1 3.1 collective-permute-start.3
  1439.4 1569.8 %reduce-scatter.17.cloned.1.call-start = ((), (), s32[]{:S(2)}) async-start(), calls=%async_computation.29 | async-start | bytes 17301504 | tf_op jit(solution)/shard_map/reduce_scatter | solution.py:430
  1449.8 1713.9 %reduce-scatter.15.cloned.1.call-start = ((), (), s32[]{:S(2)}) async-start(), calls=%async_computation.28 | async-start | bytes 8650752 | tf_op jit(solution)/shard_map/reduce_scatter | solution.py:429
  1455.7 1954.0 %reduce-scatter.11.cloned.1.call-start = ((), (), s32[]{:S(2)}) async-start(), calls=%async_computation.26 | async-start | bytes 25952256 | tf_op jit(solution)/shard_map/reduce_scatter | solution.py:426
  2376.1 53.8 %copy-start.55 = (f32[2048]{0:T(1024)S(1)}, f32[2048]{0:T(1024)}, u32[]{:S(2)}) copy-start(f32[2048]{0:T(1024)} %get-tuple-element.90) | copy-start | bytes 24580
  2376.2 53.8 %copy-start.62 = (f32[512]{0:T(512)S(1)}, f32[512]{0:T(512)}, u32[]{:S(2)}) copy-start(f32[512]{0:T(512)} %get-tuple-element.95) | copy-start | bytes 6148
  2376.2 106.5 %copy-start.68 = (f32[128]{0:T(128)S(1)}, f32[128]{0:T(128)}, u32[]{:S(2)}) copy-start(f32[128]{0:T(128)} %copy-done.67) | copy-start | bytes 1540
  2376.2 106.5 %copy-start.54 = (f32[128]{0:T(128)S(1)}, f32[128]{0:T(128)}, u32[]{:S(2)}) copy-start(f32[128]{0:T(128)} %copy-done.51) | copy-start | bytes 1540
  (43 other events, 127.1 us)
Sparse Core Ops, SparseCore 0:
  10.8 60.6 all-gather.16
  74.3 60.5 all-gather.18
  137.8 93.9 all-gather.20
  234.5 75.6 all-gather.22
  312.1 22.2 all-gather.24
  335.9 17.1 all-gather.26
  355.9 251.5 all-gather.28
  718.4 148.4 all-gather.30
  1014.6 104.9 all-gather.32
  1122.3 142.3 all-gather.34
  1282.1 75.1 all-gather.36
  1360.1 60.3 all-gather.40
  1422.7 135.2 reduce-scatter.24
  1560.1 9.4 reduce-scatter.22
  1572.3 20.0 reduce-scatter.20
  1598.7 671.7 all-reduce.17
  2273.2 94.0 all-gather.38
  2369.9 56.2 all-gather.42
  2429.1 245.9 reduce-scatter.18
  2677.8 149.6 reduce-scatter.12
  2830.4 178.7 reduce-scatter.16
  3012.0 151.5 reduce-scatter.14
  3170.7 238.9 reduce-scatter.10
where the time goes:
time: 3430 us; the launch traced here: 3420 us
  waiting for transfers between devices  2500 us (73%)
  blocking collectives  276 us (8%)
  matrix products  251 us (7%)
  local copies, waits for them, and re-layouts  204 us (6%)
  starting transfers between devices  109 us (3%)
  other arithmetic  65.1 us (2%)
    unnamed x25, waiting for transfers between devices  765 us
    reduce_scatter x1, waiting for transfers between devices, shards(): lax.psum_scatter(delta_query_weight, ('expert', 'shard'), scatter_dimensi...  246 us
    reduce_scatter x1, waiting for transfers between devices, shards(): lax.psum_scatter(delta_shared_outer, ('expert', 'shard'), scatter_dimensi...  190 us
    all_gather x2, blocking collectives, gather_feedforward(): lax.all_gather(router_weight, ('expert', 'shard'), axis=0, tiled=True)  185 us
    reduce_scatter x1, waiting for transfers between devices, shards(): lax.psum_scatter(delta_output_weight, ('expert', 'shard'), scatter_dimens...  182 us
    all_gather x2, waiting for transfers between devices, gather_attention(): lax.all_gather(query_weight, ('expert', 'shard'), axis=0, tiled=True)  179 us
    reduce_scatter x1, waiting for transfers between devices, shards(): lax.psum_scatter(delta_latent_up, ('expert', 'shard'), scatter_dimension=...  154 us
    reduce_scatter x1, waiting for transfers between devices, shards(): lax.psum_scatter(delta_latent_down, ('expert', 'shard'), scatter_dimensio...  152 us
  transfers between devices with their start and end apart: 31, of which 20 were waited for; matrix products, arithmetic and copies ran while one was open for 14% of the time, Pallas kernels for 0%

commit v1 on v0

v1 whole, which is shorter than its diff:
```python
import jax
import jax.numpy as jnp
from jax import lax
from jax.sharding import PartitionSpec as P

D = 2048
H = 16
DN = 128
DR = 64
DV = 128
KVR = 512
TOPK = 6
CL = 64

ALL = ("expert", "shard")
EPSILON = 1e-06
THETA = 10000.0
ALIGN = 8192
ROW = 1024


def passed_along(value, axis, steps):
    count = lax.axis_size(axis)
    first, last = (max(0, -steps), min(count, count - steps))
    return lax.ppermute(value, axis, [(source, source + steps) for source in range(first, last)])


def matmul(left_side, right_side):
    return jnp.dot(left_side, right_side, preferred_element_type=jnp.float32)


def norm_rows(values, gain_vector):
    return (
        values
        * lax.rsqrt(jnp.mean(values * values, axis=-1, keepdims=True) + EPSILON)
        * gain_vector
    )


def rotate(values, cosine_table, sine_table):
    middle = values.shape[-1] // 2
    first_half = values[..., :middle]
    second_half = values[..., middle:]
    return jnp.concatenate(
        [
            first_half * cosine_table - second_half * sine_table,
            second_half * cosine_table + first_half * sine_table,
        ],
        axis=-1,
    )


def angles(positions):
    inverse = THETA ** (-jnp.arange(DR // 2, dtype=jnp.float32) * 2.0 / DR)
    phases = positions.astype(jnp.float32)[:, None] * inverse[None, :]
    return (jnp.cos(phases), jnp.sin(phases))


def gated(inner_out):
    return jax.nn.silu(inner_out[..., 0, :]) * inner_out[..., 1, :]


def masked_scores(queries, key_rows, rotary_rows, visible):
    factor = (DN + DR) ** (-0.5)
    plain_part = jnp.einsum(
        "qhd,khd->hqk", queries[..., :DN], key_rows[..., :DN], preferred_element_type=jnp.float32
    )
    rotary_part = jnp.einsum(
        "qhr,kr->hqk", queries[..., DN:], rotary_rows, preferred_element_type=jnp.float32
    )
    return jnp.where(visible[None], (plain_part + rotary_part) * factor, -1e30)


def flat_pack(parts):
    flats = [part.reshape(part.shape[0], -1) for part in parts]
    sizes = [flat.shape[1] for flat in flats]
    pad = (-sum(sizes)) % ALIGN
    if pad:
        flats.append(jnp.zeros((flats[0].shape[0], pad), flats[0].dtype))
    return jnp.concatenate(flats, axis=1), sizes


def flat_unpack(packed, sizes, shapes):
    pieces = []
    offset = 0
    for size, shape in zip(sizes, shapes):
        pieces.append(packed[:, offset : offset + size].reshape((packed.shape[0],) + shape))
        offset += size
    return pieces


def gather_packed(parts, axis):
    packed, sizes = flat_pack([part[None] for part in parts])
    gathered = lax.all_gather(packed[0], axis, axis=0, tiled=False)
    return flat_unpack(gathered, sizes, [part.shape for part in parts])


def scatter_packed(parts, axis, count):
    packed, sizes = flat_pack([part.reshape((count, -1)) for part in parts])
    rows = packed.reshape(-1, ROW)
    local = lax.psum_scatter(rows, axis, scatter_dimension=0, tiled=True).reshape(1, -1)
    shapes = [(part.shape[0] // count,) + part.shape[1:] for part in parts]
    return [piece[0] for piece in flat_unpack(local, sizes, shapes)]


def shards(
    tokens_in,
    cotangent,
    expert_ids,
    attention_gain,
    query_weight,
    latent_down,
    latent_gain,
    latent_up,
    output_weight,
    feedforward_gain,
    router_weight,
    shared_inner,
    shared_outer,
    expert_inner,
    expert_outer,
):
    tok_rows = tokens_in.shape[0]
    experts_all = lax.axis_size("expert")
    shard_count = lax.axis_size("shard")
    devices = experts_all * shard_count
    slot_cap = tok_rows * TOPK * 4 // (3 * experts_all)
    factor = (DN + DR) ** (-0.5)
    side_index = lax.axis_index("shard")
    ordinal = jnp.arange(tok_rows, dtype=jnp.int32)
    positions = jnp.where(side_index == 0, ordinal, tok_rows + ordinal % CL)
    cosine_table, sine_table = angles(positions)
    query_place = ordinal[:, None]
    key_place = ordinal[None, :]
    causal = key_place <= query_place
    same_block = query_place // CL == key_place // CL
    local_mask = jnp.where(side_index == 0, causal, causal & same_block)
    remote_mask = jnp.broadcast_to(side_index == 1, (tok_rows, tok_rows))
    visible = jnp.concatenate([remote_mask, local_mask], axis=1)

    q_g, down_g, up_g, out_t_g, gain_one_g, gain_latent_g = gather_packed(
        [query_weight, latent_down, latent_up, output_weight.T, attention_gain, latent_gain], ALL
    )
    query_full = q_g.reshape(-1, q_g.shape[-1])
    down_full = down_g.reshape(-1, down_g.shape[-1])
    up_full = up_g.reshape(-1, up_g.shape[-1])
    output_t_full = out_t_g.reshape(-1, out_t_g.shape[-1])
    gain_one_float = gain_one_g.reshape(-1).astype(jnp.float32)
    gain_latent_float = gain_latent_g.reshape(-1).astype(jnp.float32)

    si_g, so_t_g, router_g, gain_two_g = gather_packed(
        [jnp.transpose(shared_inner, (1, 0, 2)), shared_outer.T, router_weight, feedforward_gain],
        ALL,
    )
    shared_in_full = si_g.reshape((-1,) + si_g.shape[2:])
    shared_out_t_full = so_t_g.reshape(-1, so_t_g.shape[-1])
    router_full = router_g.reshape(-1, router_g.shape[-1])
    gain_two_float = gain_two_g.reshape(-1).astype(jnp.float32)

    ei_g, eo_g = gather_packed([expert_inner[0], expert_outer[0]], "shard")
    inner_halves = ei_g
    outer_matrix = eo_g.reshape(-1, eo_g.shape[-1])

    tokens_float = tokens_in.astype(jnp.float32)
    normed_one = norm_rows(tokens_float, gain_one_float).astype(jnp.bfloat16)
    query_raw = matmul(normed_one, query_full).reshape(tok_rows, H, DN + DR)
    queries = jnp.concatenate(
        [
            query_raw[..., :DN],
            rotate(query_raw[..., DN:], cosine_table[:, None, :], sine_table[:, None, :]),
        ],
        axis=-1,
    ).astype(jnp.bfloat16)
    down_out = matmul(normed_one, down_full)
    latent_raw = down_out[:, :KVR]
    latents = norm_rows(latent_raw, gain_latent_float).astype(jnp.bfloat16)
    key_rotary = rotate(down_out[:, KVR:], cosine_table, sine_table).astype(jnp.bfloat16)
    expanded = matmul(latents, up_full).astype(jnp.bfloat16).reshape(tok_rows, H, DN + DV)
    kv_local = jnp.concatenate([expanded.reshape(tok_rows, -1), key_rotary], axis=1)
    kv_remote = passed_along(kv_local, "shard", 1)
    remote_expanded = kv_remote[:, : H * (DN + DV)].reshape(tok_rows, H, DN + DV)
    remote_rotary = kv_remote[:, H * (DN + DV) :]
    key_rows = jnp.concatenate([remote_expanded, expanded], axis=0)
    rotary_rows = jnp.concatenate([remote_rotary, key_rotary], axis=0)
    scores = masked_scores(queries, key_rows, rotary_rows, visible)
    score_max = jnp.max(scores, axis=-1, keepdims=True)
    log_total = score_max + jnp.log(jnp.sum(jnp.exp(scores - score_max), axis=-1, keepdims=True))
    weights_float = jnp.exp(scores - log_total)
    weights_low = weights_float.astype(jnp.bfloat16)
    mixed_heads = (
        jnp.einsum(
            "hqk,khd->qhd", weights_low, key_rows[..., DN:], preferred_element_type=jnp.float32
        )
        .astype(jnp.bfloat16)
        .reshape(tok_rows, H * DV)
    )
    attention_out = jnp.einsum(
        "tc,dc->td", mixed_heads, output_t_full, preferred_element_type=jnp.float32
    )
    residual = tokens_float + attention_out
    normed_two = norm_rows(residual, gain_two_float).astype(jnp.bfloat16)
    logits = matmul(normed_two, router_full)
    route_probs = jax.nn.softmax(logits, axis=-1)
    gate_values = jnp.take_along_axis(route_probs, expert_ids, axis=1)
    flat_experts = expert_ids.reshape(-1)
    expert_match = (
        flat_experts[:, None] == jnp.arange(experts_all, dtype=jnp.int32)[None, :]
    ).astype(jnp.int32)
    slot_rank = jnp.sum((jnp.cumsum(expert_match, axis=0) - expert_match) * expert_match, axis=1)
    pair_count = tok_rows * TOPK
    slot_of = flat_experts * slot_cap + slot_rank
    slot_pair = (
        jnp.full((experts_all * slot_cap,), pair_count, jnp.int32)
        .at[slot_of]
        .set(jnp.arange(pair_count, dtype=jnp.int32))
    )
    slot_token = slot_pair // TOPK
    delta_out = cotangent.astype(jnp.float32)
    padded_rows = jnp.concatenate([normed_two, jnp.zeros((1, D), jnp.bfloat16)], axis=0)
    send_rows = jnp.take(padded_rows, slot_token, axis=0)
    padded_gates = jnp.concatenate([gate_values.reshape(-1), jnp.zeros((1,), jnp.float32)])
    slot_gate = jnp.take(padded_gates, slot_pair, axis=0)
    padded_delta = jnp.concatenate([delta_out, jnp.zeros((1, D), jnp.float32)], axis=0)
    send_delta = (jnp.take(padded_delta, slot_token, axis=0) * slot_gate[:, None]).astype(
        jnp.bfloat16
    )
    outgoing = jnp.stack(
        [send_rows.reshape(experts_all, slot_cap, D), send_delta.reshape(experts_all, slot_cap, D)],
        axis=1,
    )
    incoming = lax.all_to_all(outgoing, "expert", split_axis=0, concat_axis=0, tiled=True)
    arrived = incoming[:, 0].reshape(-1, D)
    delta_arrived = incoming[:, 1].reshape(-1, D)

    expert_pre = jnp.einsum(
        "rd,sgdf->rgsf", arrived, inner_halves, preferred_element_type=jnp.float32
    ).reshape(arrived.shape[0], 2, -1)
    expert_hidden = gated(expert_pre).astype(jnp.bfloat16)
    expert_result = matmul(expert_hidden, outer_matrix).astype(jnp.bfloat16)
    delta_outer_matrix = jnp.einsum(
        "rf,rd->fd", expert_hidden, delta_arrived, preferred_element_type=jnp.float32
    )
    delta_expert_hidden = jnp.einsum(
        "rd,fd->rf", delta_arrived, outer_matrix, preferred_element_type=jnp.float32
    )
    unused_expert, expert_back = jax.vjp(gated, expert_pre)
    delta_expert_pre = expert_back(delta_expert_hidden)[0].astype(jnp.bfloat16)
    delta_pre_halves = delta_expert_pre.reshape(arrived.shape[0], 2, shard_count, -1)
    delta_inner_halves = jnp.einsum(
        "rd,rgsf->sgdf", arrived, delta_pre_halves, preferred_element_type=jnp.float32
    )
    delta_rows = jnp.einsum(
        "rgsf,sgdf->rd", delta_pre_halves, inner_halves, preferred_element_type=jnp.float32
    ).astype(jnp.bfloat16)
    delta_expert_inner, delta_expert_outer = scatter_packed(
        [
            delta_inner_halves.astype(jnp.bfloat16),
            delta_outer_matrix.astype(jnp.bfloat16).reshape(shard_count, -1, D),
        ],
        "shard",
        shard_count,
    )
    going_back = jnp.stack(
        [
            expert_result.reshape(experts_all, slot_cap, D),
            delta_rows.reshape(experts_all, slot_cap, D),
        ],
        axis=1,
    )
    coming_back = lax.all_to_all(going_back, "expert", split_axis=0, concat_axis=0, tiled=True)
    returned = coming_back[:, 0].reshape(-1, D)
    delta_returned = coming_back[:, 1].reshape(-1, D)

    picked = jnp.take(returned, slot_of, axis=0).reshape(tok_rows, TOPK, D).astype(jnp.float32)
    routed = jnp.sum(gate_values[..., None] * picked, axis=1)
    shared_pre = jnp.einsum(
        "td,dgf->tgf", normed_two, shared_in_full, preferred_element_type=jnp.float32
    )
    shared_hidden = gated(shared_pre).astype(jnp.bfloat16)
    shared_result = jnp.einsum(
        "tf,df->td", shared_hidden, shared_out_t_full, preferred_element_type=jnp.float32
    )
    feedforward = routed + shared_result
    layer_output = (residual + feedforward).astype(jnp.bfloat16)
    square_sums = lax.psum(
        jnp.stack(
            [
                jnp.sum(residual * residual),
                jnp.sum(attention_out * attention_out),
                jnp.sum(feedforward * feedforward),
            ]
        ),
        ALL,
    )
    statistics = jnp.sqrt(square_sums / (tok_rows * D * devices))

    delta_shared_outer_t = jnp.einsum(
        "td,tf->df", cotangent, shared_hidden, preferred_element_type=jnp.float32
    )
    delta_shared_hidden = jnp.einsum(
        "td,df->tf", cotangent, shared_out_t_full, preferred_element_type=jnp.float32
    )
    unused_shared, shared_back = jax.vjp(gated, shared_pre)
    delta_shared_pre = shared_back(delta_shared_hidden)[0].astype(jnp.bfloat16)
    delta_shared_inner_t = jnp.einsum(
        "td,tgf->dgf", normed_two, delta_shared_pre, preferred_element_type=jnp.float32
    )
    delta_normed = jnp.einsum(
        "tgf,dgf->td", delta_shared_pre, shared_in_full, preferred_element_type=jnp.float32
    )
    delta_gates = jnp.sum(delta_out[:, None, :] * picked, axis=-1)
    delta_normed = delta_normed + jnp.sum(
        jnp.take(delta_returned, slot_of, axis=0).reshape(tok_rows, TOPK, D).astype(jnp.float32),
        axis=1,
    )
    match_float = expert_match.reshape(tok_rows, TOPK, experts_all).astype(jnp.float32)
    delta_probs = jnp.einsum("tk,tke->te", delta_gates, match_float)
    delta_logits = (
        route_probs * (delta_probs - jnp.sum(route_probs * delta_probs, axis=-1, keepdims=True))
    ).astype(jnp.bfloat16)
    delta_router = jnp.einsum(
        "td,te->de", normed_two, delta_logits, preferred_element_type=jnp.float32
    )
    delta_normed = delta_normed + jnp.einsum(
        "te,de->td", delta_logits, router_full, preferred_element_type=jnp.float32
    )
    unused_second, second_back = jax.vjp(norm_rows, residual, gain_two_float)
    delta_residual_norm, delta_gain_two = second_back(delta_normed)
    delta_residual = delta_out + delta_residual_norm
    ffn_grads = scatter_packed(
        [
            delta_shared_inner_t.astype(jnp.bfloat16),
            delta_shared_outer_t.astype(jnp.bfloat16),
            delta_router.astype(jnp.bfloat16),
            delta_gain_two.astype(jnp.bfloat16),
        ],
        ALL,
        devices,
    )
    delta_shared_inner = jnp.transpose(ffn_grads[0], (1, 0, 2)).astype(jnp.float32)
    delta_shared_outer = ffn_grads[1].T.astype(jnp.float32)
    delta_router_local = ffn_grads[2].astype(jnp.float32)
    delta_gain_two_local = ffn_grads[3].astype(jnp.float32)

    delta_attention = delta_residual.astype(jnp.bfloat16)
    delta_output_t = jnp.einsum(
        "td,tc->dc", delta_attention, mixed_heads, preferred_element_type=jnp.float32
    )
    delta_mixed = (
        jnp.einsum("td,dc->tc", delta_attention, output_t_full, preferred_element_type=jnp.float32)
        .astype(jnp.bfloat16)
        .reshape(tok_rows, H, DV)
    )
    delta_weights = jnp.einsum(
        "qhd,khd->hqk", delta_mixed, key_rows[..., DN:], preferred_element_type=jnp.float32
    )
    delta_scores = (
        weights_float
        * (delta_weights - jnp.sum(weights_float * delta_weights, axis=-1, keepdims=True))
    ).astype(jnp.bfloat16)
    delta_values = jnp.einsum(
        "hqk,qhd->khd", weights_low, delta_mixed, preferred_element_type=jnp.float32
    )
    delta_query_plain = (
        jnp.einsum(
            "hqk,khd->qhd", delta_scores, key_rows[..., :DN], preferred_element_type=jnp.float32
        )
        * factor
    )
    delta_query_rotary = (
        jnp.einsum("hqk,kr->qhr", delta_scores, rotary_rows, preferred_element_type=jnp.float32)
        * factor
    )
    delta_key_plain = (
        jnp.einsum(
            "hqk,qhd->khd", delta_scores, queries[..., :DN], preferred_element_type=jnp.float32
        )
        * factor
    )
    delta_key_rotary = (
        jnp.einsum(
            "hqk,qhr->kr", delta_scores, queries[..., DN:], preferred_element_type=jnp.float32
        )
        * factor
    )
    delta_key_rows = jnp.concatenate([delta_key_plain, delta_values], axis=-1)
    back_local = jnp.concatenate(
        [delta_key_rows[:tok_rows].reshape(tok_rows, -1), delta_key_rotary[:tok_rows]], axis=1
    ).astype(jnp.bfloat16)
    back_remote = passed_along(back_local, "shard", -1).astype(jnp.float32)
    back_rows = back_remote[:, : H * (DN + DV)].reshape(tok_rows, H, DN + DV)
    back_rotary = back_remote[:, H * (DN + DV) :]
    delta_expanded = (
        (delta_key_rows[tok_rows:] + back_rows)
        .astype(jnp.bfloat16)
        .reshape(tok_rows, H * (DN + DV))
    )
    delta_rotary_total = delta_key_rotary[tok_rows:] + back_rotary
    delta_latent_up = jnp.einsum(
        "tl,tc->lc", latents, delta_expanded, preferred_element_type=jnp.float32
    )
    delta_latents = jnp.einsum(
        "tc,lc->tl", delta_expanded, up_full, preferred_element_type=jnp.float32
    )
    unused_latent, latent_back = jax.vjp(norm_rows, latent_raw, gain_latent_float)
    delta_latent_raw, delta_gain_latent = latent_back(delta_latents)
    delta_down_out = jnp.concatenate(
        [delta_latent_raw, rotate(delta_rotary_total, cosine_table, -sine_table)], axis=-1
    ).astype(jnp.bfloat16)
    delta_latent_down = jnp.einsum(
        "td,tc->dc", normed_one, delta_down_out, preferred_element_type=jnp.float32
    )
    delta_query_raw = (
        jnp.concatenate(
            [
                delta_query_plain,
                rotate(delta_query_rotary, cosine_table[:, None, :], -sine_table[:, None, :]),
            ],
            axis=-1,
        )
        .astype(jnp.bfloat16)
        .reshape(tok_rows, H * (DN + DR))
    )
    delta_query_weight = jnp.einsum(
        "td,tc->dc", normed_one, delta_query_raw, preferred_element_type=jnp.float32
    )
    delta_normed_one = jnp.einsum(
        "tc,dc->td", delta_query_raw, query_full, preferred_element_type=jnp.float32
    ) + jnp.einsum("tc,dc->td", delta_down_out, down_full, preferred_element_type=jnp.float32)
    unused_first, first_back = jax.vjp(norm_rows, tokens_float, gain_one_float)
    delta_tokens_norm, delta_gain_one = first_back(delta_normed_one)
    input_gradient = (delta_residual + delta_tokens_norm).astype(jnp.bfloat16)
    att_grads = scatter_packed(
        [
            delta_query_weight.astype(jnp.bfloat16),
            delta_latent_down.astype(jnp.bfloat16),
            delta_latent_up.astype(jnp.bfloat16),
            delta_output_t.astype(jnp.bfloat16),
            delta_gain_one.astype(jnp.bfloat16),
            delta_gain_latent.astype(jnp.bfloat16),
        ],
        ALL,
        devices,
    )
    return (
        layer_output,
        input_gradient,
        att_grads[4].astype(jnp.float32),
        att_grads[0].astype(jnp.float32),
        att_grads[1].astype(jnp.float32),
        att_grads[5].astype(jnp.float32),
        att_grads[2].astype(jnp.float32),
        att_grads[3].T.astype(jnp.float32),
        delta_gain_two_local,
        delta_router_local,
        delta_shared_inner,
        delta_shared_outer,
        delta_expert_inner.astype(jnp.float32),
        delta_expert_outer.astype(jnp.float32),
        statistics,
    )


def solution(mesh):
    return jax.shard_map(
        shards,
        mesh=mesh,
        in_specs=(
            P(ALL, None),
            P(ALL, None),
            P(ALL, None),
            P(ALL),
            P(ALL, None),
            P(ALL, None),
            P(ALL),
            P(ALL, None),
            P(None, ALL),
            P(ALL),
            P(ALL, None),
            P(None, ALL, None),
            P(None, ALL),
            P("expert", None, None, "shard"),
            P("expert", "shard", None),
        ),
        out_specs=(
            P(ALL, None),
            P(ALL, None),
            P(ALL),
            P(ALL, None),
            P(ALL, None),
            P(ALL),
            P(ALL, None),
            P(None, ALL),
            P(ALL),
            P(ALL, None),
            P(None, ALL, None),
            P(None, ALL),
            P("expert", None, None, "shard"),
            P("expert", "shard", None),
            P(),
        ),
        check_vma=False,
    )
```

time: 3430 us -> 2620 us (0.76)
  waiting for transfers between devices: 2500 us -> 770 us
  local copies, waits for them, and re-layouts: 204 us -> 1010 us
  other arithmetic: 65.1 us -> 487 us
  blocking collectives: 276 us -> 45.4 us
  starting transfers between devices: 109 us -> 48.3 us
    reduce_scatter x7 -> x1, waiting for transfers between devices: 953 us -> 0.01 us  [scatter_packed(): lax.psum_scatter(rows, axis, scatter_dimension=0, tiled=True).reshape(1, -1)]
    unnamed x25 -> x8, waiting for transfers between devices: 765 us -> 330 us
    unnamed x169 -> x284, local copies, waits for them, and re-layouts: 30.6 us -> 338 us
    reshape x1 -> x14, local copies, waits for them, and re-layouts: 1.31 us -> 233 us  [the longest x3 113 us: scatter_packed(): rows = packed.reshape(-1, ROW)]
    all_to_all x4 -> x2, waiting for transfers between devices: 251 us -> 39.8 us  [the longest x1 39.8 us: shards(): lax.all_to_all(outgoing, 'expert', split_axis=0, concat_axis=0, tiled=True)]
    all_gather x2 -> x0, blocking collectives: 185 us -> none  [gather_feedforward(): lax.all_gather(router_weight, ('expert', 'shard'), axis=0, tiled=True)]
    convert_element_type x8 -> x20, other arithmetic: 21 us -> 199 us  [the longest x1 101 us: shards(): delta_expert_inner.astype(jnp.float32)]
    concatenate x2 -> x3, other arithmetic: 0.06 us -> 155 us  [the longest x1 153 us: flat_pack(): return (jnp.concatenate(flats, axis=1), sizes)]
  transfers between devices with their start and end apart: 31 -> 10, of which waited for: 20 -> 4; matrix products, arithmetic and copies ran while one was open for 14% -> 55% of each run, Pallas kernels for 0% -> 0%
where the time goes in v1:
time: 2620 us; the launch traced here: 2600 us
  local copies, waits for them, and re-layouts  1010 us (39%)
  waiting for transfers between devices  770 us (29%)
  other arithmetic  487 us (19%)
  matrix products  223 us (9%)
  starting transfers between devices  48.3 us (2%)
  blocking collectives  45.4 us (2%)
    all_gather x3, waiting for transfers between devices, gather_packed(): gathered = lax.all_gather(packed[0], axis, axis=0, tiled=False)  401 us
    unnamed x284, local copies, waits for them, and re-layouts  338 us
    unnamed x8, waiting for transfers between devices  330 us
    concatenate x1, other arithmetic, flat_pack(): return (jnp.concatenate(flats, axis=1), sizes)  153 us
    reshape x3, local copies, waits for them, and re-layouts, scatter_packed(): rows = packed.reshape(-1, ROW)  113 us
    convert_element_type x1, other arithmetic, shards(): delta_expert_inner.astype(jnp.float32)  101 us
    reshape x8, local copies, waits for them, and re-layouts, scatter_packed(): packed, sizes = flat_pack([part.reshape((count, -1)) for part in parts])  95.6 us
    unnamed x6, other arithmetic  73.3 us
  transfers between devices with their start and end apart: 10, of which 4 were waited for; matrix products, arithmetic and copies ran while one was open for 55% of the time, Pallas kernels for 0%

profile of v1, /device:TPU:0, one launch (start us, length us, event | category | flops | bytes accessed | tf_op | source)
XLA Modules:
  0.0 2603.4 jit_solution(3391644703578602181)
XLA Ops:
  33.0 8.5 copy.153
  41.5 12.7 reshape.757
  61.7 73.3 %maximum_bitcast_fusion = bf16[1,1,4325376]{2,1,0:T(2,128)(2,1)} fusion(bf16[1,1441792]{1,0:T(2,128)(2,1)} %bitcast.328, bf16[1,2883584]{1,0:T(2,128)(2,1)S(1)} %reshape_broadcast_in_dim_squeeze.6), kind=kLoop, calls=%fused_computation.13 | loop fusion | flops 17301504 | bytes 17301504
  143.6 175.8 %all-gather.7.cloned.1.call-done = bf16[32,1,434176]{2,1,0:T(2,128)(2,1)} async-done(((bf16[1,1,434176]{2,1,0:T(2,128)(2,1)}), bf16[32,1,434176]{2,1,0:T(2,128)(2,1)}) %all-gather.7.cloned.1.call-update) | async-done | bytes 27787280 | tf_op jit(solution)/shard_map/all_gather | solution.py:94
  319.5 29.5 %copy.232 = bf16[32,1,434176]{2,0,1:T(8,128)(2,1)} copy(bf16[32,1,434176]{2,1,0:T(2,128)(2,1)} %all-gather.7.cloned.1.call-done) | data formatting | bytes 55574528
  396.9 10.5 slice.258
  407.9 12.4 reshape_reshape.29
  420.3 9.0 reshape_reshape.30
  429.3 16.7 copy.141
  466.6 224.7 %all-gather.9.cloned.1.call-done = bf16[32,1,548864]{2,1,0:T(2,128)(2,1)} async-done(((bf16[1,1,548864]{2,1,0:T(2,128)(2,1)}), bf16[32,1,548864]{2,1,0:T(2,128)(2,1)}) %all-gather.9.cloned.1.call-update) | async-done | bytes 35127312 | tf_op jit(solution)/shard_map/all_gather | solution.py:94
  691.3 46.7 %copy.231 = bf16[32,1,548864]{2,0,1:T(8,128)(2,1)} copy(bf16[32,1,548864]{2,1,0:T(2,128)(2,1)} %all-gather.9.cloned.1.call-done) | data formatting | bytes 70254592
  777.6 55.3 %copy.233 = bf16[2,1,4325376]{2,0,1:T(2,128)(2,1)S(1)} copy(bf16[2,1,4325376]{2,1,0:T(2,128)(2,1)} %all-gather.11.cloned.1.call-done) | data formatting | bytes 34603008
  837.9 9.4 slice.267
  847.2 10.7 reshape_reshape.32
  857.9 17.9 reshape.759
  875.8 21.4 reshape.582
  897.2 39.8 %all-to-all-done = bf16[16,2,64,2048]{3,2,1,0:T(8,128)(2,1)} async-done(((bf16[16,2,64,2048]{3,2,1,0:T(8,128)(2,1)}), bf16[16,2,64,2048]{3,2,1,0:T(8,128)(2,1)}, u32[]{:S(2)}, u32[]{:S(2)}) %all-to-all-start) | async-done | bytes 8388640 | tf_op jit(solution)/shard_map/all_to_all | solution.py:231
  947.1 17.6 convolution_bitcast_fusion
  964.7 10.9 copy.159
  975.6 11.2 fusion.132
  1007.0 15.1 fusion.15
  1022.2 11.1 convolution_convert_fusion.6
  1039.0 8.4 copy.162
  1047.4 19.7 bitcast_convert_fusion
  1073.3 38.0 %all-to-all-start.1 = ((bf16[16,2,64,2048]{3,2,1,0:T(8,128)(2,1)}), bf16[16,2,64,2048]{3,2,1,0:T(8,128)(2,1)}, u32[]{:S(2)}, u32[]{:S(2)}) async-start(bf16[16,2,64,2048]{3,2,1,0:T(8,128)(2,1)} %pad_maximum_fusion.2), calls=%async_computation.1 | async-start | bytes 16777216 | tf_op jit(solution)/shard_map/all_to_all | solution.py:270
  1115.8 8.5 mul.527
  1124.2 9.9 slice.277
  1134.1 19.8 slice.274
  1153.9 42.0 %reshape_reshape.33 = bf16[2048,2,2816]{2,1,0:T(2,128)(2,1)} reshape(bf16[32,360448]{1,0:T(8,128)(2,1)} %slice.274) | data formatting | bytes 46137344 | tf_op jit(solution)/shard_map/reshape;reshape | solution.py:155
  1195.9 11.3 reshape_reshape.34
  1207.1 15.0 fusion.2
  1229.9 15.2 copy.178
  1245.1 11.2 reshape.597
  1263.6 11.2 convolution_convert_fusion
  1274.8 42.1 %copy.177 = bf16[2048,2,2816]{2,1,0:T(2,128)(2,1)} copy(bf16[2048,2,2816]{2,0,1:T(8,128)(2,1)} %convolution_convert_fusion) | data formatting | bytes 46137344 | tf_op jit(solution)/shard_map/convert_element_type | solution.py:332
  1316.9 38.1 %reshape.596 = bf16[32,360448]{1,0:T(8,128)(2,1)} reshape(bf16[2048,2,2816]{2,1,0:T(2,128)(2,1)} %copy.177) | data formatting | bytes 46137344 | tf_op jit(solution)/shard_map/reshape | solution.py:99
  1355.0 10.8 convolution_convert_fusion.2
  1365.9 9.2 reshape_reshape.35
  1375.1 17.9 convert_bitcast_fusion
  1393.0 16.4 copy.180
  1409.4 24.3 reshape.761
  1433.6 13.2 reshape.601
  1453.0 9.8 gather_fusion.5
  1462.8 9.1 gather_fusion.4
  1498.9 17.7 fusion.23
  1534.8 10.7 multiply_reduce_fusion.3
  1561.5 153.3 %pad_maximum_fusion = bf16[2,4325376]{1,0:T(2,128)(2,1)} fusion(bf16[2,1441792]{1,0:T(2,128)(2,1)S(1)} %bitcast.327, bf16[2,2883584]{1,0:T(2,128)(2,1)S(1)} %bitcast.321), kind=kLoop, calls=%fused_computation.14 | loop fusion | flops 34603008 | bytes 34603008 | tf_op jit(solution)/shard_map/concatenate | solution.py:80
  1714.8 33.0 %reshape.602 = bf16[8448,1024]{1,0:T(8,128)(2,1)} reshape(bf16[2,4325376]{1,0:T(2,128)(2,1)} %pad_maximum_fusion) | data formatting | bytes 34603008 | tf_op jit(solution)/shard_map/reshape | solution.py:100
  1754.9 10.5 reshape.593
  1776.0 11.9 reshape.590
  1788.0 10.4 constant_dynamic-update-slice_fusion.10
  1804.1 9.0 fusion.137
  1853.9 35.9 %reshape.594 = bf16[13568,1024]{1,0:T(8,128)(2,1)} reshape(bf16[32,434176]{1,0:T(8,128)(2,1)} %dynamic-update-slice.11) | data formatting | bytes 55574528 | tf_op jit(solution)/shard_map/reshape | solution.py:100
  1889.8 19.9 constant_dynamic-update-slice_fusion.13
  1909.8 9.1 constant_dynamic-update-slice_fusion.12
  1925.7 43.8 %reshape.599 = bf16[17152,1024]{1,0:T(8,128)(2,1)} reshape(bf16[32,548864]{1,0:T(8,128)(2,1)} %dynamic-update-slice.4) | data formatting | bytes 70254592 | tf_op jit(solution)/shard_map/reshape | solution.py:100
  1971.8 45.4 %psum.7 = f32[3]{0:T(128)S(1)} all-reduce(f32[3]{0:T(128)S(1)} %pad_maximum_fusion.16), channel_id=1, replica_groups=mesh['expert'=16,'shard'=2] {'expert','shard'}, use_global_device_ids=true, to_apply=%region_28.30 | all-reduce | flops 3 | bytes 24 | tf_op jit(solution)/shard_map/psum | solution.py:285
  2018.8 15.9 copy.214
  2034.7 51.4 %fusion.10 = f32[1441792]{0:T(1024)} fusion(bf16[1,4325376]{1,0:T(2,128)(2,1)} %bitcast.317), kind=kLoop, calls=%fused_computation.39 | loop fusion | flops 1441792 | bytes 8650752 | tf_op jit(solution)/shard_map/convert_element_type | solution.py:459
  2093.0 101.4 %fusion.6 = f32[2883584]{0:T(1024)} fusion(bf16[1,4325376]{1,0:T(2,128)(2,1)} %bitcast.318), kind=kLoop, calls=%fused_computation.20 | loop fusion | flops 2883584 | bytes 17301504 | tf_op jit(solution)/shard_map/convert_element_type | solution.py:458
  2194.5 14.5 reshape.616
  2209.0 12.3 copy.183
  2237.5 329.8 %reduce-scatter.14.cloned.1.call-done = bf16[536,1024]{1,0:T(8,128)(2,1)} async-done(((bf16[17152,1024]{1,0:T(8,128)(2,1)}), bf16[536,1024]{1,0:T(8,128)(2,1)}) %reduce-scatter.14.cloned.1.call-update) | async-done | bytes 1097744
  2577.9 13.5 fusion.36
  (470 shorter events, 396.4 us)
Async XLA Ops:
  7.2 7.4 copy-start.108
  7.2 9.6 copy-start.94
  7.2 9.8 copy-start.56
  7.2 312.2 %all-gather.7.cloned.1.call-start = ((), (), s32[]{:S(2)}) async-start(), calls=%async_computation.6 | async-start | bytes 57311232 | tf_op jit(solution)/shard_map/all_gather | solution.py:94
  16.7 674.5 %all-gather.9.cloned.1.call-start = ((), (), s32[]{:S(2)}) async-start(), calls=%async_computation.7 | async-start | bytes 72450048 | tf_op jit(solution)/shard_map/all_gather | solution.py:94
  26.3 751.2 %all-gather.11.cloned.1.call-start = ((), (), s32[]{:S(2)}) async-start(), calls=%async_computation.8 | async-start | bytes 51904512 | tf_op jit(solution)/shard_map/all_gather | solution.py:94
  135.1 238.1 %copy-start.97 = (f32[32]{0:T(128)}, f32[32]{0:T(128)S(1)}, u32[]{:S(2)}) copy-start(f32[32]{0:T(128)S(1)} %multiply_power_fusion) | copy-start | bytes 388
  135.8 213.2 %copy-start.61 = (s32[128,6]{1,0:T(8,128)}, s32[128,6]{1,0:T(8,128)S(1)}, u32[]{:S(2)}) copy-start(s32[128,6]{1,0:T(8,128)S(1)} %copy.150) | copy-start | bytes 9220
  136.3 309.7 %copy-start.84 = (f32[128]{0:T(128)}, f32[128]{0:T(128)S(1)}, u32[]{:S(2)}) copy-start(f32[128]{0:T(128)S(1)} %fusion.110) | copy-start | bytes 1540
  136.3 236.8 %copy-start.99 = (f32[128]{0:T(128)}, f32[128]{0:T(128)S(1)}, u32[]{:S(2)}) copy-start(f32[128]{0:T(128)S(1)} %fusion.105) | copy-start | bytes 1540
  358.2 15.1 copy-start.76
  358.3 87.7 %copy-start.57 = (f32[2048]{0:T(1024)}, f32[2048]{0:T(1024)S(1)}, u32[]{:S(2)}) copy-start(f32[2048]{0:T(1024)S(1)} %reshape.604) | copy-start | bytes 24580
  373.1 9.3 copy-start.34
  373.3 79.3 %copy-start.70 = (f32[128,32]{0,1:T(8,128)}, f32[128,32]{0,1:T(8,128)S(1)}, u32[]{:S(2)}) copy-start(f32[128,32]{0,1:T(8,128)S(1)} %get-tuple-element.99) | copy-start | bytes 49156
  373.3 86.7 %copy-start.72 = (bf16[128,32]{0,1:T(8,128)(2,1)}, bf16[128,32]{0,1:T(8,128)(2,1)S(1)}, u32[]{:S(2)}) copy-start(bf16[128,32]{0,1:T(8,128)(2,1)S(1)} %get-tuple-element.101) | copy-start | bytes 24580
  373.4 86.7 %copy-start.74 = (bf16[128,32]{0,1:T(8,128)(2,1)}, bf16[128,32]{0,1:T(8,128)(2,1)S(1)}, u32[]{:S(2)}) copy-start(bf16[128,32]{0,1:T(8,128)(2,1)S(1)} %get-tuple-element.102) | copy-start | bytes 24580
  378.5 74.3 %collective-permute-start = (bf16[128,4160]{0,1:T(8,128)(2,1)}, bf16[128,4160]{0,1:T(8,128)(2,1)}, u32[]{:S(2)}, u32[]{:S(2)}) collective-permute-start(bf16[128,4160]{0,1:T(8,128)(2,1)} %pad_maximum_fusion.4), channel_id=1, source_target_pairs={{0,1},{2,3},{4,5},{6,7},{8,9},{10,11},{12,13},{14,15},{16,17},{18,... | collective-permute-start | bytes 3194888 | tf_op jit(solution)/shard_map/ppermute | solution.py:25
  407.9 53.5 %copy-start.4 = (bf16[128,16,256]{2,0,1:T(8,128)(2,1)}, bf16[128,16,256]{2,0,1:T(8,128)(2,1)S(1)}, u32[]{:S(2)}) copy-start(bf16[128,16,256]{2,0,1:T(8,128)(2,1)S(1)} %copy.140) | copy-start | bytes 3145732
  452.8 7.3 copy-start.52
  466.6 271.4 %copy-start.105 = (f32[128]{0:T(128)}, f32[128]{0:T(128)S(1)}, u32[]{:S(2)}) copy-start(f32[128]{0:T(128)S(1)} %get-tuple-element.70) | copy-start | bytes 1540
  466.6 273.4 %copy-start.28 = (f32[128,2048]{1,0:T(8,128)}, f32[128,2048]{1,0:T(8,128)S(1)}, u32[]{:S(2)}) copy-start(f32[128,2048]{1,0:T(8,128)S(1)} %get-tuple-element.71) | copy-start | bytes 3145732
  466.6 273.4 %copy-start.95 = (f32[128]{0:T(128)}, f32[128]{0:T(128)S(1)}, u32[]{:S(2)}) copy-start(f32[128]{0:T(128)S(1)} %fusion.112) | copy-start | bytes 1540
  772.8 164.2 %all-to-all-start = ((bf16[16,2,64,2048]{3,2,1,0:T(8,128)(2,1)}), bf16[16,2,64,2048]{3,2,1,0:T(8,128)(2,1)}, u32[]{:S(2)}, u32[]{:S(2)}) async-start(bf16[16,2,64,2048]{3,2,1,0:T(8,128)(2,1)} %pad_maximum_fusion.1), calls=%async_computation | async-start | bytes 16777216 | tf_op jit(solution)/shard_map/all_to_all | solution.py:231
  937.0 10.1 copy-start.24
  942.4 22.3 copy-start.44
  993.0 14.0 slice-start.7
  999.4 7.7 slice-start.8
  1022.2 11.1 copy-start.33
  1047.4 19.7 copy-start.45
  1073.3 38.0 %copy-start.35 = (bf16[128,2048]{1,0:T(8,128)(2,1)S(1)}, bf16[128,2048]{1,0:T(8,128)(2,1)}, u32[]{:S(2)}) copy-start(bf16[128,2048]{1,0:T(8,128)(2,1)} %param.18) | copy-start | bytes 1572868
  1073.3 373.6 %all-to-all-start.1 = ((bf16[16,2,64,2048]{3,2,1,0:T(8,128)(2,1)}), bf16[16,2,64,2048]{3,2,1,0:T(8,128)(2,1)}, u32[]{:S(2)}, u32[]{:S(2)}) async-start(bf16[16,2,64,2048]{3,2,1,0:T(8,128)(2,1)} %pad_maximum_fusion.2), calls=%async_computation.1 | async-start | bytes 16777216 | tf_op jit(solution)/shard_map/all_to_all | solution.py:270
  1111.3 907.6 %reduce-scatter.10.cloned.1.call-start = ((), (), s32[]{:S(2)}) async-start(), calls=%async_computation.5 | async-start | bytes 25952256 | tf_op jit(solution)/shard_map/reduce_scatter | solution.py:101
  1195.9 11.3 copy-start.22
  1263.6 11.2 copy-start.49
  1263.6 11.2 copy-start.51
  1316.9 38.1 %copy-start.47 = (bf16[1024,1,1408]{2,0,1:T(8,128)(2,1)S(1)}, bf16[1024,1,1408]{2,0,1:T(8,128)(2,1)}, u32[]{:S(2)}) copy-start(bf16[1024,1,1408]{2,0,1:T(8,128)(2,1)} %multiply_convert_fusion.1) | copy-start | bytes 8650756
  1462.8 9.1 copy-start.89
  1476.3 40.3 %copy-start.81 = (bf16[128,16]{0,1:T(8,128)(2,1)}, bf16[128,16]{0,1:T(8,128)(2,1)S(1)}, u32[]{:S(2)}) copy-start(bf16[128,16]{0,1:T(8,128)(2,1)S(1)} %fusion.96) | copy-start | bytes 12292
  1498.9 17.8 copy-start.29
  1498.9 17.8 copy-start.38
  1498.9 17.8 copy-start.79
  1498.9 17.8 copy-start.96
  1498.9 20.2 copy-start.106
  1519.1 8.1 copy-start.60
  1527.1 7.7 copy-start.36
  1527.2 19.4 slice-start.2
  1534.8 11.7 slice-start.3
  1552.6 7.8 slice-start.4
  1558.8 207.6 %collective-permute-start.1 = (bf16[128,4160]{0,1:T(8,128)(2,1)}, bf16[128,4160]{0,1:T(8,128)(2,1)}, u32[]{:S(2)}, u32[]{:S(2)}) collective-permute-start(bf16[128,4160]{0,1:T(8,128)(2,1)} %pad_maximum_fusion.5), channel_id=1, source_target_pairs={{1,0},{3,2},{5,4},{7,6},{9,8},{11,10},{13,12},{15,14},{17,16},{19,... | collective-permute-start | bytes 3194888 | tf_op jit(solution)/shard_map/ppermute | solution.py:25
  1747.8 473.4 %reduce-scatter.12.cloned.1.call-start = ((), (), s32[]{:S(2)}) async-start(), calls=%async_computation.9 | async-start | bytes 28655616
  1754.9 10.5 copy-start.8
  1754.9 10.5 copy-start.10
  1754.9 11.0 copy-start.69
  1754.9 11.0 copy-start.73
  1754.9 11.0 copy-start.75
  1801.2 11.9 copy-start.42
  1804.1 9.1 copy-start.11
  1889.8 677.5 %reduce-scatter.14.cloned.1.call-start = ((), (), s32[]{:S(2)}) async-start(), calls=%async_computation.10 | async-start | bytes 36225024
  1909.8 9.1 copy-start.23
  1909.8 9.1 copy-start.82
  1909.8 10.4 copy-start.86
  1969.6 48.1 %copy-start.102 = (f32[128]{0:T(128)S(1)}, f32[128]{0:T(128)}, u32[]{:S(2)}) copy-start(f32[128]{0:T(128)} %copy-done.101) | copy-start | bytes 1540
  1969.6 48.1 %copy-start.14 = (f32[128,2048]{1,0:T(8,128)S(1)}, f32[128,2048]{1,0:T(8,128)}, u32[]{:S(2)}) copy-start(f32[128,2048]{1,0:T(8,128)} %copy-done.12) | copy-start | bytes 3145732
  1969.6 48.1 %copy-start.43 = (f32[128,2048]{1,0:T(8,128)S(1)}, f32[128,2048]{1,0:T(8,128)}, u32[]{:S(2)}) copy-start(f32[128,2048]{1,0:T(8,128)} %get-tuple-element.111) | copy-start | bytes 3145732
  (67 other events, 228.2 us)
Sparse Core Ops, SparseCore 0:
  16.8 302.5 all-gather.6
  322.3 368.9 all-gather.8
  692.8 52.6 all-gather.10
  1748.0 27.3 reduce-scatter.9
  1889.9 297.5 reduce-scatter.11
  2189.7 377.5 reduce-scatter.13

commit v2 on v1

--- a/solution.py
+++ b/solution.py
@@ -15,8 +15,6 @@
 ALL = ("expert", "shard")
 EPSILON = 1e-06
 THETA = 10000.0
-ALIGN = 8192
-ROW = 1024
 
 
 def passed_along(value, axis, steps):
@@ -71,36 +69,49 @@
     return jnp.where(visible[None], (plain_part + rotary_part) * factor, -1e30)
 
 
-def flat_pack(parts):
-    flats = [part.reshape(part.shape[0], -1) for part in parts]
-    sizes = [flat.shape[1] for flat in flats]
-    pad = (-sum(sizes)) % ALIGN
+def swap_shard(value):
+    return lax.ppermute(value, "shard", [(0, 1), (1, 0)])
+
+
+def gather_blocks(local):
+    side = lax.axis_index("shard")
+    mine = lax.all_gather(local, "expert", axis=0, tiled=False)
+    partner = swap_shard(mine)
+    lower = jnp.where(side == 0, mine, partner)
+    upper = jnp.where(side == 0, partner, mine)
+    return jnp.stack([lower, upper], axis=1)
+
+
+def gather_rows(local):
+    blocks = gather_blocks(local)
+    return blocks.reshape((-1,) + local.shape[1:])
+
+
+def scatter_blocks(blocks):
+    side = lax.axis_index("shard")
+    mine = lax.dynamic_index_in_dim(blocks, side, axis=1, keepdims=False)
+    theirs = lax.dynamic_index_in_dim(blocks, 1 - side, axis=1, keepdims=False)
+    arrived = swap_shard(theirs.astype(jnp.bfloat16))
+    total = (mine + arrived.astype(jnp.float32)).astype(jnp.bfloat16)
+    rows = total.reshape((-1,) + total.shape[2:])
+    return lax.psum_scatter(rows, "expert", scatter_dimension=0, tiled=True)
+
+
+def scatter_rows(full, experts):
+    blocks = full.reshape((experts, 2, -1) + full.shape[1:])
+    return scatter_blocks(blocks).astype(jnp.float32)
+
+
+def pack_small(parts, devices):
+    packed = jnp.concatenate(parts, axis=1)
+    pad = (-packed.shape[1]) % 1024
     if pad:
-        flats.append(jnp.zeros((flats[0].shape[0], pad), flats[0].dtype))
-    return jnp.concatenate(flats, axis=1), sizes
-
-
-def flat_unpack(packed, sizes, shapes):
-    pieces = []
-    offset = 0
-    for size, shape in zip(sizes, shapes):
-        pieces.append(packed[:, offset : offset + size].reshape((packed.shape[0],) + shape))
-        offset += size
-    return pieces
-
-
-def gather_packed(parts, axis):
-    packed, sizes = flat_pack([part[None] for part in parts])
-    gathered = lax.all_gather(packed[0], axis, axis=0, tiled=False)
-    return flat_unpack(gathered, sizes, [part.shape for part in parts])
-
-
-def scatter_packed(parts, axis, count):
-    packed, sizes = flat_pack([part.reshape((count, -1)) for part in parts])
-    rows = packed.reshape(-1, ROW)
-    local = lax.psum_scatter(rows, axis, scatter_dimension=0, tiled=True).reshape(1, -1)
-    shapes = [(part.shape[0] // count,) + part.shape[1:] for part in parts]
-    return [piece[0] for piece in flat_unpack(local, sizes, shapes)]
+        packed = jnp.concatenate([packed, jnp.zeros((devices, pad), packed.dtype)], axis=1)
+    return packed
+
+
+def gated_pair(gate_part, up_part):
+    return jax.nn.silu(gate_part) * up_part
 
 
 def shards(
@@ -138,28 +149,34 @@
     remote_mask = jnp.broadcast_to(side_index == 1, (tok_rows, tok_rows))
     visible = jnp.concatenate([remote_mask, local_mask], axis=1)
 
-    q_g, down_g, up_g, out_t_g, gain_one_g, gain_latent_g = gather_packed(
-        [query_weight, latent_down, latent_up, output_weight.T, attention_gain, latent_gain], ALL
-    )
-    query_full = q_g.reshape(-1, q_g.shape[-1])
-    down_full = down_g.reshape(-1, down_g.shape[-1])
-    up_full = up_g.reshape(-1, up_g.shape[-1])
-    output_t_full = out_t_g.reshape(-1, out_t_g.shape[-1])
-    gain_one_float = gain_one_g.reshape(-1).astype(jnp.float32)
-    gain_latent_float = gain_latent_g.reshape(-1).astype(jnp.float32)
-
-    si_g, so_t_g, router_g, gain_two_g = gather_packed(
-        [jnp.transpose(shared_inner, (1, 0, 2)), shared_outer.T, router_weight, feedforward_gain],
-        ALL,
-    )
-    shared_in_full = si_g.reshape((-1,) + si_g.shape[2:])
-    shared_out_t_full = so_t_g.reshape(-1, so_t_g.shape[-1])
-    router_full = router_g.reshape(-1, router_g.shape[-1])
-    gain_two_float = gain_two_g.reshape(-1).astype(jnp.float32)
-
-    ei_g, eo_g = gather_packed([expert_inner[0], expert_outer[0]], "shard")
-    inner_halves = ei_g
-    outer_matrix = eo_g.reshape(-1, eo_g.shape[-1])
+    small_sizes = [attention_gain.shape[0], latent_gain.shape[0], feedforward_gain.shape[0]]
+    small_local = jnp.concatenate(
+        [attention_gain, latent_gain, feedforward_gain, router_weight.reshape(-1)]
+    )
+    small_all = lax.all_gather(small_local, ALL, axis=0, tiled=False)
+    cut_one, cut_two, cut_three = (
+        small_sizes[0],
+        small_sizes[0] + small_sizes[1],
+        sum(small_sizes),
+    )
+    gain_one_float = small_all[:, :cut_one].reshape(-1).astype(jnp.float32)
+    gain_latent_float = small_all[:, cut_one:cut_two].reshape(-1).astype(jnp.float32)
+    gain_two_float = small_all[:, cut_two:cut_three].reshape(-1).astype(jnp.float32)
+    router_full = small_all[:, cut_three:].reshape(-1, router_weight.shape[1])
+
+    down_full = gather_rows(latent_down)
+    query_full = gather_rows(query_weight)
+    up_full = gather_rows(latent_up)
+    output_t_full = gather_rows(output_weight.T)
+    inner_blocks = gather_blocks(shared_inner.reshape(-1, shared_inner.shape[-1]))
+    inner_blocks = inner_blocks.reshape(inner_blocks.shape[:2] + shared_inner.shape)
+    shared_in_full = jnp.transpose(inner_blocks, (2, 0, 1, 3, 4)).reshape(
+        (shared_inner.shape[0], -1, shared_inner.shape[-1])
+    )
+    shared_out_t_full = gather_rows(shared_outer.T)
+
+    inner_halves = (expert_inner[0], swap_shard(expert_inner[0]))
+    outer_halves = (expert_outer[0], swap_shard(expert_outer[0]))
 
     tokens_float = tokens_in.astype(jnp.float32)
     normed_one = norm_rows(tokens_float, gain_one_float).astype(jnp.bfloat16)
@@ -232,34 +249,33 @@
     arrived = incoming[:, 0].reshape(-1, D)
     delta_arrived = incoming[:, 1].reshape(-1, D)
 
-    expert_pre = jnp.einsum(
-        "rd,sgdf->rgsf", arrived, inner_halves, preferred_element_type=jnp.float32
-    ).reshape(arrived.shape[0], 2, -1)
-    expert_hidden = gated(expert_pre).astype(jnp.bfloat16)
-    expert_result = matmul(expert_hidden, outer_matrix).astype(jnp.bfloat16)
-    delta_outer_matrix = jnp.einsum(
-        "rf,rd->fd", expert_hidden, delta_arrived, preferred_element_type=jnp.float32
-    )
-    delta_expert_hidden = jnp.einsum(
-        "rd,fd->rf", delta_arrived, outer_matrix, preferred_element_type=jnp.float32
-    )
-    unused_expert, expert_back = jax.vjp(gated, expert_pre)
-    delta_expert_pre = expert_back(delta_expert_hidden)[0].astype(jnp.bfloat16)
-    delta_pre_halves = delta_expert_pre.reshape(arrived.shape[0], 2, shard_count, -1)
-    delta_inner_halves = jnp.einsum(
-        "rd,rgsf->sgdf", arrived, delta_pre_halves, preferred_element_type=jnp.float32
-    )
-    delta_rows = jnp.einsum(
-        "rgsf,sgdf->rd", delta_pre_halves, inner_halves, preferred_element_type=jnp.float32
-    ).astype(jnp.bfloat16)
-    delta_expert_inner, delta_expert_outer = scatter_packed(
-        [
-            delta_inner_halves.astype(jnp.bfloat16),
-            delta_outer_matrix.astype(jnp.bfloat16).reshape(shard_count, -1, D),
-        ],
-        "shard",
-        shard_count,
-    )
+    expert_pre = [
+        jnp.einsum("rd,gdf->rgf", arrived, weight, preferred_element_type=jnp.float32)
+        for weight in inner_halves
+    ]
+    expert_hidden = [gated(pre).astype(jnp.bfloat16) for pre in expert_pre]
+    expert_result = sum(
+        matmul(hidden, weight) for hidden, weight in zip(expert_hidden, outer_halves)
+    ).astype(jnp.bfloat16)
+    delta_outer_halves = [
+        jnp.einsum("rf,rd->fd", hidden, delta_arrived, preferred_element_type=jnp.float32)
+        for hidden in expert_hidden
+    ]
+    delta_pre_halves = []
+    for pre, weight in zip(expert_pre, outer_halves):
+        delta_hidden = jnp.einsum(
+            "rd,fd->rf", delta_arrived, weight, preferred_element_type=jnp.float32
+        )
+        unused_expert, expert_back = jax.vjp(gated, pre)
+        delta_pre_halves.append(expert_back(delta_hidden)[0].astype(jnp.bfloat16))
+    delta_inner_halves = [
+        jnp.einsum("rd,rgf->gdf", arrived, delta_pre, preferred_element_type=jnp.float32)
+        for delta_pre in delta_pre_halves
+    ]
+    delta_rows = sum(
+        jnp.einsum("rgf,gdf->rd", delta_pre, weight, preferred_element_type=jnp.float32)
+        for delta_pre, weight in zip(delta_pre_halves, inner_halves)
+    ).astype(jnp.bfloat16)
     going_back = jnp.stack(
         [
             expert_result.reshape(experts_all, slot_cap, D),
@@ -270,29 +286,28 @@
     coming_back = lax.all_to_all(going_back, "expert", split_axis=0, concat_axis=0, tiled=True)
     returned = coming_back[:, 0].reshape(-1, D)
     delta_returned = coming_back[:, 1].reshape(-1, D)
+    inner_from_partner = swap_shard(delta_inner_halves[1].astype(jnp.bfloat16))
+    outer_from_partner = swap_shard(delta_outer_halves[1].astype(jnp.bfloat16))
+    delta_expert_inner = delta_inner_halves[0] + inner_from_partner.astype(jnp.float32)
+    delta_expert_outer = delta_outer_halves[0] + outer_from_partner.astype(jnp.float32)
 
     picked = jnp.take(returned, slot_of, axis=0).reshape(tok_rows, TOPK, D).astype(jnp.float32)
     routed = jnp.sum(gate_values[..., None] * picked, axis=1)
-    shared_pre = jnp.einsum(
-        "td,dgf->tgf", normed_two, shared_in_full, preferred_element_type=jnp.float32
-    )
-    shared_hidden = gated(shared_pre).astype(jnp.bfloat16)
+    shared_gate = matmul(normed_two, shared_in_full[0])
+    shared_up = matmul(normed_two, shared_in_full[1])
+    shared_hidden = gated_pair(shared_gate, shared_up).astype(jnp.bfloat16)
     shared_result = jnp.einsum(
         "tf,df->td", shared_hidden, shared_out_t_full, preferred_element_type=jnp.float32
     )
     feedforward = routed + shared_result
     layer_output = (residual + feedforward).astype(jnp.bfloat16)
-    square_sums = lax.psum(
-        jnp.stack(
-            [
-                jnp.sum(residual * residual),
-                jnp.sum(attention_out * attention_out),
-                jnp.sum(feedforward * feedforward),
-            ]
-        ),
-        ALL,
-    )
-    statistics = jnp.sqrt(square_sums / (tok_rows * D * devices))
+    square_sums = jnp.stack(
+        [
+            jnp.sum(residual * residual),
+            jnp.sum(attention_out * attention_out),
+            jnp.sum(feedforward * feedforward),
+        ]
+    )
 
     delta_shared_outer_t = jnp.einsum(
         "td,tf->df", cotangent, shared_hidden, preferred_element_type=jnp.float32
@@ -300,13 +315,18 @@
     delta_shared_hidden = jnp.einsum(
         "td,df->tf", cotangent, shared_out_t_full, preferred_element_type=jnp.float32
     )
-    unused_shared, shared_back = jax.vjp(gated, shared_pre)
-    delta_shared_pre = shared_back(delta_shared_hidden)[0].astype(jnp.bfloat16)
-    delta_shared_inner_t = jnp.einsum(
-        "td,tgf->dgf", normed_two, delta_shared_pre, preferred_element_type=jnp.float32
-    )
-    delta_normed = jnp.einsum(
-        "tgf,dgf->td", delta_shared_pre, shared_in_full, preferred_element_type=jnp.float32
+    unused_shared, shared_back = jax.vjp(gated_pair, shared_gate, shared_up)
+    delta_gate, delta_up = [
+        part.astype(jnp.bfloat16) for part in shared_back(delta_shared_hidden)
+    ]
+    delta_shared_inner = jnp.stack(
+        [
+            jnp.einsum("td,tf->df", normed_two, part, preferred_element_type=jnp.float32)
+            for part in (delta_gate, delta_up)
+        ]
+    )
+    delta_normed = matmul(delta_gate, shared_in_full[0].T) + matmul(
+        delta_up, shared_in_full[1].T
     )
     delta_gates = jnp.sum(delta_out[:, None, :] * picked, axis=-1)
     delta_normed = delta_normed + jnp.sum(
@@ -327,25 +347,22 @@
     unused_second, second_back = jax.vjp(norm_rows, residual, gain_two_float)
     delta_residual_norm, delta_gain_two = second_back(delta_normed)
     delta_residual = delta_out + delta_residual_norm
-    ffn_grads = scatter_packed(
-        [
-            delta_shared_inner_t.astype(jnp.bfloat16),
-            delta_shared_outer_t.astype(jnp.bfloat16),
-            delta_router.astype(jnp.bfloat16),
-            delta_gain_two.astype(jnp.bfloat16),
-        ],
-        ALL,
-        devices,
-    )
-    delta_shared_inner = jnp.transpose(ffn_grads[0], (1, 0, 2)).astype(jnp.float32)
-    delta_shared_outer = ffn_grads[1].T.astype(jnp.float32)
-    delta_router_local = ffn_grads[2].astype(jnp.float32)
-    delta_gain_two_local = ffn_grads[3].astype(jnp.float32)
+    inner_grad_blocks = jnp.transpose(
+        delta_shared_inner.reshape(
+            (shared_inner.shape[0], experts_all, shard_count) + shared_inner.shape[1:]
+        ),
+        (1, 2, 0, 3, 4),
+    ).reshape((experts_all, shard_count, -1, shared_inner.shape[-1]))
+    delta_shared_inner_local = (
+        scatter_blocks(inner_grad_blocks).astype(jnp.float32).reshape(shared_inner.shape)
+    )
+    delta_shared_outer_local = scatter_rows(delta_shared_outer_t, experts_all).T
 
     delta_attention = delta_residual.astype(jnp.bfloat16)
     delta_output_t = jnp.einsum(
         "td,tc->dc", delta_attention, mixed_heads, preferred_element_type=jnp.float32
     )
+    delta_output_local = scatter_rows(delta_output_t, experts_all).T
     delta_mixed = (
         jnp.einsum("td,dc->tc", delta_attention, output_t_full, preferred_element_type=jnp.float32)
         .astype(jnp.bfloat16)
@@ -399,6 +416,7 @@
     delta_latent_up = jnp.einsum(
         "tl,tc->lc", latents, delta_expanded, preferred_element_type=jnp.float32
     )
+    delta_latent_up_local = scatter_rows(delta_latent_up, experts_all)
     delta_latents = jnp.einsum(
         "tc,lc->tl", delta_expanded, up_full, preferred_element_type=jnp.float32
     )
@@ -424,39 +442,46 @@
     delta_query_weight = jnp.einsum(
         "td,tc->dc", normed_one, delta_query_raw, preferred_element_type=jnp.float32
     )
+    delta_latent_down_local = scatter_rows(delta_latent_down, experts_all)
+    delta_query_local = scatter_rows(delta_query_weight, experts_all)
     delta_normed_one = jnp.einsum(
         "tc,dc->td", delta_query_raw, query_full, preferred_element_type=jnp.float32
     ) + jnp.einsum("tc,dc->td", delta_down_out, down_full, preferred_element_type=jnp.float32)
     unused_first, first_back = jax.vjp(norm_rows, tokens_float, gain_one_float)
     delta_tokens_norm, delta_gain_one = first_back(delta_normed_one)
     input_gradient = (delta_residual + delta_tokens_norm).astype(jnp.bfloat16)
-    att_grads = scatter_packed(
-        [
-            delta_query_weight.astype(jnp.bfloat16),
-            delta_latent_down.astype(jnp.bfloat16),
-            delta_latent_up.astype(jnp.bfloat16),
-            delta_output_t.astype(jnp.bfloat16),
-            delta_gain_one.astype(jnp.bfloat16),
-            delta_gain_latent.astype(jnp.bfloat16),
-        ],
-        ALL,
-        devices,
-    )
+
+    small_parts = [
+        delta_gain_one.reshape(devices, -1),
+        delta_gain_latent.reshape(devices, -1),
+        delta_gain_two.reshape(devices, -1),
+        delta_router.reshape(devices, -1),
+        jnp.broadcast_to(square_sums[None], (devices, 3)),
+    ]
+    small_packed = pack_small(small_parts, devices)
+    small_sum = lax.psum_scatter(
+        small_packed.reshape(-1, 128), ALL, scatter_dimension=0, tiled=True
+    ).reshape(-1)
+    small_cuts = [0]
+    for part in small_parts:
+        small_cuts.append(small_cuts[-1] + part.shape[1])
+    small_pieces = [small_sum[small_cuts[i] : small_cuts[i + 1]] for i in range(len(small_parts))]
+    statistics = jnp.sqrt(small_pieces[4] / (tok_rows * D * devices))
     return (
         layer_output,
         input_gradient,
-        att_grads[4].astype(jnp.float32),
-        att_grads[0].astype(jnp.float32),
-        att_grads[1].astype(jnp.float32),
-        att_grads[5].astype(jnp.float32),
-        att_grads[2].astype(jnp.float32),
-        att_grads[3].T.astype(jnp.float32),
-        delta_gain_two_local,
-        delta_router_local,
-        delta_shared_inner,
-        delta_shared_outer,
-        delta_expert_inner.astype(jnp.float32),
-        delta_expert_outer.astype(jnp.float32),
+        small_pieces[0],
+        delta_query_local,
+        delta_latent_down_local,
+        small_pieces[1],
+        delta_latent_up_local,
+        delta_output_local,
+        small_pieces[2],
+        small_pieces[3].reshape(router_weight.shape),
+        delta_shared_inner_local,
+        delta_shared_outer_local,
+        delta_expert_inner[None],
+        delta_expert_outer[None],
         statistics,
     )
 

time: 2620 us -> 1970 us (0.75)
  local copies, waits for them, and re-layouts: 1010 us -> 203 us
  waiting for transfers between devices: 770 us -> 1230 us
  other arithmetic: 487 us -> 235 us
  blocking collectives: 45.4 us -> 0 us
    reduce_scatter x1 -> x7, waiting for transfers between devices: 0.01 us -> 646 us  [the longest x6 638 us: scatter_blocks(): return lax.psum_scatter(rows, 'expert', scatter_dimension=0, tiled=True)]
    unnamed x284 -> x263, local copies, waits for them, and re-layouts: 338 us -> 36.9 us
    unnamed x8 -> x15, waiting for transfers between devices: 330 us -> 71.9 us
    reshape x12 -> x7, local copies, waits for them, and re-layouts: 230 us -> 3.32 us  [the longest x1 1.86 us: shards(): delta_router.reshape(devices, -1)]
    concatenate x1, other arithmetic: 153 us -> 0.06 us  [shards(): jnp.concatenate([delta_query_plain, rotate(delta_query_rotary, cosine_tab...]
    convert_element_type x20 -> x13, other arithmetic: 201 us -> 60.6 us  [the longest x6 54.3 us: scatter_blocks(): total = (mine + arrived.astype(jnp.float32)).astype(jnp.bfloat16)]
    another operation x13 -> x0, local copies, waits for them, and re-layouts: 117 us -> none  [the longest x1 42 us: shards(): shared_in_full = si_g.reshape((-1,) + si_g.shape[2:])]
    another operation x6 -> x18, other arithmetic: 2.25 us -> 87.7 us  [the longest x10 51.3 us: gather_blocks(): return jnp.stack([lower, upper], axis=1)]
  transfers between devices with their start and end apart: 10 -> 34, of which waited for: 4 -> 17; matrix products, arithmetic and copies ran while one was open for 55% -> 31% of each run, Pallas kernels for 0% -> 0%
where the time goes in v2:
time: 1970 us; the launch traced here: 1960 us
  waiting for transfers between devices  1230 us (62%)
  other arithmetic  235 us (12%)
  matrix products  213 us (11%)
  local copies, waits for them, and re-layouts  203 us (10%)
  starting transfers between devices  58.6 us (3%)
    reduce_scatter x6, waiting for transfers between devices, scatter_blocks(): return lax.psum_scatter(rows, 'expert', scatter_dimension=0, tiled=True)  638 us
    all_gather x6, waiting for transfers between devices, gather_blocks(): mine = lax.all_gather(local, 'expert', axis=0, tiled=False)  416 us
    unnamed x15, waiting for transfers between devices  71.9 us
    all_to_all x1, waiting for transfers between devices, shards(): lax.all_to_all(going_back, 'expert', split_axis=0, concat_axis=0, tiled=T...  58.5 us
    convert_element_type x6, other arithmetic, scatter_blocks(): total = (mine + arrived.astype(jnp.float32)).astype(jnp.bfloat16)  54.3 us
    dot_general x10, matrix products, matmul(): return jnp.dot(left_side, right_side, preferred_element_type=jnp.float32)  51.7 us
    another operation x10, other arithmetic, gather_blocks(): return jnp.stack([lower, upper], axis=1)  51.3 us
  transfers between devices with their start and end apart: 34, of which 17 were waited for; matrix products, arithmetic and copies ran while one was open for 31% of the time, Pallas kernels for 0%

profile of v2, /device:TPU:0, one launch (start us, length us, event | category | flops | bytes accessed | tf_op | source)
XLA Modules:
  0.0 1956.3 jit_solution(8957940418632440866)
XLA Ops:
  16.9 54.2 %all-gather.15.cloned.1.call-done = bf16[1024,576]{1,0:T(8,128)(2,1)} async-done(((bf16[64,576]{1,0:T(8,128)(2,1)}), bf16[1024,576]{1,0:T(8,128)(2,1)}) %all-gather.15.cloned.1.call-update) | async-done | bytes 1179664 | tf_op jit(solution)/shard_map/all_gather | solution.py:78
  75.5 68.1 %all-reduce.10.cloned.1.call-done = bf16[37376]{0:T(1024)(128)(2,1)} async-done(((bf16[37376]{0:T(1024)(128)(2,1)}), bf16[37376]{0:T(1024)(128)(2,1)}) %all-reduce.10.cloned.1.call-update) | async-done | bytes 74768
  149.0 79.0 %all-gather.19.cloned.1.call-done = bf16[1024,3072]{1,0:T(8,128)(2,1)} async-done(((bf16[64,3072]{1,0:T(8,128)(2,1)}), bf16[1024,3072]{1,0:T(8,128)(2,1)}) %all-gather.19.cloned.1.call-update) | async-done | bytes 6291472 | tf_op jit(solution)/shard_map/all_gather | solution.py:78
  233.3 71.4 %all-gather.21.cloned.1.call-done = bf16[1024,2048]{1,0:T(8,128)(2,1)} async-done(((bf16[64,2048]{1,0:T(8,128)(2,1)}), bf16[1024,2048]{1,0:T(8,128)(2,1)}) %all-gather.21.cloned.1.call-update) | async-done | bytes 4194320 | tf_op jit(solution)/shard_map/all_gather | solution.py:78
  320.4 6.9 gather_fusion.1
  339.2 7.6 pad_maximum_fusion.3
  357.6 15.6 copy.183
  373.2 6.6 fusion.63
  401.3 6.0 gather_fusion
  416.3 6.4 pad_maximum_fusion.4
  422.7 6.6 all-to-all-start
  430.0 9.2 collective-permute-done.8
  439.2 9.6 select_bitcast_fusion.3
  448.8 9.8 pad_maximum_fusion.2
  458.5 211.0 %all-gather.13.cloned.1.call-done = bf16[16,128,2816]{2,1,0:T(8,128)(2,1)} async-done(((bf16[1,128,2816]{2,1,0:T(8,128)(2,1)}), bf16[16,128,2816]{2,1,0:T(8,128)(2,1)}) %all-gather.13.cloned.1.call-update) | async-done | bytes 11534352 | tf_op jit(solution)/shard_map/all_gather | solution.py:78
  676.5 10.5 fusion.123
  693.7 6.1 fusion.21
  699.7 8.6 fusion.148
  710.9 6.2 multiply_bitcast_fusion
  717.1 13.5 add_convert_fusion
  730.6 7.2 fusion.68
  737.9 8.8 fusion.6
  746.7 6.2 pad_maximum_fusion.5
  752.9 38.9 %all-to-all-start.1 = ((bf16[16,2,64,2048]{3,2,1,0:T(8,128)(2,1)}), bf16[16,2,64,2048]{3,2,1,0:T(8,128)(2,1)}, u32[]{:S(2)}, u32[]{:S(2)}) async-start(bf16[16,2,64,2048]{3,2,1,0:T(8,128)(2,1)} %pad_maximum_fusion.5), calls=%async_computation.1 | async-start | bytes 16777216 | tf_op jit(solution)/shard_map/all_to_all | solution.py:286
  791.9 12.4 broadcast_select_fusion.1
  804.3 8.8 maximum_bitcast_fusion
  813.1 5.9 fusion.140
  819.1 6.3 copy.200
  840.8 9.4 fusion.158
  850.3 7.5 fusion.8
  862.1 8.2 mul.559
  870.4 9.0 fusion.151
  879.4 9.5 fusion.156
  888.9 9.4 fusion.157
  898.4 9.9 fusion.4
  908.4 58.5 %all-to-all-done.1 = bf16[16,2,64,2048]{3,2,1,0:T(8,128)(2,1)} async-done(((bf16[16,2,64,2048]{3,2,1,0:T(8,128)(2,1)}), bf16[16,2,64,2048]{3,2,1,0:T(8,128)(2,1)}, u32[]{:S(2)}, u32[]{:S(2)}) %all-to-all-start.1) | async-done | bytes 8388640 | tf_op jit(solution)/shard_map/all_to_all | solution.py:286
  966.8 6.3 fusion.141
  973.1 9.9 gather_fusion.5
  983.0 9.8 gather_fusion.4
  992.8 8.5 select_convert_fusion
  1005.7 7.9 reshape.616
  1013.6 7.0 reduce_sum.196
  1020.6 8.3 reshape.615
  1029.1 9.0 fusion.27
  1044.4 10.8 multiply_reduce_fusion.3
  1087.0 6.6 fusion.56
  1106.4 34.0 %pad_maximum_fusion = f32[2,16,2,64,2816]{4,3,0,2,1:T(8,128)} fusion(f32[1,16,2,64,2816]{4,3,0,2,1:T(8,128)} %bitcast.404, f32[1,16,2,64,2816]{4,3,0,2,1:T(8,128)} %bitcast.403), kind=kLoop, calls=%fused_computation.7 | loop fusion | flops 11534336 | bytes 92274688 | tf_op jit(solution)/shard_map/stack | solution.py:322
  1144.2 12.7 fusion.2
  1173.1 7.8 collective-permute-done.13
  1180.9 8.4 fusion.5
  1189.5 16.3 fusion
  1210.1 10.3 fusion.153
  1226.1 10.3 collective-permute-done.10
  1236.3 11.4 fusion.1
  1249.6 9.1 convert_bitcast_fusion
  1258.9 6.3 convolution_convert_fusion.1
  1265.5 6.8 collective-permute-done.17
  1277.3 9.1 fusion.3
  1288.3 7.4 reduce-scatter.8.cloned.1.call-done
  1301.0 72.7 %reduce-scatter.12.cloned.1.call-done = bf16[64,576]{1,0:T(8,128)(2,1)} async-done(((bf16[1024,576]{1,0:T(8,128)(2,1)}), bf16[64,576]{1,0:T(8,128)(2,1)}) %reduce-scatter.12.cloned.1.call-update) | async-done | bytes 73744 | tf_op jit(solution)/shard_map/reduce_scatter | solution.py:97
  1375.3 78.7 %reduce-scatter.14.cloned.1.call-done = bf16[16,4096]{1,0:T(8,128)(2,1)} async-done(((bf16[256,4096]{1,0:T(8,128)(2,1)}), bf16[16,4096]{1,0:T(8,128)(2,1)}) %reduce-scatter.14.cloned.1.call-update) | async-done | bytes 131088 | tf_op jit(solution)/shard_map/reduce_scatter | solution.py:97
  1455.6 92.5 %reduce-scatter.16.cloned.1.call-done = bf16[64,2048]{1,0:T(8,128)(2,1)} async-done(((bf16[1024,2048]{1,0:T(8,128)(2,1)}), bf16[64,2048]{1,0:T(8,128)(2,1)}) %reduce-scatter.16.cloned.1.call-update) | async-done | bytes 262160 | tf_op jit(solution)/shard_map/reduce_scatter | solution.py:97
  1549.9 240.8 %reduce-scatter.18.cloned.1.call-done = bf16[128,2816]{1,0:T(8,128)(2,1)} async-done(((bf16[2048,2816]{1,0:T(8,128)(2,1)}), bf16[128,2816]{1,0:T(8,128)(2,1)}) %reduce-scatter.18.cloned.1.call-update) | async-done | bytes 720912 | tf_op jit(solution)/shard_map/reduce_scatter | solution.py:97
  1793.0 153.7 %reduce-scatter.10.cloned.1.call-done = bf16[64,3072]{1,0:T(8,128)(2,1)} async-done(((bf16[1024,3072]{1,0:T(8,128)(2,1)}), bf16[64,3072]{1,0:T(8,128)(2,1)}) %reduce-scatter.10.cloned.1.call-update) | async-done | bytes 393232 | tf_op jit(solution)/shard_map/reduce_scatter | solution.py:97
  (489 shorter events, 237.2 us)
Async XLA Ops:
  8.0 63.1 %all-gather.15.cloned.1.call-start = ((), (), s32[]{:S(2)}) async-start(), calls=%async_computation.17 | async-start | bytes 1392640 | tf_op jit(solution)/shard_map/all_gather | solution.py:78
  8.7 134.8 %all-reduce.10.cloned.1.call-start = ((), (), s32[]{:S(2)}) async-start(), calls=%async_computation.22 | async-start | bytes 151552
  12.7 131.9 %all-gather.17.cloned.1.call-start = ((), (), s32[]{:S(2)}) async-start(), calls=%async_computation.18 | async-start | bytes 2228224 | tf_op jit(solution)/shard_map/all_gather | solution.py:78
  13.5 214.5 %all-gather.19.cloned.1.call-start = ((), (), s32[]{:S(2)}) async-start(), calls=%async_computation.19 | async-start | bytes 6684672 | tf_op jit(solution)/shard_map/all_gather | solution.py:78
  14.2 290.6 %all-gather.21.cloned.1.call-start = ((), (), s32[]{:S(2)}) async-start(), calls=%async_computation.20 | async-start | bytes 4456448 | tf_op jit(solution)/shard_map/all_gather | solution.py:78
  14.8 414.6 %all-gather.23.cloned.1.call-start = ((), (), s32[]{:S(2)}) async-start(), calls=%async_computation.21 | async-start | bytes 6127616 | tf_op jit(solution)/shard_map/all_gather | solution.py:78
  15.4 654.2 %all-gather.13.cloned.1.call-start = ((), (), s32[]{:S(2)}) async-start(), calls=%async_computation.9 | async-start | bytes 12255232 | tf_op jit(solution)/shard_map/all_gather | solution.py:78
  16.8 213.0 %copy-start.62 = (s32[128,6]{1,0:T(8,128)}, s32[128,6]{1,0:T(8,128)S(1)}, u32[]{:S(2)}) copy-start(s32[128,6]{1,0:T(8,128)S(1)} %copy.191) | copy-start | bytes 9220
  71.1 74.9 %collective-permute-start = (bf16[16,64,576]{2,1,0:T(8,128)(2,1)}, bf16[16,64,576]{2,1,0:T(8,128)(2,1)}, u32[]{:S(2)}, u32[]{:S(2)}) collective-permute-start(bf16[16,64,576]{2,1,0:T(8,128)(2,1)} %bitcast.461), channel_id=1, source_target_pairs={{0,1},{1,0},{2,3},{3,2},{4,5},{5,4},{6,7},{7,6},{8,9},{9,8},{10,11... | collective-permute-start | bytes 3538952 | tf_op jit(solution)/shard_map/ppermute | solution.py:73
  71.9 244.6 %copy-start.83 = (s32[768]{0:T(1024)}, s32[768]{0:T(1024)S(1)}, u32[]{:S(2)}) copy-start(s32[768]{0:T(1024)S(1)} %eq.71) | copy-start | bytes 9220
  74.2 158.4 %copy-start.97 = (f32[32]{0:T(128)}, f32[32]{0:T(128)S(1)}, u32[]{:S(2)}) copy-start(f32[32]{0:T(128)S(1)} %multiply_power_fusion) | copy-start | bytes 388
  74.2 158.4 %copy-start.99 = (f32[128]{0:T(128)}, f32[128]{0:T(128)S(1)}, u32[]{:S(2)}) copy-start(f32[128]{0:T(128)S(1)} %get-tuple-element.152) | copy-start | bytes 1540
  75.4 154.3 %copy-start.103 = (f32[128]{0:T(128)}, f32[128]{0:T(128)S(1)}, u32[]{:S(2)}) copy-start(f32[128]{0:T(128)S(1)} %fusion.60) | copy-start | bytes 1540
  75.5 297.7 %copy-start.87 = (f32[128]{0:T(128)}, f32[128]{0:T(128)S(1)}, u32[]{:S(2)}) copy-start(f32[128]{0:T(128)S(1)} %fusion.109) | copy-start | bytes 1540
  144.7 160.3 %collective-permute-start.1 = (bf16[16,16,4096]{2,1,0:T(8,128)(2,1)}, bf16[16,16,4096]{2,1,0:T(8,128)(2,1)}, u32[]{:S(2)}, u32[]{:S(2)}) collective-permute-start(bf16[16,16,4096]{2,1,0:T(8,128)(2,1)} %bitcast.458), channel_id=1, source_target_pairs={{0,1},{1,0},{2,3},{3,2},{4,5},{5,4},{6,7},{7,6},{8,9},{9,8},{10,11... | collective-permute-start | bytes 6291464 | tf_op jit(solution)/shard_map/ppermute | solution.py:73
  145.8 227.4 %copy-start.64 = (f32[2048]{0:T(1024)}, f32[2048]{0:T(1024)S(1)}, u32[]{:S(2)}) copy-start(f32[2048]{0:T(1024)S(1)} %reshape.612) | copy-start | bytes 24580
  145.9 158.9 %copy-start.89 = (f32[512]{0:T(512)}, f32[512]{0:T(512)S(1)}, u32[]{:S(2)}) copy-start(f32[512]{0:T(512)S(1)} %reshape.613) | copy-start | bytes 6148
  145.9 85.4 %copy-start.9 = (bf16[128,2048]{1,0:T(8,128)(2,1)S(1)}, bf16[128,2048]{1,0:T(8,128)(2,1)}, u32[]{:S(2)}) copy-start(bf16[128,2048]{1,0:T(8,128)(2,1)} %param.17) | copy-start | bytes 1572868
  228.0 118.8 %collective-permute-start.3 = (bf16[16,64,3072]{2,1,0:T(8,128)(2,1)}, bf16[16,64,3072]{2,1,0:T(8,128)(2,1)}, u32[]{:S(2)}, u32[]{:S(2)}) collective-permute-start(bf16[16,64,3072]{2,1,0:T(8,128)(2,1)} %bitcast.432), channel_id=1, source_target_pairs={{0,1},{1,0},{2,3},{3,2},{4,5},{5,4},{6,7},{7,6},{8,9},{9,8},{10,11... | collective-permute-start | bytes 18874376 | tf_op jit(solution)/shard_map/ppermute | solution.py:73
  232.5 75.0 %copy-start.37 = (f32[128,576]{0,1:T(8,128)}, f32[128,576]{0,1:T(8,128)S(1)}, u32[]{:S(2)}) copy-start(f32[128,576]{0,1:T(8,128)S(1)} %fusion.137) | copy-start | bytes 884740
  232.6 75.0 %copy-start.105 = (f32[128]{0:T(128)}, f32[128]{0:T(128)S(1)}, u32[]{:S(2)}) copy-start(f32[128]{0:T(128)S(1)} %multiply_reduce_fusion.11) | copy-start | bytes 1540
  233.3 146.5 %copy-start.73 = (f32[128,32]{0,1:T(8,128)}, f32[128,32]{0,1:T(8,128)S(1)}, u32[]{:S(2)}) copy-start(f32[128,32]{0,1:T(8,128)S(1)} %get-tuple-element.139) | copy-start | bytes 49156
  233.3 147.1 %copy-start.77 = (bf16[128,32]{0,1:T(8,128)(2,1)}, bf16[128,32]{0,1:T(8,128)(2,1)S(1)}, u32[]{:S(2)}) copy-start(bf16[128,32]{0,1:T(8,128)(2,1)S(1)} %get-tuple-element.137) | copy-start | bytes 24580
  233.3 147.1 %copy-start.79 = (bf16[128,32]{0,1:T(8,128)(2,1)}, bf16[128,32]{0,1:T(8,128)(2,1)S(1)}, u32[]{:S(2)}) copy-start(bf16[128,32]{0,1:T(8,128)(2,1)S(1)} %get-tuple-element.138) | copy-start | bytes 24580
  304.8 28.5 %collective-permute-start.4 = (bf16[16,64,2048]{2,1,0:T(8,128)(2,1)}, bf16[16,64,2048]{2,1,0:T(8,128)(2,1)}, u32[]{:S(2)}, u32[]{:S(2)}) collective-permute-start(bf16[16,64,2048]{2,1,0:T(8,128)(2,1)} %bitcast.441), channel_id=1, source_target_pairs={{0,1},{1,0},{2,3},{3,2},{4,5},{5,4},{6,7},{7,6},{8,9},{9,8},{10,11... | collective-permute-start | bytes 12582920 | tf_op jit(solution)/shard_map/ppermute | solution.py:73
  312.9 15.6 collective-permute-start.2
  327.5 61.6 %copy-start.75 = (f32[2048]{0:T(1024)}, f32[2048]{0:T(1024)S(1)}, u32[]{:S(2)}) copy-start(f32[2048]{0:T(1024)S(1)} %reshape.614) | copy-start | bytes 24580
  327.9 61.7 %copy-start.33 = (bf16[2048,16]{1,0:T(8,128)(2,1)}, bf16[2048,16]{1,0:T(8,128)(2,1)S(1)}, u32[]{:S(2)}) copy-start(bf16[2048,16]{1,0:T(8,128)(2,1)S(1)} %reshape.587) | copy-start | bytes 196612
  328.4 53.4 %copy-start.12 = (bf16[128,16,256]{2,0,1:T(8,128)(2,1)}, bf16[128,16,256]{2,0,1:T(8,128)(2,1)S(1)}, u32[]{:S(2)}) copy-start(bf16[128,16,256]{2,0,1:T(8,128)(2,1)S(1)} %copy.181) | copy-start | bytes 3145732
  332.6 49.3 %copy-start.14 = (bf16[128,16,256]{2,0,1:T(8,128)(2,1)}, bf16[128,16,256]{2,0,1:T(8,128)(2,1)S(1)}, u32[]{:S(2)}) copy-start(bf16[128,16,256]{2,0,1:T(8,128)(2,1)S(1)} %copy.180) | copy-start | bytes 3145732
  333.3 47.2 %copy-start.71 = (bf16[128,64]{0,1:T(8,128)(2,1)}, bf16[128,64]{0,1:T(8,128)(2,1)S(1)}, u32[]{:S(2)}) copy-start(bf16[128,64]{0,1:T(8,128)(2,1)S(1)} %slice.213) | copy-start | bytes 49156
  422.7 249.7 %all-to-all-start = ((bf16[16,2,64,2048]{3,2,1,0:T(8,128)(2,1)}), bf16[16,2,64,2048]{3,2,1,0:T(8,128)(2,1)}, u32[]{:S(2)}, u32[]{:S(2)}) async-start(bf16[16,2,64,2048]{3,2,1,0:T(8,128)(2,1)} %pad_maximum_fusion.4), calls=%async_computation | async-start | bytes 16777216 | tf_op jit(solution)/shard_map/all_to_all | solution.py:248
  429.4 9.8 collective-permute-start.8
  429.4 270.3 %collective-permute-start.5 = (bf16[2,2048,704]{1,2,0:T(8,128)(2,1)}, bf16[2,2048,704]{1,2,0:T(8,128)(2,1)}, u32[]{:S(2)}, u32[]{:S(2)}) collective-permute-start(bf16[2,2048,704]{1,2,0:T(8,128)(2,1)} %bitcast.472), channel_id=1, source_target_pairs={{0,1},{1,0},{2,3},{3,2},{4,5},{5,4},{6,7},{7,6},{8,9},{9,8},{10,11... | collective-permute-start | bytes 17301512 | tf_op jit(solution)/shard_map/ppermute | solution.py:73
  429.9 278.4 %collective-permute-start.6 = (bf16[704,2048]{1,0:T(8,128)(2,1)S(1)}, bf16[704,2048]{1,0:T(8,128)(2,1)}, u32[]{:S(2)}, u32[]{:S(2)}) collective-permute-start(bf16[704,2048]{1,0:T(8,128)(2,1)S(1)} %bitcast.475), channel_id=1, source_target_pairs={{0,1},{1,0},{2,3},{3,2},{4,5},{5,4},{6,7},{7,6},{8,9},{9,8},{10,11... | collective-permute-start | bytes 8650760 | tf_op jit(solution)/shard_map/ppermute | solution.py:73
  669.6 122.3 %collective-permute-start.7 = (bf16[16,128,2816]{2,1,0:T(8,128)(2,1)}, bf16[16,128,2816]{2,1,0:T(8,128)(2,1)}, u32[]{:S(2)}, u32[]{:S(2)}) collective-permute-start(bf16[16,128,2816]{2,1,0:T(8,128)(2,1)} %all-gather.13.cloned.1.call-done), channel_id=1, source_target_pairs={{0,1},{1,0},{2,3},{3,2},{4,5},{5,4},{6,7},{7,6},{8,9},{9,8},{10,11... | collective-permute-start | bytes 34603016 | tf_op jit(solution)/shard_map/ppermute | solution.py:73
  676.5 23.3 %copy-start.41 = (bf16[16,1,64,2048]{3,2,1,0:T(8,128)(2,1)}, bf16[16,1,64,2048]{3,2,1,0:T(8,128)(2,1)S(1)}, u32[]{:S(2)}) copy-start(bf16[16,1,64,2048]{3,2,1,0:T(8,128)(2,1)S(1)} %get-tuple-element.103) | copy-start | bytes 12582916
  676.5 31.9 %copy-start.43 = (bf16[16,1,64,2048]{3,2,1,0:T(8,128)(2,1)}, bf16[16,1,64,2048]{3,2,1,0:T(8,128)(2,1)S(1)}, u32[]{:S(2)}) copy-start(bf16[16,1,64,2048]{3,2,1,0:T(8,128)(2,1)S(1)} %get-tuple-element.104) | copy-start | bytes 12582916
  710.9 19.7 %slice-start.12 = ((s8[5767168]{0:T(1024)(128)(4,1)}), s8[4194304]{0:T(1024)(128)(4,1)S(1)}, s32[]{:S(2)}) async-start(s8[5767168]{0:T(1024)(128)(4,1)} %bitcast.473), calls=%async_computation.35 | async-start | bytes 8388608
  717.0 20.8 %copy-start.46 = (f32[1024,1,704]{0,2,1:T(8,128)}, f32[1024,1,704]{0,2,1:T(8,128)S(1)}, u32[]{:S(2)}) copy-start(f32[1024,1,704]{0,2,1:T(8,128)S(1)} %get-tuple-element.97) | copy-start | bytes 8650756
  717.1 20.8 %copy-start.48 = (f32[1024,1,704]{0,2,1:T(8,128)}, f32[1024,1,704]{0,2,1:T(8,128)S(1)}, u32[]{:S(2)}) copy-start(f32[1024,1,704]{0,2,1:T(8,128)S(1)} %get-tuple-element.98) | copy-start | bytes 8650756
  717.1 13.6 slice-start.13
  717.1 13.5 copy-start.110
  717.1 13.5 copy-start.112
  752.9 213.9 %all-to-all-start.1 = ((bf16[16,2,64,2048]{3,2,1,0:T(8,128)(2,1)}), bf16[16,2,64,2048]{3,2,1,0:T(8,128)(2,1)}, u32[]{:S(2)}, u32[]{:S(2)}) async-start(bf16[16,2,64,2048]{3,2,1,0:T(8,128)(2,1)} %pad_maximum_fusion.5), calls=%async_computation.1 | async-start | bytes 16777216 | tf_op jit(solution)/shard_map/all_to_all | solution.py:286
  791.9 494.6 %reduce-scatter.20.cloned.1.call-start = ((), (), s32[]{:S(2)}) async-start(), calls=%async_computation.16 | async-start | bytes 6127616 | tf_op jit(solution)/shard_map/reduce_scatter | solution.py:97
  840.8 48.1 %copy-start.49 = (bf16[128,2816]{1,0:T(8,128)(2,1)}, bf16[128,2816]{1,0:T(8,128)(2,1)S(1)}, u32[]{:S(2)}) copy-start(bf16[128,2816]{1,0:T(8,128)(2,1)S(1)} %get-tuple-element.109) | copy-start | bytes 2162692
  857.8 40.6 %collective-permute-start.15 = (bf16[16,64,2816]{2,1,0:T(8,128)(2,1)}, bf16[16,64,2816]{2,1,0:T(8,128)(2,1)}, u32[]{:S(2)}, u32[]{:S(2)}) collective-permute-start(bf16[16,64,2816]{2,1,0:T(8,128)(2,1)} %fusion.8), channel_id=1, source_target_pairs={{0,1},{1,0},{2,3},{3,2},{4,5},{5,4},{6,7},{7,6},{8,9},{9,8},{10,11... | collective-permute-start | bytes 17301512 | tf_op jit(solution)/shard_map/ppermute | solution.py:73
  908.3 387.4 %reduce-scatter.8.cloned.1.call-start = ((), (), s32[]{:S(2)}) async-start(), calls=%async_computation.10 | async-start | bytes 270336 | tf_op jit(solution)/shard_map/reduce_scatter | solution.py:462
  1040.3 15.9 slice-start.2
  1066.5 10.4 collective-permute-start.9
  1095.9 44.5 %collective-permute-start.11 = (bf16[16,64,576]{2,1,0:T(8,128)(2,1)S(1)}, bf16[16,64,576]{2,1,0:T(8,128)(2,1)}, u32[]{:S(2)}, u32[]{:S(2)}) collective-permute-start(bf16[16,64,576]{2,1,0:T(8,128)(2,1)S(1)} %fusion.48), channel_id=1, source_target_pairs={{0,1},{1,0},{2,3},{3,2},{4,5},{5,4},{6,7},{7,6},{8,9},{9,8},{10,11... | collective-permute-start | bytes 3538952 | tf_op jit(solution)/shard_map/ppermute | solution.py:73
  1104.2 64.2 %collective-permute-start.12 = (bf16[16,16,4096]{2,1,0:T(8,128)(2,1)}, bf16[16,16,4096]{2,1,0:T(8,128)(2,1)}, u32[]{:S(2)}, u32[]{:S(2)}) collective-permute-start(bf16[16,16,4096]{2,1,0:T(8,128)(2,1)} %fusion.28), channel_id=1, source_target_pairs={{0,1},{1,0},{2,3},{3,2},{4,5},{5,4},{6,7},{7,6},{8,9},{9,8},{10,11... | collective-permute-start | bytes 6291464 | tf_op jit(solution)/shard_map/ppermute | solution.py:73
  1106.3 267.4 %reduce-scatter.12.cloned.1.call-start = ((), (), s32[]{:S(2)}) async-start(), calls=%async_computation.12 | async-start | bytes 1392640 | tf_op jit(solution)/shard_map/reduce_scatter | solution.py:97
  1144.0 310.0 %reduce-scatter.14.cloned.1.call-start = ((), (), s32[]{:S(2)}) async-start(), calls=%async_computation.13 | async-start | bytes 2228224 | tf_op jit(solution)/shard_map/reduce_scatter | solution.py:97
  1156.9 32.5 %collective-permute-start.14 = (bf16[16,128,2816]{2,1,0:T(8,128)(2,1)}, bf16[16,128,2816]{2,1,0:T(8,128)(2,1)}, u32[]{:S(2)}, u32[]{:S(2)}) collective-permute-start(bf16[16,128,2816]{2,1,0:T(8,128)(2,1)} %fusion.2), channel_id=1, source_target_pairs={{0,1},{1,0},{2,3},{3,2},{4,5},{5,4},{6,7},{7,6},{8,9},{9,8},{10,11... | collective-permute-start | bytes 34603016 | tf_op jit(solution)/shard_map/ppermute | solution.py:73
  1167.8 13.1 collective-permute-start.13
  1173.1 375.1 %reduce-scatter.16.cloned.1.call-start = ((), (), s32[]{:S(2)}) async-start(), calls=%async_computation.14 | async-start | bytes 4456448 | tf_op jit(solution)/shard_map/reduce_scatter | solution.py:97
  1189.4 601.3 %reduce-scatter.18.cloned.1.call-start = ((), (), s32[]{:S(2)}) async-start(), calls=%async_computation.15 | async-start | bytes 12255232 | tf_op jit(solution)/shard_map/reduce_scatter | solution.py:97
  1205.8 741.0 %reduce-scatter.10.cloned.1.call-start = ((), (), s32[]{:S(2)}) async-start(), calls=%async_computation.11 | async-start | bytes 6684672 | tf_op jit(solution)/shard_map/reduce_scatter | solution.py:97
  1226.0 10.4 collective-permute-start.10
  1258.7 13.6 copy-start.54
  1258.7 18.6 collective-permute-start.16
  1265.2 7.1 collective-permute-start.17
  (99 other events, 536.8 us)
Sparse Core Ops, SparseCore 0:
  11.6 59.4 all-gather.14
  73.8 59.1 all-gather.16
  135.8 92.1 all-gather.18
  230.6 74.1 all-gather.20
  307.3 87.5 all-gather.22
  397.6 271.9 all-gather.12
  908.4 181.1 reduce-scatter.19
  1106.4 189.2 reduce-scatter.7
  1298.6 75.1 reduce-scatter.11
  1375.9 78.0 reduce-scatter.13
  1456.3 91.7 reduce-scatter.15
  1550.3 240.4 reduce-scatter.17
  1796.0 150.7 reduce-scatter.9
Sparse Core Ops, SparseCore 1:
  15.4 128.1 all-reduce.9

commit v3 on v2

--- a/solution.py
+++ b/solution.py
@@ -73,41 +73,49 @@
     return lax.ppermute(value, "shard", [(0, 1), (1, 0)])
 
 
-def gather_blocks(local):
+def gather_over_expert(local, by_exchange):
+    if by_exchange:
+        copies = jnp.broadcast_to(local[None], (lax.axis_size("expert"),) + local.shape)
+        return lax.all_to_all(copies, "expert", split_axis=0, concat_axis=0, tiled=True)
+    return lax.all_gather(local, "expert", axis=0, tiled=False)
+
+
+def gather_halves(local, by_exchange=False):
     side = lax.axis_index("shard")
-    mine = lax.all_gather(local, "expert", axis=0, tiled=False)
+    mine = gather_over_expert(local, by_exchange)
     partner = swap_shard(mine)
-    lower = jnp.where(side == 0, mine, partner)
-    upper = jnp.where(side == 0, partner, mine)
-    return jnp.stack([lower, upper], axis=1)
-
-
-def gather_rows(local):
-    blocks = gather_blocks(local)
-    return blocks.reshape((-1,) + local.shape[1:])
-
-
-def scatter_blocks(blocks):
+    return jnp.where(side == 0, mine, partner), jnp.where(side == 0, partner, mine)
+
+
+def assemble(halves, first=None, last=None):
+    lower, upper = [half[:, first:last] for half in halves]
+    full = jnp.stack([lower, upper], axis=1)
+    return full.reshape((-1,) + full.shape[3:])
+
+
+def gather_rows(local, by_exchange=False):
+    return assemble(gather_halves(local, by_exchange))
+
+
+def pair_total(blocks):
     side = lax.axis_index("shard")
     mine = lax.dynamic_index_in_dim(blocks, side, axis=1, keepdims=False)
     theirs = lax.dynamic_index_in_dim(blocks, 1 - side, axis=1, keepdims=False)
     arrived = swap_shard(theirs.astype(jnp.bfloat16))
-    total = (mine + arrived.astype(jnp.float32)).astype(jnp.bfloat16)
+    return (mine + arrived.astype(jnp.float32)).astype(jnp.bfloat16)
+
+
+def reduce_over_expert(total, by_exchange=False):
+    if by_exchange:
+        got = lax.all_to_all(total, "expert", split_axis=0, concat_axis=0, tiled=True)
+        return jnp.sum(got.astype(jnp.float32), axis=0)
     rows = total.reshape((-1,) + total.shape[2:])
-    return lax.psum_scatter(rows, "expert", scatter_dimension=0, tiled=True)
-
-
-def scatter_rows(full, experts):
+    return lax.psum_scatter(rows, "expert", scatter_dimension=0, tiled=True).astype(jnp.float32)
+
+
+def scatter_rows(full, experts, by_exchange=False):
     blocks = full.reshape((experts, 2, -1) + full.shape[1:])
-    return scatter_blocks(blocks).astype(jnp.float32)
-
-
-def pack_small(parts, devices):
-    packed = jnp.concatenate(parts, axis=1)
-    pad = (-packed.shape[1]) % 1024
-    if pad:
-        packed = jnp.concatenate([packed, jnp.zeros((devices, pad), packed.dtype)], axis=1)
-    return packed
+    return reduce_over_expert(pair_total(blocks), by_exchange)
 
 
 def gated_pair(gate_part, up_part):
@@ -149,31 +157,47 @@
     remote_mask = jnp.broadcast_to(side_index == 1, (tok_rows, tok_rows))
     visible = jnp.concatenate([remote_mask, local_mask], axis=1)
 
-    small_sizes = [attention_gain.shape[0], latent_gain.shape[0], feedforward_gain.shape[0]]
+    small_sizes = [
+        attention_gain.shape[0],
+        latent_gain.shape[0],
+        feedforward_gain.shape[0],
+        router_weight.size,
+    ]
     small_local = jnp.concatenate(
         [attention_gain, latent_gain, feedforward_gain, router_weight.reshape(-1)]
     )
-    small_all = lax.all_gather(small_local, ALL, axis=0, tiled=False)
-    cut_one, cut_two, cut_three = (
-        small_sizes[0],
-        small_sizes[0] + small_sizes[1],
-        sum(small_sizes),
-    )
-    gain_one_float = small_all[:, :cut_one].reshape(-1).astype(jnp.float32)
-    gain_latent_float = small_all[:, cut_one:cut_two].reshape(-1).astype(jnp.float32)
-    gain_two_float = small_all[:, cut_two:cut_three].reshape(-1).astype(jnp.float32)
-    router_full = small_all[:, cut_three:].reshape(-1, router_weight.shape[1])
-
-    down_full = gather_rows(latent_down)
+    width = latent_down.shape[1]
+    small_rows = -(-small_local.shape[0] // width)
+    small_local = jnp.concatenate(
+        [small_local, jnp.zeros((small_rows * width - small_local.shape[0],), jnp.bfloat16)]
+    ).reshape(small_rows, width)
+    down_rows = latent_down.shape[0]
+    down_halves = gather_halves(jnp.concatenate([latent_down, small_local], axis=0))
+    down_full = assemble(down_halves, 0, down_rows)
+    small_all = assemble(down_halves, down_rows).reshape(devices, -1)
+    cuts = [0]
+    for size in small_sizes:
+        cuts.append(cuts[-1] + size)
+    gain_one_float = small_all[:, cuts[0] : cuts[1]].reshape(-1).astype(jnp.float32)
+    gain_latent_float = small_all[:, cuts[1] : cuts[2]].reshape(-1).astype(jnp.float32)
+    gain_two_float = small_all[:, cuts[2] : cuts[3]].reshape(-1).astype(jnp.float32)
+    router_full = small_all[:, cuts[3] : cuts[4]].reshape(-1, router_weight.shape[1])
+
     query_full = gather_rows(query_weight)
     up_full = gather_rows(latent_up)
     output_t_full = gather_rows(output_weight.T)
-    inner_blocks = gather_blocks(shared_inner.reshape(-1, shared_inner.shape[-1]))
-    inner_blocks = inner_blocks.reshape(inner_blocks.shape[:2] + shared_inner.shape)
-    shared_in_full = jnp.transpose(inner_blocks, (2, 0, 1, 3, 4)).reshape(
-        (shared_inner.shape[0], -1, shared_inner.shape[-1])
-    )
-    shared_out_t_full = gather_rows(shared_outer.T)
+    inner_rows = shared_inner.shape[0] * shared_inner.shape[1]
+    ffn_halves = gather_halves(
+        jnp.concatenate(
+            [shared_inner.reshape(inner_rows, shared_inner.shape[-1]), shared_outer.T], axis=0
+        ),
+        by_exchange=True,
+    )
+    shared_in_full = [
+        assemble(ffn_halves, g * shared_inner.shape[1], (g + 1) * shared_inner.shape[1])
+        for g in range(shared_inner.shape[0])
+    ]
+    shared_out_t_full = assemble(ffn_halves, inner_rows)
 
     inner_halves = (expert_inner[0], swap_shard(expert_inner[0]))
     outer_halves = (expert_outer[0], swap_shard(expert_outer[0]))
@@ -353,10 +377,15 @@
         ),
         (1, 2, 0, 3, 4),
     ).reshape((experts_all, shard_count, -1, shared_inner.shape[-1]))
-    delta_shared_inner_local = (
-        scatter_blocks(inner_grad_blocks).astype(jnp.float32).reshape(shared_inner.shape)
-    )
-    delta_shared_outer_local = scatter_rows(delta_shared_outer_t, experts_all).T
+    outer_grad_blocks = delta_shared_outer_t.reshape(
+        (experts_all, shard_count, -1, delta_shared_outer_t.shape[-1])
+    )
+    ffn_total = jnp.concatenate(
+        [pair_total(inner_grad_blocks), pair_total(outer_grad_blocks)], axis=1
+    )
+    ffn_local = reduce_over_expert(ffn_total, by_exchange=True)
+    delta_shared_inner_local = ffn_local[:inner_rows].reshape(shared_inner.shape)
+    delta_shared_outer_local = ffn_local[inner_rows:].T
 
     delta_attention = delta_residual.astype(jnp.bfloat16)
     delta_output_t = jnp.einsum(
@@ -443,7 +472,7 @@
         "td,tc->dc", normed_one, delta_query_raw, preferred_element_type=jnp.float32
     )
     delta_latent_down_local = scatter_rows(delta_latent_down, experts_all)
-    delta_query_local = scatter_rows(delta_query_weight, experts_all)
+    delta_query_local = scatter_rows(delta_query_weight, experts_all, by_exchange=True)
     delta_normed_one = jnp.einsum(
         "tc,dc->td", delta_query_raw, query_full, preferred_element_type=jnp.float32
     ) + jnp.einsum("tc,dc->td", delta_down_out, down_full, preferred_element_type=jnp.float32)
@@ -458,10 +487,10 @@
         delta_router.reshape(devices, -1),
         jnp.broadcast_to(square_sums[None], (devices, 3)),
     ]
-    small_packed = pack_small(small_parts, devices)
-    small_sum = lax.psum_scatter(
-        small_packed.reshape(-1, 128), ALL, scatter_dimension=0, tiled=True
-    ).reshape(-1)
+    small_packed = jnp.concatenate(small_parts, axis=1)
+    small_sum = lax.dynamic_index_in_dim(
+        lax.psum(small_packed, ALL), lax.axis_index(ALL), axis=0, keepdims=False
+    )
     small_cuts = [0]
     for part in small_parts:
         small_cuts.append(small_cuts[-1] + part.shape[1])

time: 1970 us -> 2410 us (1.22)
  waiting for transfers between devices: 1230 us -> 1510 us
  starting transfers between devices: 58.6 us -> 196 us
    reduce_scatter x7 -> x3, waiting for transfers between devices: 646 us -> 250 us  [reduce_over_expert(): lax.psum_scatter(rows, 'expert', scatter_dimension=0, tiled=True)]
    psum x0 -> x1, waiting for transfers between devices: none -> 369 us  [shards(): lax.psum(small_packed, ALL)]
    all_to_all x0 -> x3, waiting for transfers between devices: none -> 310 us  [the longest x1 243 us: gather_over_expert(): lax.all_to_all(copies, 'expert', split_axis=0, concat_axis=0, tiled=True)]
    all_to_all x1, waiting for transfers between devices: 2.85 us -> 154 us  [shards(): lax.all_to_all(outgoing, 'expert', split_axis=0, concat_axis=0, tiled=True)]
    all_gather x6 -> x4, waiting for transfers between devices: 416 us -> 272 us  [gather_over_expert(): return lax.all_gather(local, 'expert', axis=0, tiled=False)]
    all_to_all x0 -> x3, starting transfers between devices: none -> 106 us  [the longest x2 66.3 us: reduce_over_expert(): lax.all_to_all(total, 'expert', split_axis=0, concat_axis=0, tiled=True)]
    all_to_all x1, waiting for transfers between devices: 58.5 us -> 136 us  [shards(): lax.all_to_all(going_back, 'expert', split_axis=0, concat_axis=0, tiled=T...]
    unnamed x15 -> x8, waiting for transfers between devices: 71.9 us -> 1.98 us
  transfers between devices with their start and end apart: 34 -> 30, of which waited for: 17 -> 16; matrix products, arithmetic and copies ran while one was open for 31% -> 17% of each run, Pallas kernels for 0% -> 0%
where the time goes in v3:
time: 2410 us; the launch traced here: 2400 us
  waiting for transfers between devices  1510 us (63%)
  other arithmetic  239 us (10%)
  local copies, waits for them, and re-layouts  223 us (9%)
  matrix products  216 us (9%)
  starting transfers between devices  196 us (8%)
    psum x1, waiting for transfers between devices, shards(): lax.psum(small_packed, ALL)  369 us
    all_gather x4, waiting for transfers between devices, gather_over_expert(): return lax.all_gather(local, 'expert', axis=0, tiled=False)  272 us
    reduce_scatter x3, waiting for transfers between devices, reduce_over_expert(): lax.psum_scatter(rows, 'expert', scatter_dimension=0, tiled=True)  250 us
    all_to_all x1, waiting for transfers between devices, gather_over_expert(): lax.all_to_all(copies, 'expert', split_axis=0, concat_axis=0, tiled=True)  243 us
    all_to_all x1, waiting for transfers between devices, shards(): lax.all_to_all(outgoing, 'expert', split_axis=0, concat_axis=0, tiled=True)  154 us
    all_to_all x1, waiting for transfers between devices, shards(): lax.all_to_all(going_back, 'expert', split_axis=0, concat_axis=0, tiled=T...  136 us
    all_to_all x1, starting transfers between devices, shards(): lax.all_to_all(going_back, 'expert', split_axis=0, concat_axis=0, tiled=T...  75.6 us
    all_to_all x2, waiting for transfers between devices, reduce_over_expert(): lax.all_to_all(total, 'expert', split_axis=0, concat_axis=0, tiled=True)  66.5 us
  transfers between devices with their start and end apart: 30, of which 16 were waited for; matrix products, arithmetic and copies ran while one was open for 17% of the time, Pallas kernels for 0%

profile of v3, /device:TPU:0, one launch (start us, length us, event | category | flops | bytes accessed | tf_op | source)
XLA Modules:
  0.0 2401.7 jit_solution(6610873538366034397)
XLA Ops:
  14.0 58.3 %all-gather.16.cloned.1.call-done = bf16[16,67,576]{2,1,0:T(8,128)(2,1)} async-done(((bf16[1,67,576]{2,1,0:T(8,128)(2,1)}), bf16[16,67,576]{2,1,0:T(8,128)(2,1)}) %all-gather.16.cloned.1.call-update) | async-done | bytes 1234960 | tf_op jit(solution)/shard_map/all_gather | solution.py:80
  83.1 51.1 %all-gather.10.cloned.1.call-done = bf16[256,4096]{1,0:T(8,128)(2,1)} async-done(((bf16[16,4096]{1,0:T(8,128)(2,1)}), bf16[256,4096]{1,0:T(8,128)(2,1)}) %all-gather.10.cloned.1.call-update) | async-done | bytes 2097168 | tf_op jit(solution)/shard_map/all_gather | solution.py:80
  139.2 90.0 %all-gather.12.cloned.1.call-done = bf16[1024,3072]{1,0:T(8,128)(2,1)} async-done(((bf16[64,3072]{1,0:T(8,128)(2,1)}), bf16[1024,3072]{1,0:T(8,128)(2,1)}) %all-gather.12.cloned.1.call-update) | async-done | bytes 6291472 | tf_op jit(solution)/shard_map/all_gather | solution.py:80
  233.1 73.0 %all-gather.14.cloned.1.call-done = bf16[1024,2048]{1,0:T(8,128)(2,1)} async-done(((bf16[64,2048]{1,0:T(8,128)(2,1)}), bf16[1024,2048]{1,0:T(8,128)(2,1)}) %all-gather.14.cloned.1.call-update) | async-done | bytes 4194320 | tf_op jit(solution)/shard_map/all_gather | solution.py:80
  324.0 6.9 gather_fusion.1
  343.6 7.5 pad_maximum_fusion.6
  362.0 15.8 copy.155
  377.8 6.6 fusion.63
  420.9 6.4 pad_maximum_fusion.7
  432.2 153.7 %all-to-all-done = bf16[16,2,64,2048]{3,2,1,0:T(8,128)(2,1)} async-done(((bf16[16,2,64,2048]{3,2,1,0:T(8,128)(2,1)}), bf16[16,2,64,2048]{3,2,1,0:T(8,128)(2,1)}, u32[]{:S(2)}, u32[]{:S(2)}) %all-to-all-start) | async-done | bytes 8388640 | tf_op jit(solution)/shard_map/all_to_all | solution.py:272
  585.9 6.1 broadcast_in_dim.151
  592.0 39.6 %all-to-all-start.2 = ((bf16[16,192,2816]{2,1,0:T(8,128)(2,1)}), bf16[16,192,2816]{2,1,0:T(8,128)(2,1)}, u32[]{:S(2)}, u32[]{:S(2)}) async-start(bf16[16,192,2816]{2,1,0:T(8,128)(2,1)} %broadcast_in_dim.151), calls=%async_computation.2 | async-start | bytes 34603008 | tf_op jit(solution)/shard_map/all_to_all | solution.py:79
  636.9 6.4 fusion.125
  649.9 6.2 fusion.21
  656.2 6.4 fusion.148
  665.1 7.7 multiply_bitcast_fusion
  672.8 12.7 add_convert_fusion
  685.5 8.6 fusion.68
  694.1 8.4 fusion.6
  702.5 6.4 pad_maximum_fusion.8
  708.9 243.1 %all-to-all-done.2 = bf16[16,192,2816]{2,1,0:T(8,128)(2,1)} async-done(((bf16[16,192,2816]{2,1,0:T(8,128)(2,1)}), bf16[16,192,2816]{2,1,0:T(8,128)(2,1)}, u32[]{:S(2)}, u32[]{:S(2)}) %all-to-all-start.2) | async-done | bytes 17301536 | tf_op jit(solution)/shard_map/all_to_all | solution.py:79
  952.0 75.6 %all-to-all-start.1 = ((bf16[16,2,64,2048]{3,2,1,0:T(8,128)(2,1)}), bf16[16,2,64,2048]{3,2,1,0:T(8,128)(2,1)}, u32[]{:S(2)}, u32[]{:S(2)}) async-start(bf16[16,2,64,2048]{3,2,1,0:T(8,128)(2,1)} %pad_maximum_fusion.8), calls=%async_computation.1 | async-start | bytes 16777216 | tf_op jit(solution)/shard_map/all_to_all | solution.py:310
  1032.1 8.2 mul.562
  1040.4 136.0 %all-to-all-done.1 = bf16[16,2,64,2048]{3,2,1,0:T(8,128)(2,1)} async-done(((bf16[16,2,64,2048]{3,2,1,0:T(8,128)(2,1)}), bf16[16,2,64,2048]{3,2,1,0:T(8,128)(2,1)}, u32[]{:S(2)}, u32[]{:S(2)}) %all-to-all-start.1) | async-done | bytes 8388640 | tf_op jit(solution)/shard_map/all_to_all | solution.py:310
  1176.3 6.1 fusion.142
  1182.5 9.8 gather_fusion.5
  1192.3 9.1 gather_fusion.4
  1205.7 7.3 select_convert_fusion
  1213.1 7.8 reshape.609
  1220.9 7.1 reduce_sum.212
  1227.9 8.0 reshape.608
  1236.1 7.6 multiply_reduce_fusion
  1243.7 17.8 broadcast_select_fusion.1
  1261.4 16.2 slice_bitcast_fusion
  1297.3 6.3 pad_maximum_fusion.3
  1308.3 8.3 fusion.150
  1316.7 8.4 fusion.27
  1327.2 7.5 multiply_reduce_fusion.3
  1366.4 6.8 fusion.56
  1377.9 10.3 fusion.152
  1388.3 8.3 fusion.7
  1398.7 9.3 fusion.155
  1408.0 9.4 fusion.156
  1417.3 34.1 %pad_maximum_fusion = f32[2,16,2,64,2816]{4,3,0,2,1:T(8,128)} fusion(f32[1,16,2,64,2816]{4,3,0,2,1:T(8,128)} %bitcast.416, f32[1,16,2,64,2816]{4,3,0,2,1:T(8,128)} %bitcast.415), kind=kLoop, calls=%fused_computation.7 | loop fusion | flops 11534336 | bytes 92274688 | tf_op jit(solution)/shard_map/stack | solution.py:346
  1451.4 12.5 fusion.2
  1463.9 11.5 fusion.1
  1475.3 36.9 %all-to-all-start.3 = ((bf16[16,64,3072]{2,1,0:T(8,128)(2,1)}), bf16[16,64,3072]{2,1,0:T(8,128)(2,1)}, u32[]{:S(2)}, u32[]{:S(2)}) async-start(bf16[16,64,3072]{2,1,0:T(8,128)(2,1)} %fusion.1), calls=%async_computation.3 | async-start | bytes 12582912 | tf_op jit(solution)/shard_map/all_to_all | solution.py:110
  1512.2 9.3 fusion.157
  1526.8 9.3 collective-permute-done.14
  1536.2 10.0 fusion.4
  1546.1 12.9 fusion
  1559.1 6.7 pad_maximum_fusion.1
  1565.8 66.5 %all-to-all-done.3 = bf16[16,64,3072]{2,1,0:T(8,128)(2,1)} async-done(((bf16[16,64,3072]{2,1,0:T(8,128)(2,1)}), bf16[16,64,3072]{2,1,0:T(8,128)(2,1)}, u32[]{:S(2)}, u32[]{:S(2)}) %all-to-all-start.3) | async-done | bytes 6291488 | tf_op jit(solution)/shard_map/all_to_all | solution.py:110
  1632.3 29.4 %all-to-all-start.4 = ((bf16[16,192,2816]{2,1,0:T(8,128)(2,1)}), bf16[16,192,2816]{2,1,0:T(8,128)(2,1)}, u32[]{:S(2)}, u32[]{:S(2)}) async-start(bf16[16,192,2816]{2,1,0:T(8,128)(2,1)} %pad_maximum_fusion.1), calls=%async_computation.7 | async-start | bytes 34603008 | tf_op jit(solution)/shard_map/all_to_all | solution.py:110
  1698.4 8.4 fusion.5
  1708.5 10.7 convert_bitcast_fusion
  1719.6 7.4 convolution_convert_fusion.1
  1733.1 7.5 add_bitcast_fusion
  1740.7 10.7 fusion.3
  1751.3 368.8 %all-reduce.9.cloned.1.call-done = f32[32,1171]{1,0:T(8,128)} async-done(((f32[32,1171]{1,0:T(8,128)}), f32[32,1171]{1,0:T(8,128)}) %all-reduce.9.cloned.1.call-update) | async-done | bytes 149904 | tf_op jit(solution)/shard_map/psum | solution.py:492
  2125.6 78.3 %reduce-scatter.4.cloned.1.call-done = bf16[64,576]{1,0:T(8,128)(2,1)} async-done(((bf16[1024,576]{1,0:T(8,128)(2,1)}), bf16[64,576]{1,0:T(8,128)(2,1)}) %reduce-scatter.4.cloned.1.call-update) | async-done | bytes 73744 | tf_op jit(solution)/shard_map/reduce_scatter | solution.py:113
  2205.5 78.7 %reduce-scatter.6.cloned.1.call-done = bf16[16,4096]{1,0:T(8,128)(2,1)} async-done(((bf16[256,4096]{1,0:T(8,128)(2,1)}), bf16[16,4096]{1,0:T(8,128)(2,1)}) %reduce-scatter.6.cloned.1.call-update) | async-done | bytes 131088 | tf_op jit(solution)/shard_map/reduce_scatter | solution.py:113
  2285.8 92.9 %reduce-scatter.8.cloned.1.call-done = bf16[64,2048]{1,0:T(8,128)(2,1)} async-done(((bf16[1024,2048]{1,0:T(8,128)(2,1)}), bf16[64,2048]{1,0:T(8,128)(2,1)}) %reduce-scatter.8.cloned.1.call-update) | async-done | bytes 262160 | tf_op jit(solution)/shard_map/reduce_scatter | solution.py:113
  2385.4 7.0 convert_reduce_fusion
  (489 shorter events, 263.6 us)
Async XLA Ops:
  7.2 69.6 %copy-start.91 = (s32[128,6]{0,1:T(8,128)S(1)}, s32[128,6]{0,1:T(8,128)}, u32[]{:S(2)}) copy-start(s32[128,6]{0,1:T(8,128)} %param.19) | copy-start | bytes 9220
  7.2 68.8 %copy-start.7 = (bf16[128,2048]{1,0:T(8,128)(2,1)S(1)}, bf16[128,2048]{1,0:T(8,128)(2,1)}, u32[]{:S(2)}) copy-start(bf16[128,2048]{1,0:T(8,128)(2,1)} %param.17) | copy-start | bytes 1572868
  7.2 65.1 %all-gather.16.cloned.1.call-start = ((), (), s32[]{:S(2)}) async-start(), calls=%async_computation.15 | async-start | bytes 1566720 | tf_op jit(solution)/shard_map/all_gather | solution.py:80
  11.9 122.3 %all-gather.10.cloned.1.call-start = ((), (), s32[]{:S(2)}) async-start(), calls=%async_computation.12 | async-start | bytes 2228224 | tf_op jit(solution)/shard_map/all_gather | solution.py:80
  12.7 216.6 %all-gather.12.cloned.1.call-start = ((), (), s32[]{:S(2)}) async-start(), calls=%async_computation.13 | async-start | bytes 6684672 | tf_op jit(solution)/shard_map/all_gather | solution.py:80
  13.4 292.6 %all-gather.14.cloned.1.call-start = ((), (), s32[]{:S(2)}) async-start(), calls=%async_computation.14 | async-start | bytes 4456448 | tf_op jit(solution)/shard_map/all_gather | solution.py:80
  75.0 3.5 collective-permute-start
  75.8 241.7 %copy-start.71 = (s32[128,6]{1,0:T(8,128)}, s32[128,6]{1,0:T(8,128)S(1)}, u32[]{:S(2)}) copy-start(s32[128,6]{1,0:T(8,128)S(1)} %copy.163) | copy-start | bytes 9220
  76.0 156.4 %copy-start.109 = (f32[32]{0:T(128)}, f32[32]{0:T(128)S(1)}, u32[]{:S(2)}) copy-start(f32[32]{0:T(128)S(1)} %multiply_power_fusion) | copy-start | bytes 388
  76.0 156.3 %copy-start.111 = (f32[128]{0:T(128)}, f32[128]{0:T(128)S(1)}, u32[]{:S(2)}) copy-start(f32[128]{0:T(128)S(1)} %get-tuple-element.139) | copy-start | bytes 1540
  76.8 301.0 %copy-start.99 = (f32[128]{0:T(128)}, f32[128]{0:T(128)S(1)}, u32[]{:S(2)}) copy-start(f32[128]{0:T(128)S(1)} %fusion.111) | copy-start | bytes 1540
  134.2 172.1 %collective-permute-start.1 = (bf16[16,16,4096]{2,1,0:T(8,128)(2,1)}, bf16[16,16,4096]{2,1,0:T(8,128)(2,1)}, u32[]{:S(2)}, u32[]{:S(2)}) collective-permute-start(bf16[16,16,4096]{2,1,0:T(8,128)(2,1)} %bitcast.459), channel_id=1, source_target_pairs={{0,1},{1,0},{2,3},{3,2},{4,5},{5,4},{6,7},{7,6},{8,9},{9,8},{10,11... | collective-permute-start | bytes 6291464 | tf_op jit(solution)/shard_map/ppermute | solution.py:73
  139.2 238.6 %copy-start.73 = (f32[2048]{0:T(1024)}, f32[2048]{0:T(1024)S(1)}, u32[]{:S(2)}) copy-start(f32[2048]{0:T(1024)S(1)} %reshape.605) | copy-start | bytes 24580
  229.2 121.9 %collective-permute-start.3 = (bf16[16,64,3072]{2,1,0:T(8,128)(2,1)}, bf16[16,64,3072]{2,1,0:T(8,128)(2,1)}, u32[]{:S(2)}, u32[]{:S(2)}) collective-permute-start(bf16[16,64,3072]{2,1,0:T(8,128)(2,1)} %bitcast.435), channel_id=1, source_target_pairs={{0,1},{1,0},{2,3},{3,2},{4,5},{5,4},{6,7},{7,6},{8,9},{9,8},{10,11... | collective-permute-start | bytes 18874376 | tf_op jit(solution)/shard_map/ppermute | solution.py:73
  232.1 76.7 %copy-start.44 = (f32[128,576]{0,1:T(8,128)}, f32[128,576]{0,1:T(8,128)S(1)}, u32[]{:S(2)}) copy-start(f32[128,576]{0,1:T(8,128)S(1)} %fusion.139) | copy-start | bytes 884740
  232.2 76.6 %copy-start.117 = (f32[128]{0:T(128)}, f32[128]{0:T(128)S(1)}, u32[]{:S(2)}) copy-start(f32[128]{0:T(128)S(1)} %multiply_reduce_fusion.11) | copy-start | bytes 1540
  233.1 151.4 %copy-start.82 = (f32[128,32]{0,1:T(8,128)}, f32[128,32]{0,1:T(8,128)S(1)}, u32[]{:S(2)}) copy-start(f32[128,32]{0,1:T(8,128)S(1)} %get-tuple-element.126) | copy-start | bytes 49156
  233.1 152.0 %copy-start.86 = (bf16[128,32]{0,1:T(8,128)(2,1)}, bf16[128,32]{0,1:T(8,128)(2,1)S(1)}, u32[]{:S(2)}) copy-start(bf16[128,32]{0,1:T(8,128)(2,1)S(1)} %get-tuple-element.124) | copy-start | bytes 24580
  233.1 152.0 %copy-start.88 = (bf16[128,32]{0,1:T(8,128)(2,1)}, bf16[128,32]{0,1:T(8,128)(2,1)S(1)}, u32[]{:S(2)}) copy-start(bf16[128,32]{0,1:T(8,128)(2,1)S(1)} %get-tuple-element.125) | copy-start | bytes 24580
  306.0 31.7 %collective-permute-start.4 = (bf16[16,64,2048]{2,1,0:T(8,128)(2,1)}, bf16[16,64,2048]{2,1,0:T(8,128)(2,1)}, u32[]{:S(2)}, u32[]{:S(2)}) collective-permute-start(bf16[16,64,2048]{2,1,0:T(8,128)(2,1)} %bitcast.442), channel_id=1, source_target_pairs={{0,1},{1,0},{2,3},{3,2},{4,5},{5,4},{6,7},{7,6},{8,9},{9,8},{10,11... | collective-permute-start | bytes 12582920 | tf_op jit(solution)/shard_map/ppermute | solution.py:73
  309.3 14.6 copy-start.30
  314.1 18.8 collective-permute-start.2
  331.1 62.5 %copy-start.84 = (f32[2048]{0:T(1024)}, f32[2048]{0:T(1024)S(1)}, u32[]{:S(2)}) copy-start(f32[2048]{0:T(1024)S(1)} %reshape.607) | copy-start | bytes 24580
  332.8 53.6 %copy-start.11 = (bf16[128,16,256]{2,0,1:T(8,128)(2,1)}, bf16[128,16,256]{2,0,1:T(8,128)(2,1)S(1)}, u32[]{:S(2)}) copy-start(bf16[128,16,256]{2,0,1:T(8,128)(2,1)S(1)} %copy.153) | copy-start | bytes 3145732
  337.0 49.5 %copy-start.14 = (bf16[128,16,256]{2,0,1:T(8,128)(2,1)}, bf16[128,16,256]{2,0,1:T(8,128)(2,1)S(1)}, u32[]{:S(2)}) copy-start(bf16[128,16,256]{2,0,1:T(8,128)(2,1)S(1)} %copy.152) | copy-start | bytes 3145732
  337.7 47.3 %copy-start.80 = (bf16[128,64]{0,1:T(8,128)(2,1)}, bf16[128,64]{0,1:T(8,128)(2,1)S(1)}, u32[]{:S(2)}) copy-start(bf16[128,64]{0,1:T(8,128)(2,1)S(1)} %slice.263) | copy-start | bytes 49156
  427.3 158.7 %all-to-all-start = ((bf16[16,2,64,2048]{3,2,1,0:T(8,128)(2,1)}), bf16[16,2,64,2048]{3,2,1,0:T(8,128)(2,1)}, u32[]{:S(2)}, u32[]{:S(2)}) async-start(bf16[16,2,64,2048]{3,2,1,0:T(8,128)(2,1)} %pad_maximum_fusion.7), calls=%async_computation | async-start | bytes 16777216 | tf_op jit(solution)/shard_map/all_to_all | solution.py:272
  592.0 39.7 %copy-start.121 = (bf16[1,704,2048]{2,1,0:T(8,128)(2,1)S(1)}, bf16[1,704,2048]{2,1,0:T(8,128)(2,1)}, u32[]{:S(2)}) copy-start(bf16[1,704,2048]{2,1,0:T(8,128)(2,1)} %param.31) | copy-start | bytes 8650756
  592.0 360.0 %all-to-all-start.2 = ((bf16[16,192,2816]{2,1,0:T(8,128)(2,1)}), bf16[16,192,2816]{2,1,0:T(8,128)(2,1)}, u32[]{:S(2)}, u32[]{:S(2)}) async-start(bf16[16,192,2816]{2,1,0:T(8,128)(2,1)} %broadcast_in_dim.151), calls=%async_computation.2 | async-start | bytes 34603008 | tf_op jit(solution)/shard_map/all_to_all | solution.py:79
  631.6 24.5 %collective-permute-start.5 = (bf16[2,2048,704]{1,2,0:T(8,128)(2,1)}, bf16[2,2048,704]{1,2,0:T(8,128)(2,1)S(1)}, u32[]{:S(2)}, u32[]{:S(2)}) collective-permute-start(bf16[2,2048,704]{1,2,0:T(8,128)(2,1)} %bitcast.468), channel_id=1, source_target_pairs={{0,1},{1,0},{2,3},{3,2},{4,5},{5,4},{6,7},{7,6},{8,9},{9,8},{10,11... | collective-permute-start | bytes 17301512 | tf_op jit(solution)/shard_map/ppermute | solution.py:73
  631.8 30.8 %collective-permute-start.6 = (bf16[704,2048]{1,0:T(8,128)(2,1)S(1)}, bf16[704,2048]{1,0:T(8,128)(2,1)}, u32[]{:S(2)}, u32[]{:S(2)}) collective-permute-start(bf16[704,2048]{1,0:T(8,128)(2,1)S(1)} %bitcast.471), channel_id=1, source_target_pairs={{0,1},{1,0},{2,3},{3,2},{4,5},{5,4},{6,7},{7,6},{8,9},{9,8},{10,11... | collective-permute-start | bytes 8650760 | tf_op jit(solution)/shard_map/ppermute | solution.py:73
  636.5 19.7 copy-start.48
  636.5 26.1 %copy-start.50 = (bf16[16,1,64,2048]{3,2,1,0:T(8,128)(2,1)}, bf16[16,1,64,2048]{3,2,1,0:T(8,128)(2,1)S(1)}, u32[]{:S(2)}) copy-start(bf16[16,1,64,2048]{3,2,1,0:T(8,128)(2,1)S(1)} %get-tuple-element.91) | copy-start | bytes 12582916
  672.8 21.3 copy-start.54
  672.8 12.8 copy-start.122
  708.9 318.8 %copy-start.31 = (bf16[128,2048]{1,0:T(8,128)(2,1)S(1)}, bf16[128,2048]{1,0:T(8,128)(2,1)}, u32[]{:S(2)}) copy-start(bf16[128,2048]{1,0:T(8,128)(2,1)} %param.18) | copy-start | bytes 1572868
  952.0 224.3 %all-to-all-start.1 = ((bf16[16,2,64,2048]{3,2,1,0:T(8,128)(2,1)}), bf16[16,2,64,2048]{3,2,1,0:T(8,128)(2,1)}, u32[]{:S(2)}, u32[]{:S(2)}) async-start(bf16[16,2,64,2048]{3,2,1,0:T(8,128)(2,1)} %pad_maximum_fusion.8), calls=%async_computation.1 | async-start | bytes 16777216 | tf_op jit(solution)/shard_map/all_to_all | solution.py:310
  1027.6 216.1 %collective-permute-start.7 = (bf16[16,192,2816]{2,1,0:T(8,128)(2,1)}, bf16[16,192,2816]{2,1,0:T(8,128)(2,1)}, u32[]{:S(2)}, u32[]{:S(2)}) collective-permute-start(bf16[16,192,2816]{2,1,0:T(8,128)(2,1)} %all-to-all-done.2), channel_id=1, source_target_pairs={{0,1},{1,0},{2,3},{3,2},{4,5},{5,4},{6,7},{7,6},{8,9},{9,8},{10,11... | collective-permute-start | bytes 51904520 | tf_op jit(solution)/shard_map/ppermute | solution.py:73
  1236.1 89.0 %copy-start.96 = (bf16[128,16]{0,1:T(8,128)(2,1)}, bf16[128,16]{0,1:T(8,128)(2,1)S(1)}, u32[]{:S(2)}) copy-start(bf16[128,16]{0,1:T(8,128)(2,1)S(1)} %fusion.98) | copy-start | bytes 12292
  1316.7 10.5 copy-start.120
  1350.0 6.3 collective-permute-start.8
  1388.3 10.4 copy-start.58
  1396.6 11.4 copy-start.57
  1396.6 67.3 %collective-permute-start.9 = (bf16[16,64,3072]{2,1,0:T(8,128)(2,1)}, bf16[16,64,3072]{2,1,0:T(8,128)(2,1)}, u32[]{:S(2)}, u32[]{:S(2)}) collective-permute-start(bf16[16,64,3072]{2,1,0:T(8,128)(2,1)} %fusion.7), channel_id=1, source_target_pairs={{0,1},{1,0},{2,3},{3,2},{4,5},{5,4},{6,7},{7,6},{8,9},{9,8},{10,11... | collective-permute-start | bytes 18874376 | tf_op jit(solution)/shard_map/ppermute | solution.py:73
  1463.9 82.3 %collective-permute-start.13 = (bf16[16,128,2816]{2,1,0:T(8,128)(2,1)}, bf16[16,128,2816]{2,1,0:T(8,128)(2,1)}, u32[]{:S(2)}, u32[]{:S(2)}) collective-permute-start(bf16[16,128,2816]{2,1,0:T(8,128)(2,1)} %fusion.2), channel_id=1, source_target_pairs={{0,1},{1,0},{2,3},{3,2},{4,5},{5,4},{6,7},{7,6},{8,9},{9,8},{10,11... | collective-permute-start | bytes 34603016 | tf_op jit(solution)/shard_map/ppermute | solution.py:73
  1475.3 36.9 %copy-start.53 = (bf16[128,2816]{1,0:T(8,128)(2,1)S(1)}, bf16[128,2816]{1,0:T(8,128)(2,1)}, u32[]{:S(2)}) copy-start(bf16[128,2816]{1,0:T(8,128)(2,1)} %get-tuple-element.98) | copy-start | bytes 2162692
  1475.3 157.0 %all-to-all-start.3 = ((bf16[16,64,3072]{2,1,0:T(8,128)(2,1)}), bf16[16,64,3072]{2,1,0:T(8,128)(2,1)}, u32[]{:S(2)}, u32[]{:S(2)}) async-start(bf16[16,64,3072]{2,1,0:T(8,128)(2,1)} %fusion.1), calls=%async_computation.3 | async-start | bytes 12582912 | tf_op jit(solution)/shard_map/all_to_all | solution.py:110
  1526.6 9.6 collective-permute-start.14
  1546.1 13.0 copy-start.21
  1632.3 753.0 %all-to-all-start.4 = ((bf16[16,192,2816]{2,1,0:T(8,128)(2,1)}), bf16[16,192,2816]{2,1,0:T(8,128)(2,1)}, u32[]{:S(2)}, u32[]{:S(2)}) async-start(bf16[16,192,2816]{2,1,0:T(8,128)(2,1)} %pad_maximum_fusion.1), calls=%async_computation.7 | async-start | bytes 34603008 | tf_op jit(solution)/shard_map/all_to_all | solution.py:110
  1661.8 458.3 %all-reduce.9.cloned.1.call-start = ((), (), s32[]{:S(2)}) async-start(), calls=%async_computation.8 | async-start | bytes 327680 | tf_op jit(solution)/shard_map/psum | solution.py:492
  1664.2 11.7 collective-permute-start.10
  1671.8 19.4 collective-permute-start.11
  1675.9 528.1 %reduce-scatter.4.cloned.1.call-start = ((), (), s32[]{:S(2)}) async-start(), calls=%async_computation.9 | async-start | bytes 1392640 | tf_op jit(solution)/shard_map/reduce_scatter | solution.py:113
  1679.5 604.7 %reduce-scatter.6.cloned.1.call-start = ((), (), s32[]{:S(2)}) async-start(), calls=%async_computation.10 | async-start | bytes 2228224 | tf_op jit(solution)/shard_map/reduce_scatter | solution.py:113
  1690.7 7.7 collective-permute-start.12
  1696.0 682.7 %reduce-scatter.8.cloned.1.call-start = ((), (), s32[]{:S(2)}) async-start(), calls=%async_computation.11 | async-start | bytes 4456448 | tf_op jit(solution)/shard_map/reduce_scatter | solution.py:113
  1708.5 11.0 copy-start.51
  1719.2 13.9 copy-start.63
  1719.2 21.5 collective-permute-start.15
  1727.0 6.1 collective-permute-start.16
  1727.2 13.5 copy-start.49
  1727.2 13.5 copy-start.123
  1727.2 13.5 copy-start.124
  (99 other events, 424.6 us)
Sparse Core Ops, SparseCore 0:
  12.0 60.1 all-gather.15
  75.0 59.1 all-gather.9
  137.0 92.1 all-gather.11
  231.8 74.1 all-gather.13
  1676.0 444.0 all-reduce.8
  2122.3 81.6 reduce-scatter.3
  2206.2 77.9 reduce-scatter.5
  2286.5 92.1 reduce-scatter.7

commit v4 on v3

--- a/solution.py
+++ b/solution.py
@@ -73,30 +73,6 @@
     return lax.ppermute(value, "shard", [(0, 1), (1, 0)])
 
 
-def gather_over_expert(local, by_exchange):
-    if by_exchange:
-        copies = jnp.broadcast_to(local[None], (lax.axis_size("expert"),) + local.shape)
-        return lax.all_to_all(copies, "expert", split_axis=0, concat_axis=0, tiled=True)
-    return lax.all_gather(local, "expert", axis=0, tiled=False)
-
-
-def gather_halves(local, by_exchange=False):
-    side = lax.axis_index("shard")
-    mine = gather_over_expert(local, by_exchange)
-    partner = swap_shard(mine)
-    return jnp.where(side == 0, mine, partner), jnp.where(side == 0, partner, mine)
-
-
-def assemble(halves, first=None, last=None):
-    lower, upper = [half[:, first:last] for half in halves]
-    full = jnp.stack([lower, upper], axis=1)
-    return full.reshape((-1,) + full.shape[3:])
-
-
-def gather_rows(local, by_exchange=False):
-    return assemble(gather_halves(local, by_exchange))
-
-
 def pair_total(blocks):
     side = lax.axis_index("shard")
     mine = lax.dynamic_index_in_dim(blocks, side, axis=1, keepdims=False)
@@ -105,17 +81,14 @@
     return (mine + arrived.astype(jnp.float32)).astype(jnp.bfloat16)
 
 
-def reduce_over_expert(total, by_exchange=False):
-    if by_exchange:
-        got = lax.all_to_all(total, "expert", split_axis=0, concat_axis=0, tiled=True)
-        return jnp.sum(got.astype(jnp.float32), axis=0)
+def reduce_over_expert(total):
     rows = total.reshape((-1,) + total.shape[2:])
     return lax.psum_scatter(rows, "expert", scatter_dimension=0, tiled=True).astype(jnp.float32)
 
 
-def scatter_rows(full, experts, by_exchange=False):
+def scatter_rows(full, experts):
     blocks = full.reshape((experts, 2, -1) + full.shape[1:])
-    return reduce_over_expert(pair_total(blocks), by_exchange)
+    return reduce_over_expert(pair_total(blocks))
 
 
 def gated_pair(gate_part, up_part):
@@ -172,9 +145,11 @@
         [small_local, jnp.zeros((small_rows * width - small_local.shape[0],), jnp.bfloat16)]
     ).reshape(small_rows, width)
     down_rows = latent_down.shape[0]
-    down_halves = gather_halves(jnp.concatenate([latent_down, small_local], axis=0))
-    down_full = assemble(down_halves, 0, down_rows)
-    small_all = assemble(down_halves, down_rows).reshape(devices, -1)
+    down_all = lax.all_gather(
+        jnp.concatenate([latent_down, small_local], axis=0), ALL, axis=0, tiled=False
+    )
+    down_full = down_all[:, :down_rows].reshape(-1, width)
+    small_all = down_all[:, down_rows:].reshape(devices, -1)
     cuts = [0]
     for size in small_sizes:
         cuts.append(cuts[-1] + size)
@@ -183,21 +158,29 @@
     gain_two_float = small_all[:, cuts[2] : cuts[3]].reshape(-1).astype(jnp.float32)
     router_full = small_all[:, cuts[3] : cuts[4]].reshape(-1, router_weight.shape[1])
 
-    query_full = gather_rows(query_weight)
-    up_full = gather_rows(latent_up)
-    output_t_full = gather_rows(output_weight.T)
+    query_width = query_weight.shape[1]
+    query_output_full = lax.all_gather(
+        jnp.concatenate([query_weight, output_weight.T], axis=1), ALL, axis=0, tiled=True
+    )
+    query_full = query_output_full[:, :query_width]
+    output_t_full = query_output_full[:, query_width:]
+    up_full = lax.all_gather(latent_up, ALL, axis=0, tiled=True)
     inner_rows = shared_inner.shape[0] * shared_inner.shape[1]
-    ffn_halves = gather_halves(
+    ffn_all = lax.all_gather(
         jnp.concatenate(
             [shared_inner.reshape(inner_rows, shared_inner.shape[-1]), shared_outer.T], axis=0
         ),
-        by_exchange=True,
+        ALL,
+        axis=0,
+        tiled=False,
     )
     shared_in_full = [
-        assemble(ffn_halves, g * shared_inner.shape[1], (g + 1) * shared_inner.shape[1])
+        ffn_all[:, g * shared_inner.shape[1] : (g + 1) * shared_inner.shape[1]].reshape(
+            -1, shared_inner.shape[-1]
+        )
         for g in range(shared_inner.shape[0])
     ]
-    shared_out_t_full = assemble(ffn_halves, inner_rows)
+    shared_out_t_full = ffn_all[:, inner_rows:].reshape(-1, shared_inner.shape[-1])
 
     inner_halves = (expert_inner[0], swap_shard(expert_inner[0]))
     outer_halves = (expert_outer[0], swap_shard(expert_outer[0]))
@@ -383,7 +366,7 @@
     ffn_total = jnp.concatenate(
         [pair_total(inner_grad_blocks), pair_total(outer_grad_blocks)], axis=1
     )
-    ffn_local = reduce_over_expert(ffn_total, by_exchange=True)
+    ffn_local = reduce_over_expert(ffn_total)
     delta_shared_inner_local = ffn_local[:inner_rows].reshape(shared_inner.shape)
     delta_shared_outer_local = ffn_local[inner_rows:].T
 
@@ -471,8 +454,7 @@
     delta_query_weight = jnp.einsum(
         "td,tc->dc", normed_one, delta_query_raw, preferred_element_type=jnp.float32
     )
-    delta_latent_down_local = scatter_rows(delta_latent_down, experts_all)
-    delta_query_local = scatter_rows(delta_query_weight, experts_all, by_exchange=True)
+    delta_query_local = scatter_rows(delta_query_weight, experts_all)
     delta_normed_one = jnp.einsum(
         "tc,dc->td", delta_query_raw, query_full, preferred_element_type=jnp.float32
     ) + jnp.einsum("tc,dc->td", delta_down_out, down_full, preferred_element_type=jnp.float32)
@@ -488,9 +470,23 @@
         jnp.broadcast_to(square_sums[None], (devices, 3)),
     ]
     small_packed = jnp.concatenate(small_parts, axis=1)
-    small_sum = lax.dynamic_index_in_dim(
-        lax.psum(small_packed, ALL), lax.axis_index(ALL), axis=0, keepdims=False
-    )
+    grad_rows = down_rows + -(-small_packed.shape[1] // width)
+    grad_rows = grad_rows + (-grad_rows) % 8
+    small_packed = jnp.concatenate(
+        [
+            small_packed,
+            jnp.zeros(
+                (devices, (grad_rows - down_rows) * width - small_packed.shape[1]), jnp.float32
+            ),
+        ],
+        axis=1,
+    ).reshape(devices, grad_rows - down_rows, width)
+    down_blocks = jnp.concatenate(
+        [delta_latent_down.reshape(devices, down_rows, width), small_packed], axis=1
+    ).reshape(experts_all, shard_count, grad_rows, width)
+    down_local = reduce_over_expert(pair_total(down_blocks))
+    delta_latent_down_local = down_local[:down_rows]
+    small_sum = down_local[down_rows:].reshape(-1)
     small_cuts = [0]
     for part in small_parts:
         small_cuts.append(small_cuts[-1] + part.shape[1])

time: 2410 us -> 1810 us (0.75)
  waiting for transfers between devices: 1510 us -> 1130 us
  starting transfers between devices: 196 us -> 68.4 us
  other arithmetic: 239 us -> 174 us
  local copies, waits for them, and re-layouts: 223 us -> 189 us
    psum x1 -> x0, waiting for transfers between devices: 369 us -> none  [shards(): lax.psum(small_packed, ALL)]
    all_to_all x3 -> x0, waiting for transfers between devices: 310 us -> none  [the longest x1 243 us: gather_over_expert(): lax.all_to_all(copies, 'expert', split_axis=0, concat_axis=0, tiled=True)]
    reduce_scatter x3 -> x4, waiting for transfers between devices: 250 us -> 521 us  [reduce_over_expert(): lax.psum_scatter(rows, 'expert', scatter_dimension=0, tiled=True)]
    all_to_all x3 -> x0, starting transfers between devices: 106 us -> none  [the longest x2 66.3 us: reduce_over_expert(): lax.all_to_all(total, 'expert', split_axis=0, concat_axis=0, tiled=True)]
    all_to_all x1, waiting for transfers between devices: 154 us -> 258 us  [shards(): lax.all_to_all(outgoing, 'expert', split_axis=0, concat_axis=0, tiled=True)]
    all_gather x4, waiting for transfers between devices: 272 us -> 220 us  [the longest x1 108 us: shards(): lax.all_gather(jnp.concatenate([query_weight, output_weight.T], axis=1),...]
    another operation x18 -> x6, other arithmetic: 45.1 us -> 2.25 us  [the longest x11 42.8 us: assemble(): full = jnp.stack([lower, upper], axis=1)]
    all_to_all x1, waiting for transfers between devices: 136 us -> 111 us  [shards(): lax.all_to_all(going_back, 'expert', split_axis=0, concat_axis=0, tiled=T...]
  transfers between devices with their start and end apart: 30 -> 23, of which waited for: 16 -> 11; matrix products, arithmetic and copies ran while one was open for 17% -> 24% of each run, Pallas kernels for 0% -> 0%
where the time goes in v4:
time: 1810 us; the launch traced here: 1800 us
  waiting for transfers between devices  1130 us (62%)
  matrix products  227 us (13%)
  local copies, waits for them, and re-layouts  189 us (10%)
  other arithmetic  174 us (10%)
  starting transfers between devices  68.4 us (4%)
    reduce_scatter x4, waiting for transfers between devices, reduce_over_expert(): lax.psum_scatter(rows, 'expert', scatter_dimension=0, tiled=True)  521 us
    all_to_all x1, waiting for transfers between devices, shards(): lax.all_to_all(outgoing, 'expert', split_axis=0, concat_axis=0, tiled=True)  258 us
    all_to_all x1, waiting for transfers between devices, shards(): lax.all_to_all(going_back, 'expert', split_axis=0, concat_axis=0, tiled=T...  111 us
    all_gather x1, waiting for transfers between devices, shards(): lax.all_gather(jnp.concatenate([query_weight, output_weight.T], axis=1),...  108 us
    all_gather x1, waiting for transfers between devices, shards(): up_full = lax.all_gather(latent_up, ALL, axis=0, tiled=True)  56.3 us
    all_gather x1, waiting for transfers between devices, shards(): lax.all_gather(jnp.concatenate([latent_down, small_local], axis=0), ALL,...  55.6 us
    dot_general x10, matrix products, matmul(): return jnp.dot(left_side, right_side, preferred_element_type=jnp.float32)  54.3 us
    all_to_all x1, starting transfers between devices, shards(): lax.all_to_all(going_back, 'expert', split_axis=0, concat_axis=0, tiled=T...  53 us
  transfers between devices with their start and end apart: 23, of which 11 were waited for; matrix products, arithmetic and copies ran while one was open for 24% of the time, Pallas kernels for 0%

profile of v4, /device:TPU:0, one launch (start us, length us, event | category | flops | bytes accessed | tf_op | source)
XLA Modules:
  0.0 1801.5 jit_solution(5735773226363989052)
XLA Ops:
  17.7 55.6 %all-gather.14.cloned.1.call-done = bf16[32,67,576]{2,1,0:T(8,128)(2,1)} async-done(((bf16[1,67,576]{2,1,0:T(8,128)(2,1)}), bf16[32,67,576]{2,1,0:T(8,128)(2,1)}) %all-gather.14.cloned.1.call-update) | async-done | bytes 2469904 | tf_op jit(solution)/shard_map/all_gather | solution.py:148
  80.5 56.3 %all-gather.8.cloned.1.call-done = bf16[512,4096]{1,0:T(8,128)(2,1)} async-done(((bf16[16,4096]{1,0:T(8,128)(2,1)}), bf16[512,4096]{1,0:T(8,128)(2,1)}) %all-gather.8.cloned.1.call-update) | async-done | bytes 4194320 | tf_op jit(solution)/shard_map/all_gather | solution.py:167
  151.9 6.7 gather_fusion.1
  164.6 108.2 %all-gather.10.cloned.1.call-done = bf16[2048,5120]{1,0:T(8,128)(2,1)} async-done(((bf16[64,5120]{1,0:T(8,128)(2,1)}), bf16[2048,5120]{1,0:T(8,128)(2,1)}) %all-gather.10.cloned.1.call-update) | async-done | bytes 20971536 | tf_op jit(solution)/shard_map/all_gather | solution.py:162
  272.8 8.1 fusion.7
  284.2 7.2 multiply_reduce_fusion.8
  292.9 5.1 gather_fusion.3
  303.8 6.0 gather_fusion
  314.4 5.0 multiply_convert_fusion
  319.4 6.4 pad_maximum_fusion.2
  325.7 5.0 all-to-all-start
  331.3 258.3 %all-to-all-done = bf16[16,2,64,2048]{3,2,1,0:T(8,128)(2,1)} async-done(((bf16[16,2,64,2048]{3,2,1,0:T(8,128)(2,1)}), bf16[16,2,64,2048]{3,2,1,0:T(8,128)(2,1)}, u32[]{:S(2)}, u32[]{:S(2)}) %all-to-all-start) | async-done | bytes 8388640 | tf_op jit(solution)/shard_map/all_to_all | solution.py:255
  593.7 10.6 fusion.135
  605.3 5.7 fusion.60
  611.0 6.1 fusion.35
  617.1 9.3 fusion.160
  629.0 6.2 multiply_bitcast_fusion
  635.2 13.5 add_convert_fusion
  648.7 7.0 fusion.81
  655.7 8.8 fusion.10
  664.6 6.3 pad_maximum_fusion.3
  670.9 53.0 %all-to-all-start.1 = ((bf16[16,2,64,2048]{3,2,1,0:T(8,128)(2,1)}), bf16[16,2,64,2048]{3,2,1,0:T(8,128)(2,1)}, u32[]{:S(2)}, u32[]{:S(2)}) async-start(bf16[16,2,64,2048]{3,2,1,0:T(8,128)(2,1)} %pad_maximum_fusion.3), calls=%async_computation.1 | async-start | bytes 16777216 | tf_op jit(solution)/shard_map/all_to_all | solution.py:293
  728.4 8.3 mul.559
  736.7 18.9 %fusion.152 = (bf16[32,64,2816]{2,1,0:T(8,128)(2,1)}, bf16[32,64,2816]{2,1,0:T(8,128)(2,1)}, bf16[32,64,2816]{2,1,0:T(8,128)(2,1)S(1)}) fusion(bf16[32,192,2816]{2,1,0:T(8,128)(2,1)} %bitcast.359), kind=kLoop, calls=%fused_computation.307 | loop fusion | bytes 69206016 | tf_op jit(solution)/shard_map/slice | solution.py:183
  755.7 6.1 fusion.162
  768.1 4.8 fusion.163
  772.9 111.3 %all-to-all-done.1 = bf16[16,2,64,2048]{3,2,1,0:T(8,128)(2,1)} async-done(((bf16[16,2,64,2048]{3,2,1,0:T(8,128)(2,1)}), bf16[16,2,64,2048]{3,2,1,0:T(8,128)(2,1)}, u32[]{:S(2)}, u32[]{:S(2)}) %all-to-all-start.1) | async-done | bytes 8388640 | tf_op jit(solution)/shard_map/all_to_all | solution.py:293
  884.2 6.3 fusion.153
  890.4 9.9 gather_fusion.5
  900.3 10.3 gather_fusion.4
  915.9 8.2 select_convert_fusion
  924.2 7.8 reshape.604
  932.0 7.0 reduce_sum.196
  939.0 8.9 fusion.40
  950.1 8.0 reshape.603
  958.2 6.7 multiply_reduce_fusion
  964.9 9.7 multiply_reduce_fusion.3
  975.5 5.6 fusion.41
  1014.8 7.4 fusion.5
  1044.4 5.8 copy-done
  1053.4 4.8 fusion.18
  1061.4 8.4 fusion.9
  1070.9 10.2 fusion.165
  1081.1 8.3 fusion.15
  1089.5 9.4 fusion.169
  1099.0 9.4 fusion.168
  1108.4 34.1 %pad_maximum_fusion = f32[2,16,2,64,2816]{4,3,0,2,1:T(8,128)} fusion(f32[1,16,2,64,2816]{4,3,0,2,1:T(8,128)} %bitcast.350, f32[1,16,2,64,2816]{4,3,0,2,1:T(8,128)} %bitcast.351), kind=kLoop, calls=%fused_computation.7 | loop fusion | flops 11534336 | bytes 92274688 | tf_op jit(solution)/shard_map/stack | solution.py:329
  1142.4 12.5 fusion.2
  1155.4 11.6 fusion.1
  1168.1 9.4 fusion.170
  1177.5 5.0 fusion.16
  1182.6 9.5 collective-permute-done.9
  1192.1 10.0 fusion.4
  1202.2 13.0 fusion
  1215.2 6.8 pad_maximum_fusion.1
  1223.8 9.1 convert_bitcast_fusion
  1233.2 6.3 convolution_convert_fusion.1
  1239.8 6.8 collective-permute-done.11
  1246.6 5.0 add_bitcast_fusion
  1251.6 8.9 fusion.3
  1265.3 7.7 reduce-scatter.10.cloned.1.call-done
  1274.7 92.6 %reduce-scatter.12.cloned.1.call-done = bf16[64,2048]{1,0:T(8,128)(2,1)} async-done(((bf16[1024,2048]{1,0:T(8,128)(2,1)}), bf16[64,2048]{1,0:T(8,128)(2,1)}) %reduce-scatter.12.cloned.1.call-update) | async-done | bytes 262160 | tf_op jit(solution)/shard_map/reduce_scatter | solution.py:86
  1369.0 150.7 %reduce-scatter.8.cloned.1.call-done = bf16[64,3072]{1,0:T(8,128)(2,1)} async-done(((bf16[1024,3072]{1,0:T(8,128)(2,1)}), bf16[64,3072]{1,0:T(8,128)(2,1)}) %reduce-scatter.8.cloned.1.call-update) | async-done | bytes 393232 | tf_op jit(solution)/shard_map/reduce_scatter | solution.py:86
  1521.6 269.5 %reduce-scatter.14.cloned.1.call-done = bf16[192,2816]{1,0:T(8,128)(2,1)} async-done(((bf16[3072,2816]{1,0:T(8,128)(2,1)}), bf16[192,2816]{1,0:T(8,128)(2,1)}) %reduce-scatter.14.cloned.1.call-update) | async-done | bytes 1081360 | tf_op jit(solution)/shard_map/reduce_scatter | solution.py:86
  (446 shorter events, 161.4 us)
Async XLA Ops:
  7.2 10.0 copy-start.88
  7.2 10.3 copy-start.21
  7.2 66.2 %all-gather.14.cloned.1.call-start = ((), (), s32[]{:S(2)}) async-start(), calls=%async_computation.14 | async-start | bytes 3041280 | tf_op jit(solution)/shard_map/all_gather | solution.py:148
  11.9 124.9 %all-gather.8.cloned.1.call-start = ((), (), s32[]{:S(2)}) async-start(), calls=%async_computation.7 | async-start | bytes 4325376 | tf_op jit(solution)/shard_map/all_gather | solution.py:167
  12.7 260.1 %all-gather.10.cloned.1.call-start = ((), (), s32[]{:S(2)}) async-start(), calls=%async_computation.8 | async-start | bytes 21626880 | tf_op jit(solution)/shard_map/all_gather | solution.py:162
  14.7 722.0 %all-gather.12.cloned.1.call-start = ((), (), s32[]{:S(2)}) async-start(), calls=%async_computation.13 | async-start | bytes 35684352 | tf_op jit(solution)/shard_map/all_gather | solution.py:169
  17.3 127.6 %copy-start.67 = (s32[128,6]{1,0:T(8,128)}, s32[128,6]{1,0:T(8,128)S(1)}, u32[]{:S(2)}) copy-start(s32[128,6]{1,0:T(8,128)S(1)} %copy.140) | copy-start | bytes 9220
  17.4 62.3 %copy-start.105 = (f32[32]{0:T(128)}, f32[32]{0:T(128)S(1)}, u32[]{:S(2)}) copy-start(f32[32]{0:T(128)S(1)} %multiply_power_fusion) | copy-start | bytes 388
  17.5 62.3 %copy-start.107 = (f32[128]{0:T(128)}, f32[128]{0:T(128)S(1)}, u32[]{:S(2)}) copy-start(f32[128]{0:T(128)S(1)} %get-tuple-element.126) | copy-start | bytes 1540
  17.7 56.9 %copy-start.109 = (f32[128]{0:T(128)}, f32[128]{0:T(128)S(1)}, u32[]{:S(2)}) copy-start(f32[128]{0:T(128)S(1)} %fusion.75) | copy-start | bytes 1540
  17.7 255.1 %copy-start.95 = (f32[128]{0:T(128)}, f32[128]{0:T(128)S(1)}, u32[]{:S(2)}) copy-start(f32[128]{0:T(128)S(1)} %fusion.121) | copy-start | bytes 1540
  74.8 198.0 %copy-start.69 = (f32[2048]{0:T(1024)}, f32[2048]{0:T(1024)S(1)}, u32[]{:S(2)}) copy-start(f32[2048]{0:T(1024)S(1)} %reshape.600) | copy-start | bytes 24580
  79.7 62.1 %copy-start.111 = (f32[128]{0:T(128)}, f32[128]{0:T(128)S(1)}, u32[]{:S(2)}) copy-start(f32[128]{0:T(128)S(1)} %multiply_reduce_fusion.11) | copy-start | bytes 1540
  79.7 62.1 %copy-start.103 = (f32[128]{0:T(128)}, f32[128]{0:T(128)S(1)}, u32[]{:S(2)}) copy-start(f32[128]{0:T(128)S(1)} %fusion.122) | copy-start | bytes 1540
  80.3 200.6 %copy-start.79 = (f32[128,32]{0,1:T(8,128)}, f32[128,32]{0,1:T(8,128)S(1)}, u32[]{:S(2)}) copy-start(f32[128,32]{0,1:T(8,128)S(1)} %get-tuple-element.112) | copy-start | bytes 49156
  80.3 201.7 %copy-start.83 = (bf16[128,32]{0,1:T(8,128)(2,1)}, bf16[128,32]{0,1:T(8,128)(2,1)S(1)}, u32[]{:S(2)}) copy-start(bf16[128,32]{0,1:T(8,128)(2,1)S(1)} %get-tuple-element.114) | copy-start | bytes 24580
  80.3 201.7 %copy-start.85 = (bf16[128,32]{0,1:T(8,128)(2,1)}, bf16[128,32]{0,1:T(8,128)(2,1)S(1)}, u32[]{:S(2)}) copy-start(bf16[128,32]{0,1:T(8,128)(2,1)S(1)} %get-tuple-element.115) | copy-start | bytes 24580
  80.5 61.3 %copy-start.57 = (bf16[128,512]{0,1:T(8,128)(2,1)}, bf16[128,512]{0,1:T(8,128)(2,1)S(1)}, u32[]{:S(2)}) copy-start(bf16[128,512]{0,1:T(8,128)(2,1)S(1)} %multiply_convert_fusion.8) | copy-start | bytes 393220
  80.5 71.3 %copy-start.25 = (bf16[128,2048]{1,0:T(8,128)(2,1)S(1)}, bf16[128,2048]{1,0:T(8,128)(2,1)}, u32[]{:S(2)}) copy-start(bf16[128,2048]{1,0:T(8,128)(2,1)} %param.18) | copy-start | bytes 1572868
  141.8 18.0 collective-permute-start
  158.8 132.7 %copy-start.81 = (f32[2048]{0:T(1024)}, f32[2048]{0:T(1024)S(1)}, u32[]{:S(2)}) copy-start(f32[2048]{0:T(1024)S(1)} %reshape.602) | copy-start | bytes 24580
  159.2 132.9 %copy-start.29 = (bf16[2048,16]{1,0:T(8,128)(2,1)}, bf16[2048,16]{1,0:T(8,128)(2,1)S(1)}, u32[]{:S(2)}) copy-start(bf16[2048,16]{1,0:T(8,128)(2,1)S(1)} %reshape.576) | copy-start | bytes 196612
  159.7 123.7 %copy-start.6 = (bf16[128,16,256]{2,0,1:T(8,128)(2,1)}, bf16[128,16,256]{2,0,1:T(8,128)(2,1)S(1)}, u32[]{:S(2)}) copy-start(bf16[128,16,256]{2,0,1:T(8,128)(2,1)S(1)} %copy.132) | copy-start | bytes 3145732
  163.9 119.5 %copy-start.9 = (bf16[128,16,256]{2,0,1:T(8,128)(2,1)}, bf16[128,16,256]{2,0,1:T(8,128)(2,1)S(1)}, u32[]{:S(2)}) copy-start(bf16[128,16,256]{2,0,1:T(8,128)(2,1)S(1)} %copy.131) | copy-start | bytes 3145732
  164.6 117.4 %copy-start.77 = (bf16[128,64]{0,1:T(8,128)(2,1)}, bf16[128,64]{0,1:T(8,128)(2,1)S(1)}, u32[]{:S(2)}) copy-start(bf16[128,64]{0,1:T(8,128)(2,1)S(1)} %slice.248) | copy-start | bytes 49156
  325.7 263.9 %all-to-all-start = ((bf16[16,2,64,2048]{3,2,1,0:T(8,128)(2,1)}), bf16[16,2,64,2048]{3,2,1,0:T(8,128)(2,1)}, u32[]{:S(2)}, u32[]{:S(2)}) async-start(bf16[16,2,64,2048]{3,2,1,0:T(8,128)(2,1)} %pad_maximum_fusion.2), calls=%async_computation | async-start | bytes 16777216 | tf_op jit(solution)/shard_map/all_to_all | solution.py:255
  330.7 286.4 %collective-permute-start.1 = (bf16[2,2048,704]{1,2,0:T(8,128)(2,1)}, bf16[2,2048,704]{1,2,0:T(8,128)(2,1)}, u32[]{:S(2)}, u32[]{:S(2)}) collective-permute-start(bf16[2,2048,704]{1,2,0:T(8,128)(2,1)} %bitcast.402), channel_id=1, source_target_pairs={{0,1},{1,0},{2,3},{3,2},{4,5},{5,4},{6,7},{7,6},{8,9},{9,8},{10,11... | collective-permute-start | bytes 17301512 | tf_op jit(solution)/shard_map/ppermute | solution.py:73
  331.1 295.3 %collective-permute-start.2 = (bf16[704,2048]{1,0:T(8,128)(2,1)S(1)}, bf16[704,2048]{1,0:T(8,128)(2,1)}, u32[]{:S(2)}, u32[]{:S(2)}) collective-permute-start(bf16[704,2048]{1,0:T(8,128)(2,1)S(1)} %bitcast.405), channel_id=1, source_target_pairs={{0,1},{1,0},{2,3},{3,2},{4,5},{5,4},{6,7},{7,6},{8,9},{9,8},{10,11... | collective-permute-start | bytes 8650760 | tf_op jit(solution)/shard_map/ppermute | solution.py:73
  593.7 23.4 %copy-start.41 = (bf16[16,1,64,2048]{3,2,1,0:T(8,128)(2,1)}, bf16[16,1,64,2048]{3,2,1,0:T(8,128)(2,1)S(1)}, u32[]{:S(2)}) copy-start(bf16[16,1,64,2048]{3,2,1,0:T(8,128)(2,1)S(1)} %get-tuple-element.83) | copy-start | bytes 12582916
  593.7 32.8 %copy-start.43 = (bf16[16,1,64,2048]{3,2,1,0:T(8,128)(2,1)}, bf16[16,1,64,2048]{3,2,1,0:T(8,128)(2,1)S(1)}, u32[]{:S(2)}) copy-start(bf16[16,1,64,2048]{3,2,1,0:T(8,128)(2,1)S(1)} %get-tuple-element.84) | copy-start | bytes 12582916
  629.0 19.7 %slice-start.3 = ((s8[5767168]{0:T(1024)(128)(4,1)}), s8[4194304]{0:T(1024)(128)(4,1)S(1)}, s32[]{:S(2)}) async-start(s8[5767168]{0:T(1024)(128)(4,1)} %bitcast.403), calls=%async_computation.19 | async-start | bytes 8388608
  635.1 20.6 %copy-start.49 = (f32[1024,1,704]{0,2,1:T(8,128)}, f32[1024,1,704]{0,2,1:T(8,128)S(1)}, u32[]{:S(2)}) copy-start(f32[1024,1,704]{0,2,1:T(8,128)S(1)} %get-tuple-element.77) | copy-start | bytes 8650756
  635.1 20.6 %copy-start.51 = (f32[1024,1,704]{0,2,1:T(8,128)}, f32[1024,1,704]{0,2,1:T(8,128)S(1)}, u32[]{:S(2)}) copy-start(f32[1024,1,704]{0,2,1:T(8,128)S(1)} %get-tuple-element.78) | copy-start | bytes 8650756
  635.1 13.5 slice-start.4
  635.2 13.5 copy-start.116
  635.2 13.5 copy-start.118
  670.9 53.0 %copy-start.26 = (bf16[128,2048]{1,0:T(8,128)(2,1)S(1)}, bf16[128,2048]{1,0:T(8,128)(2,1)}, u32[]{:S(2)}) copy-start(bf16[128,2048]{1,0:T(8,128)(2,1)} %param.18) | copy-start | bytes 1572868
  670.9 213.3 %all-to-all-start.1 = ((bf16[16,2,64,2048]{3,2,1,0:T(8,128)(2,1)}), bf16[16,2,64,2048]{3,2,1,0:T(8,128)(2,1)}, u32[]{:S(2)}, u32[]{:S(2)}) async-start(bf16[16,2,64,2048]{3,2,1,0:T(8,128)(2,1)} %pad_maximum_fusion.3), calls=%async_computation.1 | async-start | bytes 16777216 | tf_op jit(solution)/shard_map/all_to_all | solution.py:293
  723.8 536.6 %reduce-scatter.16.cloned.1.call-start = ((), (), s32[]{:S(2)}) async-start(), calls=%async_computation.15 | async-start | bytes 1566720
  736.7 19.0 %copy-start.5 = (bf16[128,2048]{1,0:T(8,128)(2,1)S(1)}, bf16[128,2048]{1,0:T(8,128)(2,1)}, u32[]{:S(2)}) copy-start(bf16[128,2048]{1,0:T(8,128)(2,1)} %copy-done.4) | copy-start | bytes 1572868
  939.0 8.9 copy-start.82
  939.0 8.9 copy-start.102
  988.8 9.1 copy-start.8
  988.8 9.1 copy-start.11
  990.3 11.4 collective-permute-start.3
  1028.2 8.5 collective-permute-start.4
  1036.7 16.7 collective-permute-start.6
  1040.4 232.6 %reduce-scatter.10.cloned.1.call-start = ((), (), s32[]{:S(2)}) async-start(), calls=%async_computation.10 | async-start | bytes 2228224 | tf_op jit(solution)/shard_map/reduce_scatter | solution.py:86
  1052.9 8.5 collective-permute-start.7
  1058.2 309.0 %reduce-scatter.12.cloned.1.call-start = ((), (), s32[]{:S(2)}) async-start(), calls=%async_computation.11 | async-start | bytes 4456448 | tf_op jit(solution)/shard_map/reduce_scatter | solution.py:86
  1069.8 449.9 %reduce-scatter.8.cloned.1.call-start = ((), (), s32[]{:S(2)}) async-start(), calls=%async_computation.9 | async-start | bytes 6684672 | tf_op jit(solution)/shard_map/reduce_scatter | solution.py:86
  1089.4 9.5 copy-start.53
  1089.4 66.0 %collective-permute-start.5 = (bf16[16,64,3072]{2,1,0:T(8,128)(2,1)}, bf16[16,64,3072]{2,1,0:T(8,128)(2,1)}, u32[]{:S(2)}, u32[]{:S(2)}) collective-permute-start(bf16[16,64,3072]{2,1,0:T(8,128)(2,1)} %fusion.15), channel_id=1, source_target_pairs={{0,1},{1,0},{2,3},{3,2},{4,5},{5,4},{6,7},{7,6},{8,9},{9,8},{10,11... | collective-permute-start | bytes 18874376 | tf_op jit(solution)/shard_map/ppermute | solution.py:73
  1154.9 47.2 %collective-permute-start.8 = (bf16[16,128,2816]{2,1,0:T(8,128)(2,1)}, bf16[16,128,2816]{2,1,0:T(8,128)(2,1)}, u32[]{:S(2)}, u32[]{:S(2)}) collective-permute-start(bf16[16,128,2816]{2,1,0:T(8,128)(2,1)} %fusion.2), channel_id=1, source_target_pairs={{0,1},{1,0},{2,3},{3,2},{4,5},{5,4},{6,7},{7,6},{8,9},{9,8},{10,11... | collective-permute-start | bytes 34603016 | tf_op jit(solution)/shard_map/ppermute | solution.py:73
  1167.1 624.1 %reduce-scatter.14.cloned.1.call-start = ((), (), s32[]{:S(2)}) async-start(), calls=%async_computation.12 | async-start | bytes 18382848 | tf_op jit(solution)/shard_map/reduce_scatter | solution.py:86
  1182.5 9.6 collective-permute-start.9
  1202.1 13.1 copy-start.16
  1223.8 9.4 copy-start.44
  1233.0 13.6 copy-start.60
  1233.0 18.6 %collective-permute-start.10 = (bf16[2,2048,704]{1,2,0:T(8,128)(2,1)S(1)}, bf16[2,2048,704]{1,2,0:T(8,128)(2,1)S(1)}, u32[]{:S(2)}, u32[]{:S(2)}) collective-permute-start(bf16[2,2048,704]{1,2,0:T(8,128)(2,1)S(1)} %convert_bitcast_fusion), channel_id=1, source_target_pairs={{0,1},{1,0},{2,3},{3,2},{4,5},{5,4},{6,7},{7,6},{8,9},{9,8},{10,11... | collective-permute-start | bytes 17301512 | tf_op jit(solution)/shard_map/ppermute | solution.py:73
  1239.5 12.1 copy-start.42
  1239.5 12.1 copy-start.117
  1239.5 12.1 copy-start.119
  1239.5 7.0 collective-permute-start.11
  (85 other events, 341.3 us)
Sparse Core Ops, SparseCore 0:
  12.0 61.2 all-gather.13
  76.2 60.5 all-gather.7
  140.2 132.5 all-gather.9
  275.6 345.2 all-gather.11
  1040.6 149.7 reduce-scatter.15
  1192.5 80.5 reduce-scatter.9
  1275.3 91.8 reduce-scatter.11
  1372.5 147.1 reduce-scatter.7
  1525.6 265.4 reduce-scatter.13

commit v5 on v4

--- a/solution.py
+++ b/solution.py
@@ -81,14 +81,17 @@
     return (mine + arrived.astype(jnp.float32)).astype(jnp.bfloat16)
 
 
-def reduce_over_expert(total):
+def reduce_over_expert(total, by_exchange=False):
+    if by_exchange:
+        got = lax.all_to_all(total, "expert", split_axis=0, concat_axis=0, tiled=True)
+        return jnp.sum(got.astype(jnp.float32), axis=0)
     rows = total.reshape((-1,) + total.shape[2:])
     return lax.psum_scatter(rows, "expert", scatter_dimension=0, tiled=True).astype(jnp.float32)
 
 
-def scatter_rows(full, experts):
+def scatter_rows(full, experts, by_exchange=False):
     blocks = full.reshape((experts, 2, -1) + full.shape[1:])
-    return reduce_over_expert(pair_total(blocks))
+    return reduce_over_expert(pair_total(blocks), by_exchange)
 
 
 def gated_pair(gate_part, up_part):
@@ -366,7 +369,7 @@
     ffn_total = jnp.concatenate(
         [pair_total(inner_grad_blocks), pair_total(outer_grad_blocks)], axis=1
     )
-    ffn_local = reduce_over_expert(ffn_total)
+    ffn_local = reduce_over_expert(ffn_total, by_exchange=True)
     delta_shared_inner_local = ffn_local[:inner_rows].reshape(shared_inner.shape)
     delta_shared_outer_local = ffn_local[inner_rows:].T
 
@@ -454,7 +457,7 @@
     delta_query_weight = jnp.einsum(
         "td,tc->dc", normed_one, delta_query_raw, preferred_element_type=jnp.float32
     )
-    delta_query_local = scatter_rows(delta_query_weight, experts_all)
+    delta_query_local = scatter_rows(delta_query_weight, experts_all, by_exchange=True)
     delta_normed_one = jnp.einsum(
         "tc,dc->td", delta_query_raw, query_full, preferred_element_type=jnp.float32
     ) + jnp.einsum("tc,dc->td", delta_down_out, down_full, preferred_element_type=jnp.float32)

time: 1810 us -> 1950 us (1.077)
  waiting for transfers between devices: 1130 us -> 1210 us
  starting transfers between devices: 68.4 us -> 133 us
    unnamed x10 -> x8, waiting for transfers between devices: 0.83 us -> 367 us
    reduce_scatter x4 -> x2, waiting for transfers between devices: 521 us -> 170 us  [reduce_over_expert(): lax.psum_scatter(rows, 'expert', scatter_dimension=0, tiled=True)]
    all_to_all x0 -> x2, waiting for transfers between devices: none -> 66.6 us  [reduce_over_expert(): lax.all_to_all(total, 'expert', split_axis=0, concat_axis=0, tiled=True)]
    all_to_all x0 -> x2, starting transfers between devices: none -> 65.9 us  [reduce_over_expert(): lax.all_to_all(total, 'expert', split_axis=0, concat_axis=0, tiled=True)]
  transfers between devices with their start and end apart: 23 -> 23, of which waited for: 11 -> 13; matrix products, arithmetic and copies ran while one was open for 24% -> 21% of each run, Pallas kernels for 0% -> 0%
where the time goes in v5:
time: 1950 us; the launch traced here: 1940 us
  waiting for transfers between devices  1210 us (62%)
  matrix products  221 us (11%)
  local copies, waits for them, and re-layouts  183 us (9%)
  other arithmetic  174 us (9%)
  starting transfers between devices  133 us (7%)
    unnamed x8, waiting for transfers between devices  367 us
    all_to_all x1, waiting for transfers between devices, shards(): lax.all_to_all(outgoing, 'expert', split_axis=0, concat_axis=0, tiled=True)  258 us
    reduce_scatter x2, waiting for transfers between devices, reduce_over_expert(): lax.psum_scatter(rows, 'expert', scatter_dimension=0, tiled=True)  170 us
    all_to_all x1, waiting for transfers between devices, shards(): lax.all_to_all(going_back, 'expert', split_axis=0, concat_axis=0, tiled=T...  111 us
    all_gather x1, waiting for transfers between devices, shards(): lax.all_gather(jnp.concatenate([query_weight, output_weight.T], axis=1),...  108 us
    all_to_all x2, waiting for transfers between devices, reduce_over_expert(): lax.all_to_all(total, 'expert', split_axis=0, concat_axis=0, tiled=True)  66.6 us
    all_to_all x2, starting transfers between devices, reduce_over_expert(): lax.all_to_all(total, 'expert', split_axis=0, concat_axis=0, tiled=True)  65.9 us
    all_gather x1, waiting for transfers between devices, shards(): up_full = lax.all_gather(latent_up, ALL, axis=0, tiled=True)  56.3 us
  transfers between devices with their start and end apart: 23, of which 13 were waited for; matrix products, arithmetic and copies ran while one was open for 21% of the time, Pallas kernels for 0%

profile of v5, /device:TPU:0, one launch (start us, length us, event | category | flops | bytes accessed | tf_op | source)
XLA Modules:
  0.0 1941.3 jit_solution(6195196832643097780)
XLA Ops:
  17.6 55.7 %all-gather.14.cloned.1.call-done = bf16[32,67,576]{2,1,0:T(8,128)(2,1)} async-done(((bf16[1,67,576]{2,1,0:T(8,128)(2,1)}), bf16[32,67,576]{2,1,0:T(8,128)(2,1)}) %all-gather.14.cloned.1.call-update) | async-done | bytes 2469904 | tf_op jit(solution)/shard_map/all_gather | solution.py:151
  80.5 56.3 %all-gather.8.cloned.1.call-done = bf16[512,4096]{1,0:T(8,128)(2,1)} async-done(((bf16[16,4096]{1,0:T(8,128)(2,1)}), bf16[512,4096]{1,0:T(8,128)(2,1)}) %all-gather.8.cloned.1.call-update) | async-done | bytes 4194320 | tf_op jit(solution)/shard_map/all_gather | solution.py:170
  151.9 6.7 gather_fusion.1
  164.6 108.2 %all-gather.10.cloned.1.call-done = bf16[2048,5120]{1,0:T(8,128)(2,1)} async-done(((bf16[64,5120]{1,0:T(8,128)(2,1)}), bf16[2048,5120]{1,0:T(8,128)(2,1)}) %all-gather.10.cloned.1.call-update) | async-done | bytes 20971536 | tf_op jit(solution)/shard_map/all_gather | solution.py:165
  272.8 8.1 fusion.7
  283.7 7.3 multiply_reduce_fusion.8
  292.5 5.1 gather_fusion.3
  303.4 6.0 gather_fusion
  314.0 5.0 multiply_convert_fusion
  319.0 6.4 pad_maximum_fusion.2
  325.4 5.0 all-to-all-start
  331.0 258.1 %all-to-all-done = bf16[16,2,64,2048]{3,2,1,0:T(8,128)(2,1)} async-done(((bf16[16,2,64,2048]{3,2,1,0:T(8,128)(2,1)}), bf16[16,2,64,2048]{3,2,1,0:T(8,128)(2,1)}, u32[]{:S(2)}, u32[]{:S(2)}) %all-to-all-start) | async-done | bytes 8388640 | tf_op jit(solution)/shard_map/all_to_all | solution.py:258
  593.1 10.6 fusion.135
  604.7 5.7 fusion.60
  610.4 6.1 fusion.35
  616.5 8.8 fusion.160
  627.9 6.2 multiply_bitcast_fusion
  634.1 13.5 add_convert_fusion
  647.6 7.0 fusion.81
  654.6 8.8 fusion.10
  663.5 6.3 pad_maximum_fusion.3
  669.8 54.1 %all-to-all-start.1 = ((bf16[16,2,64,2048]{3,2,1,0:T(8,128)(2,1)}), bf16[16,2,64,2048]{3,2,1,0:T(8,128)(2,1)}, u32[]{:S(2)}, u32[]{:S(2)}) async-start(bf16[16,2,64,2048]{3,2,1,0:T(8,128)(2,1)} %pad_maximum_fusion.3), calls=%async_computation.1 | async-start | bytes 16777216 | tf_op jit(solution)/shard_map/all_to_all | solution.py:296
  728.4 8.2 mul.559
  736.7 18.9 fusion.152
  755.7 6.1 fusion.162
  772.8 111.4 %all-to-all-done.1 = bf16[16,2,64,2048]{3,2,1,0:T(8,128)(2,1)} async-done(((bf16[16,2,64,2048]{3,2,1,0:T(8,128)(2,1)}), bf16[16,2,64,2048]{3,2,1,0:T(8,128)(2,1)}, u32[]{:S(2)}, u32[]{:S(2)}) %all-to-all-start.1) | async-done | bytes 8388640 | tf_op jit(solution)/shard_map/all_to_all | solution.py:296
  884.2 6.3 fusion.153
  890.4 9.8 gather_fusion.5
  900.3 10.3 gather_fusion.4
  915.9 8.2 select_convert_fusion
  924.2 7.8 reshape.596
  932.0 7.0 reduce_sum.212
  939.0 8.9 fusion.40
  950.1 8.0 reshape.595
  958.2 6.7 multiply_reduce_fusion
  964.9 9.7 multiply_reduce_fusion.3
  975.5 5.6 fusion.41
  1003.0 7.6 fusion.5
  1013.8 11.2 fusion.165
  1025.0 8.3 fusion.15
  1034.8 9.3 fusion.169
  1044.1 9.3 fusion.168
  1053.5 34.0 %pad_maximum_fusion = f32[2,16,2,64,2816]{4,3,0,2,1:T(8,128)} fusion(f32[1,16,2,64,2816]{4,3,0,2,1:T(8,128)} %bitcast.348, f32[1,16,2,64,2816]{4,3,0,2,1:T(8,128)} %bitcast.349), kind=kLoop, calls=%fused_computation.7 | loop fusion | flops 11534336 | bytes 92274688 | tf_op jit(solution)/shard_map/stack | solution.py:332
  1087.4 12.9 fusion.2
  1100.4 11.4 fusion.1
  1111.8 36.5 %all-to-all-start.2 = ((bf16[16,64,3072]{2,1,0:T(8,128)(2,1)}), bf16[16,64,3072]{2,1,0:T(8,128)(2,1)}, u32[]{:S(2)}, u32[]{:S(2)}) async-start(bf16[16,64,3072]{2,1,0:T(8,128)(2,1)} %fusion.1), calls=%async_computation.2 | async-start | bytes 12582912 | tf_op jit(solution)/shard_map/all_to_all | solution.py:86
  1148.3 9.4 fusion.170
  1157.7 5.0 fusion.16
  1162.9 9.3 collective-permute-done.9
  1172.3 9.9 fusion.4
  1182.2 12.9 fusion
  1195.2 6.8 pad_maximum_fusion.1
  1201.9 66.6 %all-to-all-done.2 = bf16[16,64,3072]{2,1,0:T(8,128)(2,1)} async-done(((bf16[16,64,3072]{2,1,0:T(8,128)(2,1)}), bf16[16,64,3072]{2,1,0:T(8,128)(2,1)}, u32[]{:S(2)}, u32[]{:S(2)}) %all-to-all-start.2) | async-done | bytes 6291488 | tf_op jit(solution)/shard_map/all_to_all | solution.py:86
  1268.5 29.4 %all-to-all-start.3 = ((bf16[16,192,2816]{2,1,0:T(8,128)(2,1)}), bf16[16,192,2816]{2,1,0:T(8,128)(2,1)}, u32[]{:S(2)}, u32[]{:S(2)}) async-start(bf16[16,192,2816]{2,1,0:T(8,128)(2,1)} %pad_maximum_fusion.1), calls=%async_computation.5 | async-start | bytes 34603008 | tf_op jit(solution)/shard_map/all_to_all | solution.py:86
  1312.7 5.8 copy-done
  1328.6 8.3 fusion.9
  1338.7 9.1 convert_bitcast_fusion
  1348.1 6.3 convolution_convert_fusion.1
  1354.7 6.8 collective-permute-done.11
  1366.5 8.8 fusion.3
  1375.3 366.5 %reduce-scatter.10.cloned.1.call-done = bf16[72,576]{1,0:T(8,128)(2,1)} async-done(((bf16[1152,576]{1,0:T(8,128)(2,1)}), bf16[72,576]{1,0:T(8,128)(2,1)}) %reduce-scatter.10.cloned.1.call-update) | async-done | bytes 82960
  1746.7 77.8 %reduce-scatter.6.cloned.1.call-done = bf16[16,4096]{1,0:T(8,128)(2,1)} async-done(((bf16[256,4096]{1,0:T(8,128)(2,1)}), bf16[16,4096]{1,0:T(8,128)(2,1)}) %reduce-scatter.6.cloned.1.call-update) | async-done | bytes 131088 | tf_op jit(solution)/shard_map/reduce_scatter | solution.py:89
  1826.1 92.4 %reduce-scatter.8.cloned.1.call-done = bf16[64,2048]{1,0:T(8,128)(2,1)} async-done(((bf16[1024,2048]{1,0:T(8,128)(2,1)}), bf16[64,2048]{1,0:T(8,128)(2,1)}) %reduce-scatter.8.cloned.1.call-update) | async-done | bytes 262160 | tf_op jit(solution)/shard_map/reduce_scatter | solution.py:89
  1925.2 7.0 convert_reduce_fusion
  (442 shorter events, 158.4 us)
Async XLA Ops:
  7.2 9.9 copy-start.84
  7.2 10.2 copy-start.21
  7.2 66.2 %all-gather.14.cloned.1.call-start = ((), (), s32[]{:S(2)}) async-start(), calls=%async_computation.12 | async-start | bytes 3041280 | tf_op jit(solution)/shard_map/all_gather | solution.py:151
  11.9 124.9 %all-gather.8.cloned.1.call-start = ((), (), s32[]{:S(2)}) async-start(), calls=%async_computation.7 | async-start | bytes 4325376 | tf_op jit(solution)/shard_map/all_gather | solution.py:170
  12.7 260.1 %all-gather.10.cloned.1.call-start = ((), (), s32[]{:S(2)}) async-start(), calls=%async_computation.8 | async-start | bytes 21626880 | tf_op jit(solution)/shard_map/all_gather | solution.py:165
  14.7 722.0 %all-gather.12.cloned.1.call-start = ((), (), s32[]{:S(2)}) async-start(), calls=%async_computation.11 | async-start | bytes 35684352 | tf_op jit(solution)/shard_map/all_gather | solution.py:172
  17.2 127.7 %copy-start.66 = (s32[128,6]{1,0:T(8,128)}, s32[128,6]{1,0:T(8,128)S(1)}, u32[]{:S(2)}) copy-start(s32[128,6]{1,0:T(8,128)S(1)} %copy.140) | copy-start | bytes 9220
  17.4 62.4 %copy-start.104 = (f32[32]{0:T(128)}, f32[32]{0:T(128)S(1)}, u32[]{:S(2)}) copy-start(f32[32]{0:T(128)S(1)} %multiply_power_fusion) | copy-start | bytes 388
  17.4 62.3 %copy-start.106 = (f32[128]{0:T(128)}, f32[128]{0:T(128)S(1)}, u32[]{:S(2)}) copy-start(f32[128]{0:T(128)S(1)} %get-tuple-element.126) | copy-start | bytes 1540
  17.6 56.9 %copy-start.108 = (f32[128]{0:T(128)}, f32[128]{0:T(128)S(1)}, u32[]{:S(2)}) copy-start(f32[128]{0:T(128)S(1)} %fusion.75) | copy-start | bytes 1540
  17.6 255.2 %copy-start.94 = (f32[128]{0:T(128)}, f32[128]{0:T(128)S(1)}, u32[]{:S(2)}) copy-start(f32[128]{0:T(128)S(1)} %fusion.121) | copy-start | bytes 1540
  74.8 198.0 %copy-start.68 = (f32[2048]{0:T(1024)}, f32[2048]{0:T(1024)S(1)}, u32[]{:S(2)}) copy-start(f32[2048]{0:T(1024)S(1)} %reshape.592) | copy-start | bytes 24580
  79.7 62.1 %copy-start.110 = (f32[128]{0:T(128)}, f32[128]{0:T(128)S(1)}, u32[]{:S(2)}) copy-start(f32[128]{0:T(128)S(1)} %multiply_reduce_fusion.11) | copy-start | bytes 1540
  79.7 62.1 %copy-start.102 = (f32[128]{0:T(128)}, f32[128]{0:T(128)S(1)}, u32[]{:S(2)}) copy-start(f32[128]{0:T(128)S(1)} %fusion.122) | copy-start | bytes 1540
  80.3 200.6 %copy-start.76 = (f32[128,32]{0,1:T(8,128)}, f32[128,32]{0,1:T(8,128)S(1)}, u32[]{:S(2)}) copy-start(f32[128,32]{0,1:T(8,128)S(1)} %get-tuple-element.112) | copy-start | bytes 49156
  80.3 201.2 %copy-start.80 = (bf16[128,32]{0,1:T(8,128)(2,1)}, bf16[128,32]{0,1:T(8,128)(2,1)S(1)}, u32[]{:S(2)}) copy-start(bf16[128,32]{0,1:T(8,128)(2,1)S(1)} %get-tuple-element.114) | copy-start | bytes 24580
  80.3 201.2 %copy-start.82 = (bf16[128,32]{0,1:T(8,128)(2,1)}, bf16[128,32]{0,1:T(8,128)(2,1)S(1)}, u32[]{:S(2)}) copy-start(bf16[128,32]{0,1:T(8,128)(2,1)S(1)} %get-tuple-element.115) | copy-start | bytes 24580
  80.5 61.3 %copy-start.56 = (bf16[128,512]{0,1:T(8,128)(2,1)}, bf16[128,512]{0,1:T(8,128)(2,1)S(1)}, u32[]{:S(2)}) copy-start(bf16[128,512]{0,1:T(8,128)(2,1)S(1)} %multiply_convert_fusion.8) | copy-start | bytes 393220
  80.5 71.3 %copy-start.25 = (bf16[128,2048]{1,0:T(8,128)(2,1)S(1)}, bf16[128,2048]{1,0:T(8,128)(2,1)}, u32[]{:S(2)}) copy-start(bf16[128,2048]{1,0:T(8,128)(2,1)} %param.18) | copy-start | bytes 1572868
  141.8 18.0 collective-permute-start
  158.8 132.3 %copy-start.78 = (f32[2048]{0:T(1024)}, f32[2048]{0:T(1024)S(1)}, u32[]{:S(2)}) copy-start(f32[2048]{0:T(1024)S(1)} %reshape.594) | copy-start | bytes 24580
  159.2 132.5 %copy-start.28 = (bf16[2048,16]{1,0:T(8,128)(2,1)}, bf16[2048,16]{1,0:T(8,128)(2,1)S(1)}, u32[]{:S(2)}) copy-start(bf16[2048,16]{1,0:T(8,128)(2,1)S(1)} %reshape.570) | copy-start | bytes 196612
  159.7 123.2 %copy-start.6 = (bf16[128,16,256]{2,0,1:T(8,128)(2,1)}, bf16[128,16,256]{2,0,1:T(8,128)(2,1)S(1)}, u32[]{:S(2)}) copy-start(bf16[128,16,256]{2,0,1:T(8,128)(2,1)S(1)} %copy.132) | copy-start | bytes 3145732
  163.9 119.0 %copy-start.9 = (bf16[128,16,256]{2,0,1:T(8,128)(2,1)}, bf16[128,16,256]{2,0,1:T(8,128)(2,1)S(1)}, u32[]{:S(2)}) copy-start(bf16[128,16,256]{2,0,1:T(8,128)(2,1)S(1)} %copy.131) | copy-start | bytes 3145732
  164.6 116.9 %copy-start.74 = (bf16[128,64]{0,1:T(8,128)(2,1)}, bf16[128,64]{0,1:T(8,128)(2,1)S(1)}, u32[]{:S(2)}) copy-start(bf16[128,64]{0,1:T(8,128)(2,1)S(1)} %slice.248) | copy-start | bytes 49156
  325.4 263.7 %all-to-all-start = ((bf16[16,2,64,2048]{3,2,1,0:T(8,128)(2,1)}), bf16[16,2,64,2048]{3,2,1,0:T(8,128)(2,1)}, u32[]{:S(2)}, u32[]{:S(2)}) async-start(bf16[16,2,64,2048]{3,2,1,0:T(8,128)(2,1)} %pad_maximum_fusion.2), calls=%async_computation | async-start | bytes 16777216 | tf_op jit(solution)/shard_map/all_to_all | solution.py:258
  330.4 286.1 %collective-permute-start.1 = (bf16[2,2048,704]{1,2,0:T(8,128)(2,1)}, bf16[2,2048,704]{1,2,0:T(8,128)(2,1)}, u32[]{:S(2)}, u32[]{:S(2)}) collective-permute-start(bf16[2,2048,704]{1,2,0:T(8,128)(2,1)} %bitcast.398), channel_id=1, source_target_pairs={{0,1},{1,0},{2,3},{3,2},{4,5},{5,4},{6,7},{7,6},{8,9},{9,8},{10,11... | collective-permute-start | bytes 17301512 | tf_op jit(solution)/shard_map/ppermute | solution.py:73
  330.8 294.6 %collective-permute-start.2 = (bf16[704,2048]{1,0:T(8,128)(2,1)S(1)}, bf16[704,2048]{1,0:T(8,128)(2,1)}, u32[]{:S(2)}, u32[]{:S(2)}) collective-permute-start(bf16[704,2048]{1,0:T(8,128)(2,1)S(1)} %bitcast.401), channel_id=1, source_target_pairs={{0,1},{1,0},{2,3},{3,2},{4,5},{5,4},{6,7},{7,6},{8,9},{9,8},{10,11... | collective-permute-start | bytes 8650760 | tf_op jit(solution)/shard_map/ppermute | solution.py:73
  593.1 23.4 %copy-start.40 = (bf16[16,1,64,2048]{3,2,1,0:T(8,128)(2,1)}, bf16[16,1,64,2048]{3,2,1,0:T(8,128)(2,1)S(1)}, u32[]{:S(2)}) copy-start(bf16[16,1,64,2048]{3,2,1,0:T(8,128)(2,1)S(1)} %get-tuple-element.83) | copy-start | bytes 12582916
  593.1 32.3 %copy-start.42 = (bf16[16,1,64,2048]{3,2,1,0:T(8,128)(2,1)}, bf16[16,1,64,2048]{3,2,1,0:T(8,128)(2,1)S(1)}, u32[]{:S(2)}) copy-start(bf16[16,1,64,2048]{3,2,1,0:T(8,128)(2,1)S(1)} %get-tuple-element.84) | copy-start | bytes 12582916
  627.9 19.7 %slice-start.3 = ((s8[5767168]{0:T(1024)(128)(4,1)}), s8[4194304]{0:T(1024)(128)(4,1)S(1)}, s32[]{:S(2)}) async-start(s8[5767168]{0:T(1024)(128)(4,1)} %bitcast.399), calls=%async_computation.17 | async-start | bytes 8388608
  634.0 20.5 %copy-start.47 = (f32[1024,1,704]{0,2,1:T(8,128)}, f32[1024,1,704]{0,2,1:T(8,128)S(1)}, u32[]{:S(2)}) copy-start(f32[1024,1,704]{0,2,1:T(8,128)S(1)} %get-tuple-element.77) | copy-start | bytes 8650756
  634.0 20.5 %copy-start.49 = (f32[1024,1,704]{0,2,1:T(8,128)}, f32[1024,1,704]{0,2,1:T(8,128)S(1)}, u32[]{:S(2)}) copy-start(f32[1024,1,704]{0,2,1:T(8,128)S(1)} %get-tuple-element.78) | copy-start | bytes 8650756
  634.1 13.5 slice-start.4
  634.1 13.5 copy-start.115
  634.1 13.5 copy-start.117
  669.8 54.1 %copy-start.26 = (bf16[128,2048]{1,0:T(8,128)(2,1)S(1)}, bf16[128,2048]{1,0:T(8,128)(2,1)}, u32[]{:S(2)}) copy-start(bf16[128,2048]{1,0:T(8,128)(2,1)} %param.18) | copy-start | bytes 1572868
  669.8 214.4 %all-to-all-start.1 = ((bf16[16,2,64,2048]{3,2,1,0:T(8,128)(2,1)}), bf16[16,2,64,2048]{3,2,1,0:T(8,128)(2,1)}, u32[]{:S(2)}, u32[]{:S(2)}) async-start(bf16[16,2,64,2048]{3,2,1,0:T(8,128)(2,1)} %pad_maximum_fusion.3), calls=%async_computation.1 | async-start | bytes 16777216 | tf_op jit(solution)/shard_map/all_to_all | solution.py:296
  736.7 19.0 copy-start.5
  915.9 32.0 %copy-start.89 = (bf16[128,16]{0,1:T(8,128)(2,1)}, bf16[128,16]{0,1:T(8,128)(2,1)S(1)}, u32[]{:S(2)}) copy-start(bf16[128,16]{0,1:T(8,128)(2,1)S(1)} %fusion.110) | copy-start | bytes 12292
  989.7 5.0 collective-permute-start.3
  1025.0 9.8 copy-start.52
  1033.3 10.8 copy-start.51
  1033.3 67.2 %collective-permute-start.5 = (bf16[16,64,3072]{2,1,0:T(8,128)(2,1)}, bf16[16,64,3072]{2,1,0:T(8,128)(2,1)}, u32[]{:S(2)}, u32[]{:S(2)}) collective-permute-start(bf16[16,64,3072]{2,1,0:T(8,128)(2,1)} %fusion.15), channel_id=1, source_target_pairs={{0,1},{1,0},{2,3},{3,2},{4,5},{5,4},{6,7},{7,6},{8,9},{9,8},{10,11... | collective-permute-start | bytes 18874376 | tf_op jit(solution)/shard_map/ppermute | solution.py:73
  1100.4 81.8 %collective-permute-start.8 = (bf16[16,128,2816]{2,1,0:T(8,128)(2,1)}, bf16[16,128,2816]{2,1,0:T(8,128)(2,1)}, u32[]{:S(2)}, u32[]{:S(2)}) collective-permute-start(bf16[16,128,2816]{2,1,0:T(8,128)(2,1)} %fusion.2), channel_id=1, source_target_pairs={{0,1},{1,0},{2,3},{3,2},{4,5},{5,4},{6,7},{7,6},{8,9},{9,8},{10,11... | collective-permute-start | bytes 34603016 | tf_op jit(solution)/shard_map/ppermute | solution.py:73
  1111.8 36.5 %copy-start.45 = (bf16[128,2816]{1,0:T(8,128)(2,1)S(1)}, bf16[128,2816]{1,0:T(8,128)(2,1)}, u32[]{:S(2)}) copy-start(bf16[128,2816]{1,0:T(8,128)(2,1)} %get-tuple-element.87) | copy-start | bytes 2162692
  1111.8 156.7 %all-to-all-start.2 = ((bf16[16,64,3072]{2,1,0:T(8,128)(2,1)}), bf16[16,64,3072]{2,1,0:T(8,128)(2,1)}, u32[]{:S(2)}, u32[]{:S(2)}) async-start(bf16[16,64,3072]{2,1,0:T(8,128)(2,1)} %fusion.1), calls=%async_computation.2 | async-start | bytes 12582912 | tf_op jit(solution)/shard_map/all_to_all | solution.py:86
  1162.7 9.6 collective-permute-start.9
  1182.2 13.0 copy-start.16
  1201.9 96.1 %copy-start.90 = (bf16[128,16]{0,1:T(8,128)(2,1)S(1)}, bf16[128,16]{0,1:T(8,128)(2,1)}, u32[]{:S(2)}) copy-start(bf16[128,16]{0,1:T(8,128)(2,1)} %copy-done.89) | copy-start | bytes 12292
  1201.9 97.1 %copy-start.91 = (f32[2048]{0:T(1024)S(1)}, f32[2048]{0:T(1024)}, u32[]{:S(2)}) copy-start(f32[2048]{0:T(1024)} %get-tuple-element.61) | copy-start | bytes 24580
  1268.5 656.7 %all-to-all-start.3 = ((bf16[16,192,2816]{2,1,0:T(8,128)(2,1)}), bf16[16,192,2816]{2,1,0:T(8,128)(2,1)}, u32[]{:S(2)}, u32[]{:S(2)}) async-start(bf16[16,192,2816]{2,1,0:T(8,128)(2,1)} %pad_maximum_fusion.1), calls=%async_computation.5 | async-start | bytes 34603008 | tf_op jit(solution)/shard_map/all_to_all | solution.py:86
  1298.0 443.8 %reduce-scatter.10.cloned.1.call-start = ((), (), s32[]{:S(2)}) async-start(), calls=%async_computation.13 | async-start | bytes 1566720
  1303.0 4.1 collective-permute-start.4
  1307.1 14.0 collective-permute-start.6
  1309.8 514.7 %reduce-scatter.6.cloned.1.call-start = ((), (), s32[]{:S(2)}) async-start(), calls=%async_computation.9 | async-start | bytes 2228224 | tf_op jit(solution)/shard_map/reduce_scatter | solution.py:89
  1321.1 7.5 collective-permute-start.7
  1325.9 592.7 %reduce-scatter.8.cloned.1.call-start = ((), (), s32[]{:S(2)}) async-start(), calls=%async_computation.10 | async-start | bytes 4456448 | tf_op jit(solution)/shard_map/reduce_scatter | solution.py:89
  1347.8 13.6 copy-start.59
  1347.9 18.6 collective-permute-start.10
  1354.3 12.1 copy-start.41
  1354.3 12.1 copy-start.116
  1354.3 12.1 copy-start.118
  1354.4 7.1 collective-permute-start.11
  (84 other events, 338.1 us)
Sparse Core Ops, SparseCore 0:
  12.0 61.2 all-gather.13
  76.2 60.5 all-gather.7
  140.2 132.5 all-gather.9
  275.6 345.2 all-gather.11
  1309.9 431.8 reduce-scatter.9
  1744.0 80.5 reduce-scatter.5
  1826.8 91.7 reduce-scatter.7

commit v6 on v5

--- a/solution.py
+++ b/solution.py
@@ -457,7 +457,7 @@
     delta_query_weight = jnp.einsum(
         "td,tc->dc", normed_one, delta_query_raw, preferred_element_type=jnp.float32
     )
-    delta_query_local = scatter_rows(delta_query_weight, experts_all, by_exchange=True)
+    delta_query_local = scatter_rows(delta_query_weight, experts_all)
     delta_normed_one = jnp.einsum(
         "tc,dc->td", delta_query_raw, query_full, preferred_element_type=jnp.float32
     ) + jnp.einsum("tc,dc->td", delta_down_out, down_full, preferred_element_type=jnp.float32)

time: 1950 us -> 1890 us (0.969)
  waiting for transfers between devices: 1210 us -> 1180 us
  starting transfers between devices: 133 us -> 105 us
    reduce_scatter x2 -> x3, waiting for transfers between devices: 170 us -> 320 us  [reduce_over_expert(): lax.psum_scatter(rows, 'expert', scatter_dimension=0, tiled=True)]
    all_to_all x1, waiting for transfers between devices: 111 us -> 26.4 us  [shards(): lax.all_to_all(going_back, 'expert', split_axis=0, concat_axis=0, tiled=T...]
    all_to_all x2 -> x1, waiting for transfers between devices: 66.6 us -> 0.01 us  [reduce_over_expert(): lax.all_to_all(total, 'expert', split_axis=0, concat_axis=0, tiled=True)]
    all_to_all x2 -> x1, starting transfers between devices: 65.9 us -> 36.4 us  [reduce_over_expert(): lax.all_to_all(total, 'expert', split_axis=0, concat_axis=0, tiled=True)]
    unnamed x8 -> x9, waiting for transfers between devices: 367 us -> 341 us
  transfers between devices with their start and end apart: 23 -> 23, of which waited for: 13 -> 12; matrix products, arithmetic and copies ran while one was open for 21% -> 27% of each run, Pallas kernels for 0% -> 0%
where the time goes in v6:
time: 1890 us
  waiting for transfers between devices  1180 us (62%)
  matrix products  222 us (12%)
  local copies, waits for them, and re-layouts  189 us (10%)
  other arithmetic  170 us (9%)
  starting transfers between devices  105 us (6%)
    unnamed x9, waiting for transfers between devices  341 us
    reduce_scatter x3, waiting for transfers between devices, reduce_over_expert(): lax.psum_scatter(rows, 'expert', scatter_dimension=0, tiled=True)  320 us
    all_to_all x1, waiting for transfers between devices, shards(): lax.all_to_all(outgoing, 'expert', split_axis=0, concat_axis=0, tiled=True)  258 us
    all_gather x1, waiting for transfers between devices, shards(): lax.all_gather(jnp.concatenate([query_weight, output_weight.T], axis=1),...  108 us
    all_gather x1, waiting for transfers between devices, shards(): up_full = lax.all_gather(latent_up, ALL, axis=0, tiled=True)  56.4 us
    all_gather x1, waiting for transfers between devices, shards(): lax.all_gather(jnp.concatenate([latent_down, small_local], axis=0), ALL,...  55.7 us
    dot_general x10, matrix products, matmul(): return jnp.dot(left_side, right_side, preferred_element_type=jnp.float32)  53.7 us
    all_to_all x1, starting transfers between devices, shards(): lax.all_to_all(going_back, 'expert', split_axis=0, concat_axis=0, tiled=T...  53.4 us
  transfers between devices with their start and end apart: 23, of which 12 were waited for; matrix products, arithmetic and copies ran while one was open for 27% of the time, Pallas kernels for 0%

profile of v6, /device:TPU:0, one launch (start us, length us, event | category | flops | bytes accessed | tf_op | source)
XLA Modules:
  0.0 1885.4 jit_solution(5496666525788474103)
XLA Ops:
  17.6 55.7 %all-gather.14.cloned.1.call-done = bf16[32,67,576]{2,1,0:T(8,128)(2,1)} async-done(((bf16[1,67,576]{2,1,0:T(8,128)(2,1)}), bf16[32,67,576]{2,1,0:T(8,128)(2,1)}) %all-gather.14.cloned.1.call-update) | async-done | bytes 2469904 | tf_op jit(solution)/shard_map/all_gather | solution.py:151
  80.4 56.4 %all-gather.8.cloned.1.call-done = bf16[512,4096]{1,0:T(8,128)(2,1)} async-done(((bf16[16,4096]{1,0:T(8,128)(2,1)}), bf16[512,4096]{1,0:T(8,128)(2,1)}) %all-gather.8.cloned.1.call-update) | async-done | bytes 4194320 | tf_op jit(solution)/shard_map/all_gather | solution.py:170
  151.7 6.7 gather_fusion.1
  164.4 108.4 %all-gather.10.cloned.1.call-done = bf16[2048,5120]{1,0:T(8,128)(2,1)} async-done(((bf16[64,5120]{1,0:T(8,128)(2,1)}), bf16[2048,5120]{1,0:T(8,128)(2,1)}) %all-gather.10.cloned.1.call-update) | async-done | bytes 20971536 | tf_op jit(solution)/shard_map/all_gather | solution.py:165
  272.8 8.1 fusion.7
  283.7 7.3 multiply_reduce_fusion.8
  292.5 5.1 gather_fusion.3
  303.4 6.0 gather_fusion
  314.0 5.3 multiply_convert_fusion
  319.3 6.4 pad_maximum_fusion.2
  325.6 5.0 all-to-all-start
  331.2 258.2 %all-to-all-done = bf16[16,2,64,2048]{3,2,1,0:T(8,128)(2,1)} async-done(((bf16[16,2,64,2048]{3,2,1,0:T(8,128)(2,1)}), bf16[16,2,64,2048]{3,2,1,0:T(8,128)(2,1)}, u32[]{:S(2)}, u32[]{:S(2)}) %all-to-all-start) | async-done | bytes 8388640 | tf_op jit(solution)/shard_map/all_to_all | solution.py:258
  593.5 10.6 fusion.135
  605.0 5.7 fusion.60
  610.8 6.1 fusion.35
  616.9 8.9 fusion.160
  628.3 6.2 multiply_bitcast_fusion
  634.5 13.5 add_convert_fusion
  648.0 7.2 fusion.81
  655.2 8.8 fusion.10
  664.1 6.3 pad_maximum_fusion.3
  670.4 53.4 %all-to-all-start.1 = ((bf16[16,2,64,2048]{3,2,1,0:T(8,128)(2,1)}), bf16[16,2,64,2048]{3,2,1,0:T(8,128)(2,1)}, u32[]{:S(2)}, u32[]{:S(2)}) async-start(bf16[16,2,64,2048]{3,2,1,0:T(8,128)(2,1)} %pad_maximum_fusion.3), calls=%async_computation.1 | async-start | bytes 16777216 | tf_op jit(solution)/shard_map/all_to_all | solution.py:296
  728.2 8.3 mul.559
  736.6 15.8 fusion.152
  766.5 9.4 fusion.169
  775.9 9.4 fusion.168
  785.3 34.0 %pad_maximum_fusion = f32[2,16,2,64,2816]{4,3,0,2,1:T(8,128)} fusion(f32[1,16,2,64,2816]{4,3,0,2,1:T(8,128)} %bitcast.349, f32[1,16,2,64,2816]{4,3,0,2,1:T(8,128)} %bitcast.350), kind=kLoop, calls=%fused_computation.7 | loop fusion | flops 11534336 | bytes 92274688 | tf_op jit(solution)/shard_map/stack | solution.py:332
  819.3 12.8 fusion.2
  832.2 8.0 fusion.163
  840.2 9.4 fusion.170
  849.7 7.5 fusion.16
  857.6 26.4 %all-to-all-done.1 = bf16[16,2,64,2048]{3,2,1,0:T(8,128)(2,1)} async-done(((bf16[16,2,64,2048]{3,2,1,0:T(8,128)(2,1)}), bf16[16,2,64,2048]{3,2,1,0:T(8,128)(2,1)}, u32[]{:S(2)}, u32[]{:S(2)}) %all-to-all-start.1) | async-done | bytes 8388640 | tf_op jit(solution)/shard_map/all_to_all | solution.py:296
  884.1 6.2 fusion.153
  890.3 9.8 gather_fusion.5
  900.1 9.8 gather_fusion.4
  915.2 8.4 select_convert_fusion
  923.6 8.2 reshape.600
  931.9 7.0 reduce_sum.204
  939.0 9.5 fusion.40
  955.7 7.9 reshape.599
  963.6 6.6 multiply_reduce_fusion
  970.2 9.7 multiply_reduce_fusion.3
  980.9 5.6 fusion.41
  1001.0 10.0 fusion.4
  1016.8 12.8 fusion
  1029.7 6.8 pad_maximum_fusion.1
  1036.5 36.4 %all-to-all-start.2 = ((bf16[16,192,2816]{2,1,0:T(8,128)(2,1)}), bf16[16,192,2816]{2,1,0:T(8,128)(2,1)}, u32[]{:S(2)}, u32[]{:S(2)}) async-start(bf16[16,192,2816]{2,1,0:T(8,128)(2,1)} %pad_maximum_fusion.1), calls=%async_computation.5 | async-start | bytes 34603008 | tf_op jit(solution)/shard_map/all_to_all | solution.py:86
  1073.6 7.5 fusion.5
  1096.8 5.8 copy-done.2
  1113.0 8.4 fusion.9
  1122.5 10.2 fusion.165
  1132.7 5.5 fusion.15
  1138.7 9.9 collective-permute-done.5
  1148.6 11.4 fusion.1
  1161.8 9.1 convert_bitcast_fusion
  1171.4 6.2 convolution_convert_fusion.1
  1177.9 6.6 collective-permute-done.11
  1184.5 5.0 add_bitcast_fusion
  1189.6 9.1 fusion.3
  1198.7 339.9 %reduce-scatter.13.cloned.1.call-done = bf16[72,576]{1,0:T(8,128)(2,1)} async-done(((bf16[1152,576]{1,0:T(8,128)(2,1)}), bf16[72,576]{1,0:T(8,128)(2,1)}) %reduce-scatter.13.cloned.1.call-update) | async-done | bytes 82960
  1543.4 77.9 %reduce-scatter.9.cloned.1.call-done = bf16[16,4096]{1,0:T(8,128)(2,1)} async-done(((bf16[256,4096]{1,0:T(8,128)(2,1)}), bf16[16,4096]{1,0:T(8,128)(2,1)}) %reduce-scatter.9.cloned.1.call-update) | async-done | bytes 131088 | tf_op jit(solution)/shard_map/reduce_scatter | solution.py:89
  1622.9 92.6 %reduce-scatter.11.cloned.1.call-done = bf16[64,2048]{1,0:T(8,128)(2,1)} async-done(((bf16[1024,2048]{1,0:T(8,128)(2,1)}), bf16[64,2048]{1,0:T(8,128)(2,1)}) %reduce-scatter.11.cloned.1.call-update) | async-done | bytes 262160 | tf_op jit(solution)/shard_map/reduce_scatter | solution.py:89
  1717.3 149.8 %reduce-scatter.7.cloned.1.call-done = bf16[64,3072]{1,0:T(8,128)(2,1)} async-done(((bf16[1024,3072]{1,0:T(8,128)(2,1)}), bf16[64,3072]{1,0:T(8,128)(2,1)}) %reduce-scatter.7.cloned.1.call-update) | async-done | bytes 393232 | tf_op jit(solution)/shard_map/reduce_scatter | solution.py:89
  1869.0 7.0 convert_reduce_fusion
  (437 shorter events, 156.2 us)
Async XLA Ops:
  7.2 66.2 %all-gather.14.cloned.1.call-start = ((), (), s32[]{:S(2)}) async-start(), calls=%async_computation.13 | async-start | bytes 3041280 | tf_op jit(solution)/shard_map/all_gather | solution.py:151
  11.9 124.9 %all-gather.8.cloned.1.call-start = ((), (), s32[]{:S(2)}) async-start(), calls=%async_computation.7 | async-start | bytes 4325376 | tf_op jit(solution)/shard_map/all_gather | solution.py:170
  12.7 260.1 %all-gather.10.cloned.1.call-start = ((), (), s32[]{:S(2)}) async-start(), calls=%async_computation.8 | async-start | bytes 21626880 | tf_op jit(solution)/shard_map/all_gather | solution.py:165
  14.7 721.9 %all-gather.12.cloned.1.call-start = ((), (), s32[]{:S(2)}) async-start(), calls=%async_computation.12 | async-start | bytes 35684352 | tf_op jit(solution)/shard_map/all_gather | solution.py:172
  17.2 127.7 %copy-start.62 = (s32[128,6]{1,0:T(8,128)}, s32[128,6]{1,0:T(8,128)S(1)}, u32[]{:S(2)}) copy-start(s32[128,6]{1,0:T(8,128)S(1)} %copy.140) | copy-start | bytes 9220
  17.4 62.3 %copy-start.101 = (f32[32]{0:T(128)}, f32[32]{0:T(128)S(1)}, u32[]{:S(2)}) copy-start(f32[32]{0:T(128)S(1)} %multiply_power_fusion) | copy-start | bytes 388
  17.4 62.3 %copy-start.103 = (f32[128]{0:T(128)}, f32[128]{0:T(128)S(1)}, u32[]{:S(2)}) copy-start(f32[128]{0:T(128)S(1)} %get-tuple-element.126) | copy-start | bytes 1540
  17.6 56.9 %copy-start.105 = (f32[128]{0:T(128)}, f32[128]{0:T(128)S(1)}, u32[]{:S(2)}) copy-start(f32[128]{0:T(128)S(1)} %fusion.75) | copy-start | bytes 1540
  17.6 255.2 %copy-start.89 = (f32[128]{0:T(128)}, f32[128]{0:T(128)S(1)}, u32[]{:S(2)}) copy-start(f32[128]{0:T(128)S(1)} %fusion.121) | copy-start | bytes 1540
  74.8 198.0 %copy-start.64 = (f32[2048]{0:T(1024)}, f32[2048]{0:T(1024)S(1)}, u32[]{:S(2)}) copy-start(f32[2048]{0:T(1024)S(1)} %reshape.596) | copy-start | bytes 24580
  79.6 62.1 %copy-start.107 = (f32[128]{0:T(128)}, f32[128]{0:T(128)S(1)}, u32[]{:S(2)}) copy-start(f32[128]{0:T(128)S(1)} %multiply_reduce_fusion.11) | copy-start | bytes 1540
  79.6 62.1 %copy-start.98 = (f32[128]{0:T(128)}, f32[128]{0:T(128)S(1)}, u32[]{:S(2)}) copy-start(f32[128]{0:T(128)S(1)} %fusion.122) | copy-start | bytes 1540
  80.2 200.7 %copy-start.72 = (f32[128,32]{0,1:T(8,128)}, f32[128,32]{0,1:T(8,128)S(1)}, u32[]{:S(2)}) copy-start(f32[128,32]{0,1:T(8,128)S(1)} %get-tuple-element.112) | copy-start | bytes 49156
  80.2 201.3 %copy-start.76 = (bf16[128,32]{0,1:T(8,128)(2,1)}, bf16[128,32]{0,1:T(8,128)(2,1)S(1)}, u32[]{:S(2)}) copy-start(bf16[128,32]{0,1:T(8,128)(2,1)S(1)} %get-tuple-element.114) | copy-start | bytes 24580
  80.2 201.3 %copy-start.78 = (bf16[128,32]{0,1:T(8,128)(2,1)}, bf16[128,32]{0,1:T(8,128)(2,1)S(1)}, u32[]{:S(2)}) copy-start(bf16[128,32]{0,1:T(8,128)(2,1)S(1)} %get-tuple-element.115) | copy-start | bytes 24580
  80.4 61.4 %copy-start.52 = (bf16[128,512]{0,1:T(8,128)(2,1)}, bf16[128,512]{0,1:T(8,128)(2,1)S(1)}, u32[]{:S(2)}) copy-start(bf16[128,512]{0,1:T(8,128)(2,1)S(1)} %multiply_convert_fusion.8) | copy-start | bytes 393220
  80.4 71.2 %copy-start.23 = (bf16[128,2048]{1,0:T(8,128)(2,1)S(1)}, bf16[128,2048]{1,0:T(8,128)(2,1)}, u32[]{:S(2)}) copy-start(bf16[128,2048]{1,0:T(8,128)(2,1)} %param.18) | copy-start | bytes 1572868
  141.8 17.7 collective-permute-start
  158.5 132.6 %copy-start.74 = (f32[2048]{0:T(1024)}, f32[2048]{0:T(1024)S(1)}, u32[]{:S(2)}) copy-start(f32[2048]{0:T(1024)S(1)} %reshape.598) | copy-start | bytes 24580
  158.9 132.8 %copy-start.26 = (bf16[2048,16]{1,0:T(8,128)(2,1)}, bf16[2048,16]{1,0:T(8,128)(2,1)S(1)}, u32[]{:S(2)}) copy-start(bf16[2048,16]{1,0:T(8,128)(2,1)S(1)} %reshape.573) | copy-start | bytes 196612
  159.5 123.4 %copy-start.9 = (bf16[128,16,256]{2,0,1:T(8,128)(2,1)}, bf16[128,16,256]{2,0,1:T(8,128)(2,1)S(1)}, u32[]{:S(2)}) copy-start(bf16[128,16,256]{2,0,1:T(8,128)(2,1)S(1)} %copy.132) | copy-start | bytes 3145732
  163.6 119.3 %copy-start.11 = (bf16[128,16,256]{2,0,1:T(8,128)(2,1)}, bf16[128,16,256]{2,0,1:T(8,128)(2,1)S(1)}, u32[]{:S(2)}) copy-start(bf16[128,16,256]{2,0,1:T(8,128)(2,1)S(1)} %copy.131) | copy-start | bytes 3145732
  164.4 117.2 %copy-start.70 = (bf16[128,64]{0,1:T(8,128)(2,1)}, bf16[128,64]{0,1:T(8,128)(2,1)S(1)}, u32[]{:S(2)}) copy-start(bf16[128,64]{0,1:T(8,128)(2,1)S(1)} %slice.248) | copy-start | bytes 49156
  325.6 263.8 %all-to-all-start = ((bf16[16,2,64,2048]{3,2,1,0:T(8,128)(2,1)}), bf16[16,2,64,2048]{3,2,1,0:T(8,128)(2,1)}, u32[]{:S(2)}, u32[]{:S(2)}) async-start(bf16[16,2,64,2048]{3,2,1,0:T(8,128)(2,1)} %pad_maximum_fusion.2), calls=%async_computation | async-start | bytes 16777216 | tf_op jit(solution)/shard_map/all_to_all | solution.py:258
  330.6 286.2 %collective-permute-start.1 = (bf16[2,2048,704]{1,2,0:T(8,128)(2,1)}, bf16[2,2048,704]{1,2,0:T(8,128)(2,1)}, u32[]{:S(2)}, u32[]{:S(2)}) collective-permute-start(bf16[2,2048,704]{1,2,0:T(8,128)(2,1)} %bitcast.400), channel_id=1, source_target_pairs={{0,1},{1,0},{2,3},{3,2},{4,5},{5,4},{6,7},{7,6},{8,9},{9,8},{10,11... | collective-permute-start | bytes 17301512 | tf_op jit(solution)/shard_map/ppermute | solution.py:73
  331.0 294.8 %collective-permute-start.2 = (bf16[704,2048]{1,0:T(8,128)(2,1)S(1)}, bf16[704,2048]{1,0:T(8,128)(2,1)}, u32[]{:S(2)}, u32[]{:S(2)}) collective-permute-start(bf16[704,2048]{1,0:T(8,128)(2,1)S(1)} %bitcast.403), channel_id=1, source_target_pairs={{0,1},{1,0},{2,3},{3,2},{4,5},{5,4},{6,7},{7,6},{8,9},{9,8},{10,11... | collective-permute-start | bytes 8650760 | tf_op jit(solution)/shard_map/ppermute | solution.py:73
  593.4 23.4 %copy-start.36 = (bf16[16,1,64,2048]{3,2,1,0:T(8,128)(2,1)}, bf16[16,1,64,2048]{3,2,1,0:T(8,128)(2,1)S(1)}, u32[]{:S(2)}) copy-start(bf16[16,1,64,2048]{3,2,1,0:T(8,128)(2,1)S(1)} %get-tuple-element.83) | copy-start | bytes 12582916
  593.4 32.3 %copy-start.38 = (bf16[16,1,64,2048]{3,2,1,0:T(8,128)(2,1)}, bf16[16,1,64,2048]{3,2,1,0:T(8,128)(2,1)S(1)}, u32[]{:S(2)}) copy-start(bf16[16,1,64,2048]{3,2,1,0:T(8,128)(2,1)S(1)} %get-tuple-element.84) | copy-start | bytes 12582916
  628.3 19.7 %slice-start.2 = ((s8[5767168]{0:T(1024)(128)(4,1)}), s8[4194304]{0:T(1024)(128)(4,1)S(1)}, s32[]{:S(2)}) async-start(s8[5767168]{0:T(1024)(128)(4,1)} %bitcast.401), calls=%async_computation.17 | async-start | bytes 8388608
  634.5 20.8 %copy-start.42 = (f32[1024,1,704]{0,2,1:T(8,128)}, f32[1024,1,704]{0,2,1:T(8,128)S(1)}, u32[]{:S(2)}) copy-start(f32[1024,1,704]{0,2,1:T(8,128)S(1)} %get-tuple-element.77) | copy-start | bytes 8650756
  634.5 20.8 %copy-start.44 = (f32[1024,1,704]{0,2,1:T(8,128)}, f32[1024,1,704]{0,2,1:T(8,128)S(1)}, u32[]{:S(2)}) copy-start(f32[1024,1,704]{0,2,1:T(8,128)S(1)} %get-tuple-element.78) | copy-start | bytes 8650756
  634.5 13.5 slice-start.3
  634.5 13.5 copy-start.113
  634.5 13.5 copy-start.115
  670.4 53.4 %copy-start.24 = (bf16[128,2048]{1,0:T(8,128)(2,1)S(1)}, bf16[128,2048]{1,0:T(8,128)(2,1)}, u32[]{:S(2)}) copy-start(bf16[128,2048]{1,0:T(8,128)(2,1)} %param.18) | copy-start | bytes 1572868
  670.4 213.7 %all-to-all-start.1 = ((bf16[16,2,64,2048]{3,2,1,0:T(8,128)(2,1)}), bf16[16,2,64,2048]{3,2,1,0:T(8,128)(2,1)}, u32[]{:S(2)}, u32[]{:S(2)}) async-start(bf16[16,2,64,2048]{3,2,1,0:T(8,128)(2,1)} %pad_maximum_fusion.3), calls=%async_computation.1 | async-start | bytes 16777216 | tf_op jit(solution)/shard_map/all_to_all | solution.py:296
  736.6 15.8 copy-start.8
  819.3 12.9 copy-start.46
  832.1 184.7 %collective-permute-start.8 = (bf16[16,128,2816]{2,1,0:T(8,128)(2,1)}, bf16[16,128,2816]{2,1,0:T(8,128)(2,1)}, u32[]{:S(2)}, u32[]{:S(2)}) collective-permute-start(bf16[16,128,2816]{2,1,0:T(8,128)(2,1)} %fusion.2), channel_id=1, source_target_pairs={{0,1},{1,0},{2,3},{3,2},{4,5},{5,4},{6,7},{7,6},{8,9},{9,8},{10,11... | collective-permute-start | bytes 34603016 | tf_op jit(solution)/shard_map/ppermute | solution.py:73
  857.2 143.8 %collective-permute-start.9 = (bf16[16,64,2816]{2,1,0:T(8,128)(2,1)}, bf16[16,64,2816]{2,1,0:T(8,128)(2,1)}, u32[]{:S(2)}, u32[]{:S(2)}) collective-permute-start(bf16[16,64,2816]{2,1,0:T(8,128)(2,1)} %fusion.16), channel_id=1, source_target_pairs={{0,1},{1,0},{2,3},{3,2},{4,5},{5,4},{6,7},{7,6},{8,9},{9,8},{10,11... | collective-permute-start | bytes 17301512 | tf_op jit(solution)/shard_map/ppermute | solution.py:73
  938.9 12.7 copy-start.27
  938.9 12.7 copy-start.75
  939.0 12.7 copy-start.97
  995.2 15.7 collective-permute-start.3
  1015.5 14.2 slice-start
  1016.8 12.8 slice-start.1
  1036.4 36.5 %copy-start.102 = (f32[32]{0:T(128)S(1)}, f32[32]{0:T(128)}, u32[]{:S(2)}) copy-start(f32[32]{0:T(128)} %copy-done.101) | copy-start | bytes 388
  1036.4 36.5 %copy-start.104 = (f32[128]{0:T(128)S(1)}, f32[128]{0:T(128)}, u32[]{:S(2)}) copy-start(f32[128]{0:T(128)} %copy-done.103) | copy-start | bytes 1540
  1036.4 36.8 %copy-start.73 = (f32[128,32]{0,1:T(8,128)S(1)}, f32[128,32]{0,1:T(8,128)}, u32[]{:S(2)}) copy-start(f32[128,32]{0,1:T(8,128)} %copy-done.72) | copy-start | bytes 49156
  1036.4 36.8 %copy-start.50 = (bf16[128,16,128]{0,2,1:T(8,128)(2,1)S(1)}, bf16[128,16,128]{0,2,1:T(8,128)(2,1)}, u32[]{:S(2)}) copy-start(bf16[128,16,128]{0,2,1:T(8,128)(2,1)} %fusion.65) | copy-start | bytes 1572868
  1036.4 36.9 %copy-start.108 = (f32[128]{0:T(128)S(1)}, f32[128]{0:T(128)}, u32[]{:S(2)}) copy-start(f32[128]{0:T(128)} %copy-done.107) | copy-start | bytes 1540
  1036.5 832.6 %all-to-all-start.2 = ((bf16[16,192,2816]{2,1,0:T(8,128)(2,1)}), bf16[16,192,2816]{2,1,0:T(8,128)(2,1)}, u32[]{:S(2)}, u32[]{:S(2)}) async-start(bf16[16,192,2816]{2,1,0:T(8,128)(2,1)} %pad_maximum_fusion.1), calls=%async_computation.5 | async-start | bytes 34603008 | tf_op jit(solution)/shard_map/all_to_all | solution.py:86
  1072.9 465.7 %reduce-scatter.13.cloned.1.call-start = ((), (), s32[]{:S(2)}) async-start(), calls=%async_computation.14 | async-start | bytes 1566720
  1087.1 4.7 collective-permute-start.4
  1091.2 14.7 collective-permute-start.6
  1093.9 527.4 %reduce-scatter.9.cloned.1.call-start = ((), (), s32[]{:S(2)}) async-start(), calls=%async_computation.10 | async-start | bytes 2228224 | tf_op jit(solution)/shard_map/reduce_scatter | solution.py:89
  1105.2 7.8 collective-permute-start.7
  1110.6 604.9 %reduce-scatter.11.cloned.1.call-start = ((), (), s32[]{:S(2)}) async-start(), calls=%async_computation.11 | async-start | bytes 4456448 | tf_op jit(solution)/shard_map/reduce_scatter | solution.py:89
  1121.4 745.7 %reduce-scatter.7.cloned.1.call-start = ((), (), s32[]{:S(2)}) async-start(), calls=%async_computation.9 | async-start | bytes 6684672 | tf_op jit(solution)/shard_map/reduce_scatter | solution.py:89
  1138.3 10.4 collective-permute-start.5
  1170.9 13.6 copy-start.55
  1170.9 18.6 collective-permute-start.10
  1177.5 12.0 copy-start.37
  1177.6 7.0 collective-permute-start.11
  (81 other events, 380.7 us)
Sparse Core Ops, SparseCore 0:
  12.0 61.2 all-gather.13
  76.2 60.5 all-gather.7
  140.2 132.5 all-gather.9
  275.6 345.2 all-gather.11
  1094.0 444.5 reduce-scatter.12
  1540.7 80.5 reduce-scatter.8
  1623.6 91.8 reduce-scatter.10
  1720.8 146.2 reduce-scatter.6

commit v7 on v4

--- a/solution.py
+++ b/solution.py
@@ -2,6 +2,7 @@
 import jax.numpy as jnp
 from jax import lax
 from jax.sharding import PartitionSpec as P
+
 
 D = 2048
 H = 16
@@ -83,7 +84,8 @@
 
 def reduce_over_expert(total):
     rows = total.reshape((-1,) + total.shape[2:])
-    return lax.psum_scatter(rows, "expert", scatter_dimension=0, tiled=True).astype(jnp.float32)
+    summed = lax.psum_scatter(rows, "expert", scatter_dimension=0, tiled=True)
+    return summed.astype(jnp.float32)
 
 
 def scatter_rows(full, experts):
@@ -253,6 +255,45 @@
         axis=1,
     )
     incoming = lax.all_to_all(outgoing, "expert", split_axis=0, concat_axis=0, tiled=True)
+
+    shared_gate = matmul(normed_two, shared_in_full[0])
+    shared_up = matmul(normed_two, shared_in_full[1])
+    shared_hidden = gated_pair(shared_gate, shared_up).astype(jnp.bfloat16)
+    shared_result = jnp.einsum(
+        "tf,df->td", shared_hidden, shared_out_t_full, preferred_element_type=jnp.float32
+    )
+    delta_shared_outer_t = jnp.einsum(
+        "td,tf->df", cotangent, shared_hidden, preferred_element_type=jnp.float32
+    )
+    delta_shared_hidden = jnp.einsum(
+        "td,df->tf", cotangent, shared_out_t_full, preferred_element_type=jnp.float32
+    )
+    _, shared_back = jax.vjp(gated_pair, shared_gate, shared_up)
+    delta_gate, delta_up = [
+        part.astype(jnp.bfloat16) for part in shared_back(delta_shared_hidden)
+    ]
+    delta_shared_inner = jnp.stack(
+        [
+            jnp.einsum("td,tf->df", normed_two, part, preferred_element_type=jnp.float32)
+            for part in (delta_gate, delta_up)
+        ]
+    )
+    delta_normed = matmul(delta_gate, shared_in_full[0].T) + matmul(
+        delta_up, shared_in_full[1].T
+    )
+    inner_grad_blocks = jnp.transpose(
+        delta_shared_inner.reshape(
+            (shared_inner.shape[0], experts_all, shard_count) + shared_inner.shape[1:]
+        ),
+        (1, 2, 0, 3, 4),
+    ).reshape((experts_all, shard_count, -1, shared_inner.shape[-1]))
+    outer_grad_blocks = delta_shared_outer_t.reshape(
+        (experts_all, shard_count, -1, delta_shared_outer_t.shape[-1])
+    )
+    ffn_total = jnp.concatenate(
+        [pair_total(inner_grad_blocks), pair_total(outer_grad_blocks)], axis=1
+    )
+    incoming, ffn_total = lax.optimization_barrier((incoming, ffn_total))
     arrived = incoming[:, 0].reshape(-1, D)
     delta_arrived = incoming[:, 1].reshape(-1, D)
 
@@ -273,7 +314,7 @@
         delta_hidden = jnp.einsum(
             "rd,fd->rf", delta_arrived, weight, preferred_element_type=jnp.float32
         )
-        unused_expert, expert_back = jax.vjp(gated, pre)
+        _, expert_back = jax.vjp(gated, pre)
         delta_pre_halves.append(expert_back(delta_hidden)[0].astype(jnp.bfloat16))
     delta_inner_halves = [
         jnp.einsum("rd,rgf->gdf", arrived, delta_pre, preferred_element_type=jnp.float32)
@@ -300,12 +341,6 @@
 
     picked = jnp.take(returned, slot_of, axis=0).reshape(tok_rows, TOPK, D).astype(jnp.float32)
     routed = jnp.sum(gate_values[..., None] * picked, axis=1)
-    shared_gate = matmul(normed_two, shared_in_full[0])
-    shared_up = matmul(normed_two, shared_in_full[1])
-    shared_hidden = gated_pair(shared_gate, shared_up).astype(jnp.bfloat16)
-    shared_result = jnp.einsum(
-        "tf,df->td", shared_hidden, shared_out_t_full, preferred_element_type=jnp.float32
-    )
     feedforward = routed + shared_result
     layer_output = (residual + feedforward).astype(jnp.bfloat16)
     square_sums = jnp.stack(
@@ -316,25 +351,6 @@
         ]
     )
 
-    delta_shared_outer_t = jnp.einsum(
-        "td,tf->df", cotangent, shared_hidden, preferred_element_type=jnp.float32
-    )
-    delta_shared_hidden = jnp.einsum(
-        "td,df->tf", cotangent, shared_out_t_full, preferred_element_type=jnp.float32
-    )
-    unused_shared, shared_back = jax.vjp(gated_pair, shared_gate, shared_up)
-    delta_gate, delta_up = [
-        part.astype(jnp.bfloat16) for part in shared_back(delta_shared_hidden)
-    ]
-    delta_shared_inner = jnp.stack(
-        [
-            jnp.einsum("td,tf->df", normed_two, part, preferred_element_type=jnp.float32)
-            for part in (delta_gate, delta_up)
-        ]
-    )
-    delta_normed = matmul(delta_gate, shared_in_full[0].T) + matmul(
-        delta_up, shared_in_full[1].T
-    )
     delta_gates = jnp.sum(delta_out[:, None, :] * picked, axis=-1)
     delta_normed = delta_normed + jnp.sum(
         jnp.take(delta_returned, slot_of, axis=0).reshape(tok_rows, TOPK, D).astype(jnp.float32),
@@ -351,21 +367,9 @@
     delta_normed = delta_normed + jnp.einsum(
         "te,de->td", delta_logits, router_full, preferred_element_type=jnp.float32
     )
-    unused_second, second_back = jax.vjp(norm_rows, residual, gain_two_float)
+    _, second_back = jax.vjp(norm_rows, residual, gain_two_float)
     delta_residual_norm, delta_gain_two = second_back(delta_normed)
     delta_residual = delta_out + delta_residual_norm
-    inner_grad_blocks = jnp.transpose(
-        delta_shared_inner.reshape(
-            (shared_inner.shape[0], experts_all, shard_count) + shared_inner.shape[1:]
-        ),
-        (1, 2, 0, 3, 4),
-    ).reshape((experts_all, shard_count, -1, shared_inner.shape[-1]))
-    outer_grad_blocks = delta_shared_outer_t.reshape(
-        (experts_all, shard_count, -1, delta_shared_outer_t.shape[-1])
-    )
-    ffn_total = jnp.concatenate(
-        [pair_total(inner_grad_blocks), pair_total(outer_grad_blocks)], axis=1
-    )
     ffn_local = reduce_over_expert(ffn_total)
     delta_shared_inner_local = ffn_local[:inner_rows].reshape(shared_inner.shape)
     delta_shared_outer_local = ffn_local[inner_rows:].T
@@ -375,11 +379,10 @@
         "td,tc->dc", delta_attention, mixed_heads, preferred_element_type=jnp.float32
     )
     delta_output_local = scatter_rows(delta_output_t, experts_all).T
-    delta_mixed = (
-        jnp.einsum("td,dc->tc", delta_attention, output_t_full, preferred_element_type=jnp.float32)
-        .astype(jnp.bfloat16)
-        .reshape(tok_rows, H, DV)
-    )
+    delta_mixed = jnp.einsum(
+        "td,dc->tc", delta_attention, output_t_full, preferred_element_type=jnp.float32
+    )
+    delta_mixed = delta_mixed.astype(jnp.bfloat16).reshape(tok_rows, H, DV)
     delta_weights = jnp.einsum(
         "qhd,khd->hqk", delta_mixed, key_rows[..., DN:], preferred_element_type=jnp.float32
     )
@@ -432,7 +435,7 @@
     delta_latents = jnp.einsum(
         "tc,lc->tl", delta_expanded, up_full, preferred_element_type=jnp.float32
     )
-    unused_latent, latent_back = jax.vjp(norm_rows, latent_raw, gain_latent_float)
+    _, latent_back = jax.vjp(norm_rows, latent_raw, gain_latent_float)
     delta_latent_raw, delta_gain_latent = latent_back(delta_latents)
     delta_down_out = jnp.concatenate(
         [delta_latent_raw, rotate(delta_rotary_total, cosine_table, -sine_table)], axis=-1
@@ -458,7 +461,7 @@
     delta_normed_one = jnp.einsum(
         "tc,dc->td", delta_query_raw, query_full, preferred_element_type=jnp.float32
     ) + jnp.einsum("tc,dc->td", delta_down_out, down_full, preferred_element_type=jnp.float32)
-    unused_first, first_back = jax.vjp(norm_rows, tokens_float, gain_one_float)
+    _, first_back = jax.vjp(norm_rows, tokens_float, gain_one_float)
     delta_tokens_norm, delta_gain_one = first_back(delta_normed_one)
     input_gradient = (delta_residual + delta_tokens_norm).astype(jnp.bfloat16)
 

time: 1810 us -> 1960 us (1.083)
  waiting for transfers between devices: 1130 us -> 1310 us
  starting transfers between devices: 68.4 us -> 34 us
    all_gather x1, waiting for transfers between devices: 0.02 us -> 291 us  [shards(): lax.all_gather(jnp.concatenate([shared_inner.reshape(inner_rows, shared_i...]
    all_to_all x1, waiting for transfers between devices: 258 us -> 0.01 us  [shards(): lax.all_to_all(outgoing, 'expert', split_axis=0, concat_axis=0, tiled=True)]
    reduce_scatter x4, waiting for transfers between devices: 521 us -> 589 us  [reduce_over_expert(): summed = lax.psum_scatter(rows, 'expert', scatter_dimension=0, tiled=True)]
    unnamed x10, waiting for transfers between devices: 0.83 us -> 45.2 us
    all_to_all x1, starting transfers between devices: 53 us -> 19.8 us  [shards(): lax.all_to_all(going_back, 'expert', split_axis=0, concat_axis=0, tiled=T...]
    all_to_all x1, waiting for transfers between devices: 111 us -> 137 us  [shards(): lax.all_to_all(going_back, 'expert', split_axis=0, concat_axis=0, tiled=T...]
  transfers between devices with their start and end apart: 23 -> 23, of which waited for: 11 -> 14; matrix products, arithmetic and copies ran while one was open for 24% -> 21% of each run, Pallas kernels for 0% -> 0%
where the time goes in v7:
time: 1960 us; the launch traced here: 1950 us
  waiting for transfers between devices  1310 us (67%)
  matrix products  243 us (12%)
  local copies, waits for them, and re-layouts  184 us (9%)
  other arithmetic  166 us (8%)
  starting transfers between devices  34 us (2%)
    reduce_scatter x4, waiting for transfers between devices, reduce_over_expert(): summed = lax.psum_scatter(rows, 'expert', scatter_dimension=0, tiled=True)  589 us
    all_gather x1, waiting for transfers between devices, shards(): lax.all_gather(jnp.concatenate([shared_inner.reshape(inner_rows, shared_i...  291 us
    all_to_all x1, waiting for transfers between devices, shards(): lax.all_to_all(going_back, 'expert', split_axis=0, concat_axis=0, tiled=T...  137 us
    all_gather x1, waiting for transfers between devices, shards(): lax.all_gather(jnp.concatenate([query_weight, output_weight.T], axis=1),...  110 us
    dot_general x10, matrix products, matmul(): return jnp.dot(left_side, right_side, preferred_element_type=jnp.float32)  62.4 us
    all_gather x1, waiting for transfers between devices, shards(): up_full = lax.all_gather(latent_up, ALL, axis=0, tiled=True)  56.2 us
    all_gather x1, waiting for transfers between devices, shards(): lax.all_gather(jnp.concatenate([latent_down, small_local], axis=0), ALL,...  53.6 us
    convert_element_type x6, other arithmetic, pair_total(): return (mine + arrived.astype(jnp.float32)).astype(jnp.bfloat16)  48.9 us
  transfers between devices with their start and end apart: 23, of which 14 were waited for; matrix products, arithmetic and copies ran while one was open for 21% of the time, Pallas kernels for 0%

profile of v7, /device:TPU:0, one launch (start us, length us, event | category | flops | bytes accessed | tf_op | source)
XLA Modules:
  0.0 1953.8 jit_solution(2915364573437374996)
XLA Ops:
  19.7 53.6 %all-gather.14.cloned.1.call-done = bf16[32,67,576]{2,1,0:T(8,128)(2,1)} async-done(((bf16[1,67,576]{2,1,0:T(8,128)(2,1)}), bf16[32,67,576]{2,1,0:T(8,128)(2,1)}) %all-gather.14.cloned.1.call-update) | async-done | bytes 2469904 | tf_op jit(solution)/shard_map/all_gather | solution.py:150
  80.5 56.2 %all-gather.8.cloned.1.call-done = bf16[512,4096]{1,0:T(8,128)(2,1)} async-done(((bf16[16,4096]{1,0:T(8,128)(2,1)}), bf16[512,4096]{1,0:T(8,128)(2,1)}) %all-gather.8.cloned.1.call-update) | async-done | bytes 4194320 | tf_op jit(solution)/shard_map/all_gather | solution.py:169
  149.4 6.7 gather_fusion.1
  162.9 109.8 %all-gather.10.cloned.1.call-done = bf16[2048,5120]{1,0:T(8,128)(2,1)} async-done(((bf16[64,5120]{1,0:T(8,128)(2,1)}), bf16[2048,5120]{1,0:T(8,128)(2,1)}) %all-gather.10.cloned.1.call-update) | async-done | bytes 20971536 | tf_op jit(solution)/shard_map/all_gather | solution.py:164
  272.7 8.1 fusion.7
  284.1 7.3 multiply_reduce_fusion.8
  292.1 6.0 gather_fusion
  298.5 5.1 gather_fusion.3
  319.2 6.2 pad_maximum_fusion.2
  330.1 291.2 %all-gather.12.cloned.1.call-done = bf16[6144,2816]{1,0:T(8,128)(2,1)} async-done(((bf16[192,2816]{1,0:T(8,128)(2,1)}), bf16[6144,2816]{1,0:T(8,128)(2,1)}) %all-gather.12.cloned.1.call-update) | async-done | bytes 34603024 | tf_op jit(solution)/shard_map/all_gather | solution.py:171
  621.3 18.9 fusion.152
  640.2 6.0 fusion.160
  646.8 8.9 convolution_bitcast_fusion
  655.7 7.2 fusion.55
  662.9 9.8 fusion.161
  672.7 9.4 fusion.162
  682.1 34.1 %pad_maximum_fusion = f32[2,16,2,64,2816]{4,3,0,2,1:T(8,128)} fusion(f32[1,16,2,64,2816]{4,3,0,2,1:T(8,128)} %bitcast.348, f32[1,16,2,64,2816]{4,3,0,2,1:T(8,128)} %bitcast.347), kind=kLoop, calls=%fused_computation.7 | loop fusion | flops 11534336 | bytes 92274688 | tf_op jit(solution)/shard_map/stack | solution.py:275
  716.2 12.8 fusion.2
  729.2 9.3 fusion.163
  738.6 7.5 fusion.16
  746.9 9.0 collective-permute-done.2
  755.9 10.0 fusion.4
  765.8 12.9 fusion
  778.8 6.7 pad_maximum_fusion.1
  789.6 10.7 fusion.135
  800.3 6.0 fusion.35
  806.4 12.0 fusion.164
  819.3 8.1 fusion.60
  827.4 9.4 fusion.81
  836.9 7.8 multiply_bitcast_fusion
  844.7 9.5 add_convert_fusion
  854.2 9.4 fusion.10
  863.6 6.3 pad_maximum_fusion.3
  869.8 19.8 %all-to-all-start.1 = ((bf16[16,2,64,2048]{3,2,1,0:T(8,128)(2,1)}), bf16[16,2,64,2048]{3,2,1,0:T(8,128)(2,1)}, u32[]{:S(2)}, u32[]{:S(2)}) async-start(bf16[16,2,64,2048]{3,2,1,0:T(8,128)(2,1)} %pad_maximum_fusion.3), calls=%async_computation.1 | async-start | bytes 16777216 | tf_op jit(solution)/shard_map/all_to_all | solution.py:334
  894.1 8.6 mul.559
  902.7 9.1 fusion.165
  911.9 136.9 %all-to-all-done.1 = bf16[16,2,64,2048]{3,2,1,0:T(8,128)(2,1)} async-done(((bf16[16,2,64,2048]{3,2,1,0:T(8,128)(2,1)}), bf16[16,2,64,2048]{3,2,1,0:T(8,128)(2,1)}, u32[]{:S(2)}, u32[]{:S(2)}) %all-to-all-start.1) | async-done | bytes 8388640 | tf_op jit(solution)/shard_map/all_to_all | solution.py:334
  1048.8 6.0 fusion.153
  1054.8 9.1 gather_fusion.4
  1063.9 9.9 gather_fusion.5
  1073.8 7.3 select_convert_fusion
  1081.1 7.9 reshape.603
  1089.0 7.5 multiply_reduce_fusion
  1100.9 8.0 reshape.604
  1108.9 7.2 reduce_sum.196
  1116.2 9.0 fusion.40
  1127.5 7.2 multiply_reduce_fusion.3
  1135.7 5.6 fusion.41
  1171.4 7.5 fusion.5
  1195.3 5.8 copy-done.1
  1211.3 8.3 fusion.9
  1222.8 11.3 fusion.167
  1234.1 5.5 fusion.15
  1239.9 10.1 collective-permute-done.7
  1250.0 11.4 fusion.1
  1263.3 9.1 convert_bitcast_fusion
  1272.7 6.3 convolution_convert_fusion.1
  1279.4 6.7 collective-permute-done.11
  1291.1 9.1 fusion.3
  1300.1 43.8 %reduce-scatter.16.cloned.1.call-done = bf16[72,576]{1,0:T(8,128)(2,1)} async-done(((bf16[1152,576]{1,0:T(8,128)(2,1)}), bf16[72,576]{1,0:T(8,128)(2,1)}) %reduce-scatter.16.cloned.1.call-update) | async-done | bytes 82960
  1348.7 77.7 %reduce-scatter.10.cloned.1.call-done = bf16[16,4096]{1,0:T(8,128)(2,1)} async-done(((bf16[256,4096]{1,0:T(8,128)(2,1)}), bf16[16,4096]{1,0:T(8,128)(2,1)}) %reduce-scatter.10.cloned.1.call-update) | async-done | bytes 131088 | tf_op jit(solution)/shard_map/reduce_scatter | solution.py:87
  1428.1 92.5 %reduce-scatter.12.cloned.1.call-done = bf16[64,2048]{1,0:T(8,128)(2,1)} async-done(((bf16[1024,2048]{1,0:T(8,128)(2,1)}), bf16[64,2048]{1,0:T(8,128)(2,1)}) %reduce-scatter.12.cloned.1.call-update) | async-done | bytes 262160 | tf_op jit(solution)/shard_map/reduce_scatter | solution.py:87
  1522.4 270.5 %reduce-scatter.14.cloned.1.call-done = bf16[192,2816]{1,0:T(8,128)(2,1)} async-done(((bf16[3072,2816]{1,0:T(8,128)(2,1)}), bf16[192,2816]{1,0:T(8,128)(2,1)}) %reduce-scatter.14.cloned.1.call-update) | async-done | bytes 1081360 | tf_op jit(solution)/shard_map/reduce_scatter | solution.py:87
  1796.6 148.5 %reduce-scatter.8.cloned.1.call-done = bf16[64,3072]{1,0:T(8,128)(2,1)} async-done(((bf16[1024,3072]{1,0:T(8,128)(2,1)}), bf16[64,3072]{1,0:T(8,128)(2,1)}) %reduce-scatter.8.cloned.1.call-update) | async-done | bytes 393232 | tf_op jit(solution)/shard_map/reduce_scatter | solution.py:87
  (445 shorter events, 162.6 us)
Async XLA Ops:
  7.2 9.8 copy-start.81
  7.2 66.1 %all-gather.14.cloned.1.call-start = ((), (), s32[]{:S(2)}) async-start(), calls=%async_computation.14 | async-start | bytes 3041280 | tf_op jit(solution)/shard_map/all_gather | solution.py:150
  11.9 124.9 %all-gather.8.cloned.1.call-start = ((), (), s32[]{:S(2)}) async-start(), calls=%async_computation.7 | async-start | bytes 4325376 | tf_op jit(solution)/shard_map/all_gather | solution.py:169
  12.6 260.1 %all-gather.10.cloned.1.call-start = ((), (), s32[]{:S(2)}) async-start(), calls=%async_computation.8 | async-start | bytes 21626880 | tf_op jit(solution)/shard_map/all_gather | solution.py:164
  14.6 606.6 %all-gather.12.cloned.1.call-start = ((), (), s32[]{:S(2)}) async-start(), calls=%async_computation.13 | async-start | bytes 35684352 | tf_op jit(solution)/shard_map/all_gather | solution.py:171
  17.4 127.5 %copy-start.82 = (s32[768]{0:T(1024)}, s32[768]{0:T(1024)S(1)}, u32[]{:S(2)}) copy-start(s32[768]{0:T(1024)S(1)} %eq.59) | copy-start | bytes 9220
  19.4 60.7 %copy-start.98 = (f32[32]{0:T(128)}, f32[32]{0:T(128)S(1)}, u32[]{:S(2)}) copy-start(f32[32]{0:T(128)S(1)} %multiply_power_fusion) | copy-start | bytes 388
  19.5 60.7 %copy-start.100 = (f32[128]{0:T(128)}, f32[128]{0:T(128)S(1)}, u32[]{:S(2)}) copy-start(f32[128]{0:T(128)S(1)} %get-tuple-element.130) | copy-start | bytes 1540
  19.7 57.1 %copy-start.102 = (f32[128]{0:T(128)}, f32[128]{0:T(128)S(1)}, u32[]{:S(2)}) copy-start(f32[128]{0:T(128)S(1)} %fusion.75) | copy-start | bytes 1540
  19.7 253.1 %copy-start.88 = (f32[128]{0:T(128)}, f32[128]{0:T(128)S(1)}, u32[]{:S(2)}) copy-start(f32[128]{0:T(128)S(1)} %fusion.121) | copy-start | bytes 1540
  74.6 198.1 %copy-start.65 = (f32[2048]{0:T(1024)}, f32[2048]{0:T(1024)S(1)}, u32[]{:S(2)}) copy-start(f32[2048]{0:T(1024)S(1)} %reshape.600) | copy-start | bytes 24580
  80.1 61.6 %copy-start.96 = (f32[128]{0:T(128)}, f32[128]{0:T(128)S(1)}, u32[]{:S(2)}) copy-start(f32[128]{0:T(128)S(1)} %fusion.122) | copy-start | bytes 1540
  80.3 200.6 %copy-start.73 = (f32[128,32]{0,1:T(8,128)}, f32[128,32]{0,1:T(8,128)S(1)}, u32[]{:S(2)}) copy-start(f32[128,32]{0,1:T(8,128)S(1)} %get-tuple-element.116) | copy-start | bytes 49156
  80.3 201.7 %copy-start.77 = (bf16[128,32]{0,1:T(8,128)(2,1)}, bf16[128,32]{0,1:T(8,128)(2,1)S(1)}, u32[]{:S(2)}) copy-start(bf16[128,32]{0,1:T(8,128)(2,1)S(1)} %get-tuple-element.118) | copy-start | bytes 24580
  80.3 201.7 %copy-start.79 = (bf16[128,32]{0,1:T(8,128)(2,1)}, bf16[128,32]{0,1:T(8,128)(2,1)S(1)}, u32[]{:S(2)}) copy-start(bf16[128,32]{0,1:T(8,128)(2,1)S(1)} %get-tuple-element.119) | copy-start | bytes 24580
  80.5 61.2 %copy-start.53 = (bf16[128,512]{0,1:T(8,128)(2,1)}, bf16[128,512]{0,1:T(8,128)(2,1)S(1)}, u32[]{:S(2)}) copy-start(bf16[128,512]{0,1:T(8,128)(2,1)S(1)} %multiply_convert_fusion.8) | copy-start | bytes 393220
  80.5 68.8 %copy-start.24 = (bf16[128,2048]{1,0:T(8,128)(2,1)S(1)}, bf16[128,2048]{1,0:T(8,128)(2,1)}, u32[]{:S(2)}) copy-start(bf16[128,2048]{1,0:T(8,128)(2,1)} %param.18) | copy-start | bytes 1572868
  141.7 16.3 collective-permute-start
  156.3 135.3 %copy-start.75 = (f32[2048]{0:T(1024)}, f32[2048]{0:T(1024)S(1)}, u32[]{:S(2)}) copy-start(f32[2048]{0:T(1024)S(1)} %reshape.602) | copy-start | bytes 24580
  158.0 125.3 %copy-start.5 = (bf16[128,16,256]{2,0,1:T(8,128)(2,1)}, bf16[128,16,256]{2,0,1:T(8,128)(2,1)S(1)}, u32[]{:S(2)}) copy-start(bf16[128,16,256]{2,0,1:T(8,128)(2,1)S(1)} %copy.144) | copy-start | bytes 3145732
  162.2 121.2 %copy-start.7 = (bf16[128,16,256]{2,0,1:T(8,128)(2,1)}, bf16[128,16,256]{2,0,1:T(8,128)(2,1)S(1)}, u32[]{:S(2)}) copy-start(bf16[128,16,256]{2,0,1:T(8,128)(2,1)S(1)} %copy.143) | copy-start | bytes 3145732
  162.9 119.1 %copy-start.71 = (bf16[128,64]{0,1:T(8,128)(2,1)}, bf16[128,64]{0,1:T(8,128)(2,1)S(1)}, u32[]{:S(2)}) copy-start(bf16[128,64]{0,1:T(8,128)(2,1)S(1)} %slice.248) | copy-start | bytes 49156
  292.1 380.6 %copy-start.11 = (bf16[128,2048]{1,0:T(8,128)(2,1)}, bf16[128,2048]{1,0:T(8,128)(2,1)S(1)}, u32[]{:S(2)}) copy-start(bf16[128,2048]{1,0:T(8,128)(2,1)S(1)} %multiply_convert_fusion.7) | copy-start | bytes 1572868
  325.4 460.2 %all-to-all-start = ((bf16[16,2,64,2048]{3,2,1,0:T(8,128)(2,1)}), bf16[16,2,64,2048]{3,2,1,0:T(8,128)(2,1)}, u32[]{:S(2)}, u32[]{:S(2)}) async-start(bf16[16,2,64,2048]{3,2,1,0:T(8,128)(2,1)} %pad_maximum_fusion.2), calls=%async_computation | async-start | bytes 16777216 | tf_op jit(solution)/shard_map/all_to_all | solution.py:257
  640.2 15.5 slice-start.5
  640.2 15.5 slice-start.6
  662.9 9.8 copy-start.47
  662.9 9.8 copy-start.49
  716.2 13.0 copy-start.25
  716.2 13.0 copy-start.42
  729.0 36.9 %collective-permute-start.1 = (bf16[16,128,2816]{2,1,0:T(8,128)(2,1)}, bf16[16,128,2816]{2,1,0:T(8,128)(2,1)}, u32[]{:S(2)}, u32[]{:S(2)}) collective-permute-start(bf16[16,128,2816]{2,1,0:T(8,128)(2,1)} %fusion.2), channel_id=1, source_target_pairs={{0,1},{1,0},{2,3},{3,2},{4,5},{5,4},{6,7},{7,6},{8,9},{9,8},{10,11... | collective-permute-start | bytes 34603016 | tf_op jit(solution)/shard_map/ppermute | solution.py:74
  746.1 9.8 collective-permute-start.2
  746.4 60.0 %collective-permute-start.3 = (bf16[2,2048,704]{1,2,0:T(8,128)(2,1)}, bf16[2,2048,704]{1,2,0:T(8,128)(2,1)}, u32[]{:S(2)}, u32[]{:S(2)}) collective-permute-start(bf16[2,2048,704]{1,2,0:T(8,128)(2,1)} %bitcast.39), channel_id=1, source_target_pairs={{0,1},{1,0},{2,3},{3,2},{4,5},{5,4},{6,7},{7,6},{8,9},{9,8},{10,11... | collective-permute-start | bytes 17301512 | tf_op jit(solution)/shard_map/ppermute | solution.py:74
  746.6 90.3 %collective-permute-start.4 = (bf16[704,2048]{1,0:T(8,128)(2,1)}, bf16[704,2048]{1,0:T(8,128)(2,1)}, u32[]{:S(2)}, u32[]{:S(2)}) collective-permute-start(bf16[704,2048]{1,0:T(8,128)(2,1)} %bitcast.41), channel_id=1, source_target_pairs={{0,1},{1,0},{2,3},{3,2},{4,5},{5,4},{6,7},{7,6},{8,9},{9,8},{10,11... | collective-permute-start | bytes 8650760 | tf_op jit(solution)/shard_map/ppermute | solution.py:74
  765.8 13.0 copy-start.15
  789.6 16.8 copy-start.38
  789.6 47.3 %copy-start.40 = (bf16[16,1,64,2048]{3,2,1,0:T(8,128)(2,1)}, bf16[16,1,64,2048]{3,2,1,0:T(8,128)(2,1)S(1)}, u32[]{:S(2)}) copy-start(bf16[16,1,64,2048]{3,2,1,0:T(8,128)(2,1)S(1)} %get-tuple-element.88) | copy-start | bytes 12582916
  806.3 21.1 %copy-start.108 = (f32[1024,1,704]{0,2,1:T(8,128)}, f32[1024,1,704]{0,2,1:T(8,128)S(1)}, u32[]{:S(2)}) copy-start(f32[1024,1,704]{0,2,1:T(8,128)S(1)} %get-tuple-element.83) | copy-start | bytes 8650756
  806.3 21.1 %copy-start.110 = (f32[1024,1,704]{0,2,1:T(8,128)}, f32[1024,1,704]{0,2,1:T(8,128)S(1)}, u32[]{:S(2)}) copy-start(f32[1024,1,704]{0,2,1:T(8,128)S(1)} %get-tuple-element.84) | copy-start | bytes 8650756
  819.3 17.6 slice-start.8
  827.4 9.5 slice-start.9
  827.4 17.3 slice-start.10
  844.7 9.5 copy-start.44
  844.7 9.5 copy-start.46
  869.8 179.0 %all-to-all-start.1 = ((bf16[16,2,64,2048]{3,2,1,0:T(8,128)(2,1)}), bf16[16,2,64,2048]{3,2,1,0:T(8,128)(2,1)}, u32[]{:S(2)}, u32[]{:S(2)}) async-start(bf16[16,2,64,2048]{3,2,1,0:T(8,128)(2,1)} %pad_maximum_fusion.3), calls=%async_computation.1 | async-start | bytes 16777216 | tf_op jit(solution)/shard_map/all_to_all | solution.py:334
  889.6 454.3 %reduce-scatter.16.cloned.1.call-start = ((), (), s32[]{:S(2)}) async-start(), calls=%async_computation.15 | async-start | bytes 1566720
  1108.9 18.5 slice-start.2
  1116.1 11.3 slice-start.3
  1116.1 11.3 slice-start.4
  1152.2 8.2 collective-permute-start.5
  1184.6 5.1 collective-permute-start.6
  1189.6 14.2 collective-permute-start.8
  1192.6 233.9 %reduce-scatter.10.cloned.1.call-start = ((), (), s32[]{:S(2)}) async-start(), calls=%async_computation.10 | async-start | bytes 2228224 | tf_op jit(solution)/shard_map/reduce_scatter | solution.py:87
  1203.8 7.5 collective-permute-start.9
  1208.6 312.1 %reduce-scatter.12.cloned.1.call-start = ((), (), s32[]{:S(2)}) async-start(), calls=%async_computation.11 | async-start | bytes 4456448 | tf_op jit(solution)/shard_map/reduce_scatter | solution.py:87
  1219.7 573.3 %reduce-scatter.14.cloned.1.call-start = ((), (), s32[]{:S(2)}) async-start(), calls=%async_computation.12 | async-start | bytes 18382848 | tf_op jit(solution)/shard_map/reduce_scatter | solution.py:87
  1220.4 724.7 %reduce-scatter.8.cloned.1.call-start = ((), (), s32[]{:S(2)}) async-start(), calls=%async_computation.9 | async-start | bytes 6684672 | tf_op jit(solution)/shard_map/reduce_scatter | solution.py:87
  1239.7 10.4 collective-permute-start.7
  1272.4 13.6 copy-start.56
  1272.4 18.6 collective-permute-start.10
  1279.1 12.0 copy-start.39
  1279.1 12.0 copy-start.109
  1279.1 12.0 copy-start.111
  1279.1 7.0 collective-permute-start.11
  (83 other events, 356.9 us)
Sparse Core Ops, SparseCore 0:
  12.0 61.2 all-gather.13
  76.2 60.5 all-gather.7
  140.2 132.5 all-gather.9
  276.1 345.1 all-gather.11
  1192.8 151.0 reduce-scatter.15
  1346.0 80.4 reduce-scatter.9
  1428.8 91.8 reduce-scatter.11
  1526.6 266.3 reduce-scatter.13
  1798.2 146.8 reduce-scatter.7

commit v8 on v7

--- a/solution.py
+++ b/solution.py
@@ -263,7 +263,7 @@
         "tf,df->td", shared_hidden, shared_out_t_full, preferred_element_type=jnp.float32
     )
     delta_shared_outer_t = jnp.einsum(
-        "td,tf->df", cotangent, shared_hidden, preferred_element_type=jnp.float32
+        "td,tf->df", cotangent, shared_hidden, preferred_element_type=jnp.bfloat16
     )
     delta_shared_hidden = jnp.einsum(
         "td,df->tf", cotangent, shared_out_t_full, preferred_element_type=jnp.float32
@@ -274,7 +274,7 @@
     ]
     delta_shared_inner = jnp.stack(
         [
-            jnp.einsum("td,tf->df", normed_two, part, preferred_element_type=jnp.float32)
+            jnp.einsum("td,tf->df", normed_two, part, preferred_element_type=jnp.bfloat16)
             for part in (delta_gate, delta_up)
         ]
     )
@@ -457,7 +457,6 @@
     delta_query_weight = jnp.einsum(
         "td,tc->dc", normed_one, delta_query_raw, preferred_element_type=jnp.float32
     )
-    delta_query_local = scatter_rows(delta_query_weight, experts_all)
     delta_normed_one = jnp.einsum(
         "tc,dc->td", delta_query_raw, query_full, preferred_element_type=jnp.float32
     ) + jnp.einsum("tc,dc->td", delta_down_out, down_full, preferred_element_type=jnp.float32)
@@ -473,23 +472,28 @@
         jnp.broadcast_to(square_sums[None], (devices, 3)),
     ]
     small_packed = jnp.concatenate(small_parts, axis=1)
-    grad_rows = down_rows + -(-small_packed.shape[1] // width)
-    grad_rows = grad_rows + (-grad_rows) % 8
-    small_packed = jnp.concatenate(
+    query_rows = query_weight.shape[0]
+    down_size = latent_down.size
+    extra = jnp.concatenate([delta_latent_down.reshape(devices, -1), small_packed], axis=1)
+    total_rows = query_rows + -(-extra.shape[1] // query_width)
+    total_rows = total_rows + (-total_rows) % 8
+    extra = jnp.concatenate(
         [
-            small_packed,
+            extra,
             jnp.zeros(
-                (devices, (grad_rows - down_rows) * width - small_packed.shape[1]), jnp.float32
+                (devices, (total_rows - query_rows) * query_width - extra.shape[1]), jnp.float32
             ),
         ],
         axis=1,
-    ).reshape(devices, grad_rows - down_rows, width)
-    down_blocks = jnp.concatenate(
-        [delta_latent_down.reshape(devices, down_rows, width), small_packed], axis=1
-    ).reshape(experts_all, shard_count, grad_rows, width)
-    down_local = reduce_over_expert(pair_total(down_blocks))
-    delta_latent_down_local = down_local[:down_rows]
-    small_sum = down_local[down_rows:].reshape(-1)
+    ).reshape(devices, total_rows - query_rows, query_width)
+    query_blocks = jnp.concatenate(
+        [delta_query_weight.reshape(devices, query_rows, query_width), extra], axis=1
+    ).reshape(experts_all, shard_count, total_rows, query_width)
+    query_out = reduce_over_expert(pair_total(query_blocks))
+    delta_query_local = query_out[:query_rows]
+    rest = query_out[query_rows:].reshape(-1)
+    delta_latent_down_local = rest[:down_size].reshape(latent_down.shape)
+    small_sum = rest[down_size:]
     small_cuts = [0]
     for part in small_parts:
         small_cuts.append(small_cuts[-1] + part.shape[1])

time: 1960 us -> 1790 us (0.913)
  waiting for transfers between devices: 1310 us -> 1180 us
  other arithmetic: 166 us -> 133 us
  local copies, waits for them, and re-layouts: 184 us -> 206 us
    reduce_scatter x4, waiting for transfers between devices: 589 us -> 492 us  [reduce_over_expert(): summed = lax.psum_scatter(rows, 'expert', scatter_dimension=0, tiled=True)]
    unnamed x10 -> x8, waiting for transfers between devices: 45.2 us -> 1.47 us
    unnamed x251 -> x246, local copies, waits for them, and re-layouts: 22.1 us -> 48 us
    convert_element_type x5 -> x2, local copies, waits for them, and re-layouts: 30.1 us -> 4.26 us  [pair_total(): arrived = swap_shard(theirs.astype(jnp.bfloat16))]
    another operation x1, other arithmetic: 34.1 us -> 9.12 us  [shards(): jnp.stack([jnp.einsum('td,tf->df', normed_two, part, preferred_element_ty...]
    convert_element_type x6 -> x5, other arithmetic: 48.9 us -> 38.5 us  [pair_total(): return (mine + arrived.astype(jnp.float32)).astype(jnp.bfloat16)]
  transfers between devices with their start and end apart: 23 -> 21, of which waited for: 14 -> 13; matrix products, arithmetic and copies ran while one was open for 21% -> 22% of each run, Pallas kernels for 0% -> 0%
where the time goes in v8:
time: 1790 us; the launch traced here: 1780 us
  waiting for transfers between devices  1180 us (66%)
  matrix products  225 us (13%)
  local copies, waits for them, and re-layouts  206 us (12%)
  other arithmetic  133 us (7%)
  starting transfers between devices  20.9 us (1%)
    reduce_scatter x4, waiting for transfers between devices, reduce_over_expert(): summed = lax.psum_scatter(rows, 'expert', scatter_dimension=0, tiled=True)  492 us
    all_gather x1, waiting for transfers between devices, shards(): lax.all_gather(jnp.concatenate([shared_inner.reshape(inner_rows, shared_i...  288 us
    all_to_all x1, waiting for transfers between devices, shards(): lax.all_to_all(going_back, 'expert', split_axis=0, concat_axis=0, tiled=T...  137 us
    all_gather x1, waiting for transfers between devices, shards(): lax.all_gather(jnp.concatenate([query_weight, output_weight.T], axis=1),...  108 us
    dot_general x10, matrix products, matmul(): return jnp.dot(left_side, right_side, preferred_element_type=jnp.float32)  63.1 us
    all_gather x1, waiting for transfers between devices, shards(): up_full = lax.all_gather(latent_up, ALL, axis=0, tiled=True)  56.4 us
    all_gather x1, waiting for transfers between devices, shards(): lax.all_gather(jnp.concatenate([latent_down, small_local], axis=0), ALL,...  55.7 us
    unnamed x246, local copies, waits for them, and re-layouts  48 us
  transfers between devices with their start and end apart: 21, of which 13 were waited for; matrix products, arithmetic and copies ran while one was open for 22% of the time, Pallas kernels for 0%

profile of v8, /device:TPU:0, one launch (start us, length us, event | category | flops | bytes accessed | tf_op | source)
XLA Modules:
  0.0 1779.9 jit_solution(14553283260046775757)
XLA Ops:
  17.6 55.7 %all-gather.14.cloned.1.call-done = bf16[32,67,576]{2,1,0:T(8,128)(2,1)} async-done(((bf16[1,67,576]{2,1,0:T(8,128)(2,1)}), bf16[32,67,576]{2,1,0:T(8,128)(2,1)}) %all-gather.14.cloned.1.call-update) | async-done | bytes 2469904 | tf_op jit(solution)/shard_map/all_gather | solution.py:150
  80.4 56.4 %all-gather.8.cloned.1.call-done = bf16[512,4096]{1,0:T(8,128)(2,1)} async-done(((bf16[16,4096]{1,0:T(8,128)(2,1)}), bf16[512,4096]{1,0:T(8,128)(2,1)}) %all-gather.8.cloned.1.call-update) | async-done | bytes 4194320 | tf_op jit(solution)/shard_map/all_gather | solution.py:169
  151.6 6.7 gather_fusion.1
  165.1 107.7 %all-gather.10.cloned.1.call-done = bf16[2048,5120]{1,0:T(8,128)(2,1)} async-done(((bf16[64,5120]{1,0:T(8,128)(2,1)}), bf16[2048,5120]{1,0:T(8,128)(2,1)}) %all-gather.10.cloned.1.call-update) | async-done | bytes 20971536 | tf_op jit(solution)/shard_map/all_gather | solution.py:164
  272.8 8.1 fusion.11
  284.4 7.3 multiply_reduce_fusion.8
  293.2 5.1 gather_fusion.3
  303.5 6.0 gather_fusion
  314.2 7.0 multiply_convert_fusion
  321.1 7.6 pad_maximum_fusion.2
  333.5 287.9 %all-gather.12.cloned.1.call-done = bf16[6144,2816]{1,0:T(8,128)(2,1)} async-done(((bf16[192,2816]{1,0:T(8,128)(2,1)}), bf16[6144,2816]{1,0:T(8,128)(2,1)}) %all-gather.12.cloned.1.call-update) | async-done | bytes 34603024 | tf_op jit(solution)/shard_map/all_gather | solution.py:171
  621.4 18.9 %fusion.148 = (bf16[32,64,2816]{2,1,0:T(8,128)(2,1)}, bf16[32,64,2816]{2,1,0:T(8,128)(2,1)}, bf16[32,64,2816]{2,1,0:T(8,128)(2,1)S(1)}) fusion(bf16[32,192,2816]{2,1,0:T(8,128)(2,1)} %bitcast.350), kind=kLoop, calls=%fused_computation.303 | loop fusion | bytes 69206016 | tf_op jit(solution)/shard_map/slice | solution.py:185
  640.4 10.3 convolution_bitcast_fusion
  650.6 4.9 fusion.156
  655.5 9.2 fusion.51
  668.3 5.9 fusion.158
  674.2 9.1 pad_maximum_fusion
  683.4 7.4 dynamic-slice_bitcast_fusion
  704.9 15.8 collective-permute-done.2
  720.7 6.0 fusion.7
  726.7 10.9 fusion
  737.7 6.8 pad_maximum_fusion.1
  748.5 10.8 fusion.131
  759.3 6.0 fusion.32
  765.3 12.0 fusion.160
  778.3 8.5 fusion.56
  786.8 7.0 fusion.77
  793.8 8.3 multiply_bitcast_fusion
  802.2 9.4 add_convert_fusion
  811.6 9.4 fusion.14
  821.0 6.3 pad_maximum_fusion.3
  827.3 8.2 all-to-all-start.1
  840.0 8.5 mul.559
  848.5 9.2 fusion.161
  857.7 137.0 %all-to-all-done.1 = bf16[16,2,64,2048]{3,2,1,0:T(8,128)(2,1)} async-done(((bf16[16,2,64,2048]{3,2,1,0:T(8,128)(2,1)}), bf16[16,2,64,2048]{3,2,1,0:T(8,128)(2,1)}, u32[]{:S(2)}, u32[]{:S(2)}) %all-to-all-start.1) | async-done | bytes 8388640 | tf_op jit(solution)/shard_map/all_to_all | solution.py:334
  994.7 6.1 fusion.149
  1000.8 9.8 gather_fusion.5
  1010.6 9.1 gather_fusion.4
  1024.1 7.3 select_convert_fusion
  1031.4 8.0 reshape.611
  1039.5 6.1 reduce_sum.196
  1045.6 8.5 fusion.37
  1055.3 7.9 reshape.610
  1063.2 6.6 multiply_reduce_fusion
  1069.9 9.7 multiply_reduce_fusion.3
  1080.6 5.6 fusion.38
  1109.5 5.7 copy-done.2
  1125.4 8.3 fusion.13
  1147.7 7.4 fusion.9
  1161.7 6.4 reshape.594
  1168.0 4.9 constant_dynamic-update-slice_fusion
  1180.7 6.4 dynamic-update-slice.6
  1187.0 9.1 copy.204
  1199.6 5.8 fusion.15
  1205.8 12.4 collective-permute-done.6
  1218.1 8.5 fusion.6
  1228.5 9.1 convert_bitcast_fusion
  1238.1 6.4 convolution_convert_fusion.1
  1244.9 6.4 collective-permute-done.10
  1251.2 5.0 add_bitcast_fusion
  1256.3 8.8 fusion.8
  1266.7 64.1 %reduce-scatter.9.cloned.1.call-done = bf16[64,2048]{1,0:T(8,128)(2,1)} async-done(((bf16[1024,2048]{1,0:T(8,128)(2,1)}), bf16[64,2048]{1,0:T(8,128)(2,1)}) %reduce-scatter.9.cloned.1.call-update) | async-done | bytes 262160 | tf_op jit(solution)/shard_map/reduce_scatter | solution.py:87
  1332.6 270.4 %reduce-scatter.11.cloned.1.call-done = bf16[192,2816]{1,0:T(8,128)(2,1)} async-done(((bf16[3072,2816]{1,0:T(8,128)(2,1)}), bf16[192,2816]{1,0:T(8,128)(2,1)}) %reduce-scatter.11.cloned.1.call-update) | async-done | bytes 1081360 | tf_op jit(solution)/shard_map/reduce_scatter | solution.py:87
  1607.6 157.0 %reduce-scatter.5.cloned.1.call-done = bf16[80,3072]{1,0:T(8,128)(2,1)} async-done(((bf16[1280,3072]{1,0:T(8,128)(2,1)}), bf16[80,3072]{1,0:T(8,128)(2,1)}) %reduce-scatter.5.cloned.1.call-update) | async-done | bytes 491536 | tf_op jit(solution)/shard_map/reduce_scatter | solution.py:87
  (431 shorter events, 175.5 us)
Async XLA Ops:
  7.2 9.9 copy-start.82
  7.2 10.2 copy-start.18
  7.2 66.2 %all-gather.14.cloned.1.call-start = ((), (), s32[]{:S(2)}) async-start(), calls=%async_computation.13 | async-start | bytes 3041280 | tf_op jit(solution)/shard_map/all_gather | solution.py:150
  11.9 124.9 %all-gather.8.cloned.1.call-start = ((), (), s32[]{:S(2)}) async-start(), calls=%async_computation.6 | async-start | bytes 4325376 | tf_op jit(solution)/shard_map/all_gather | solution.py:169
  12.7 260.1 %all-gather.10.cloned.1.call-start = ((), (), s32[]{:S(2)}) async-start(), calls=%async_computation.7 | async-start | bytes 21626880 | tf_op jit(solution)/shard_map/all_gather | solution.py:164
  14.7 606.7 %all-gather.12.cloned.1.call-start = ((), (), s32[]{:S(2)}) async-start(), calls=%async_computation.12 | async-start | bytes 35684352 | tf_op jit(solution)/shard_map/all_gather | solution.py:171
  17.2 127.7 %copy-start.64 = (s32[128,6]{1,0:T(8,128)}, s32[128,6]{1,0:T(8,128)S(1)}, u32[]{:S(2)}) copy-start(s32[128,6]{1,0:T(8,128)S(1)} %copy.151) | copy-start | bytes 9220
  17.3 62.3 %copy-start.99 = (f32[32]{0:T(128)}, f32[32]{0:T(128)S(1)}, u32[]{:S(2)}) copy-start(f32[32]{0:T(128)S(1)} %multiply_power_fusion) | copy-start | bytes 388
  17.4 62.3 %copy-start.101 = (f32[128]{0:T(128)}, f32[128]{0:T(128)S(1)}, u32[]{:S(2)}) copy-start(f32[128]{0:T(128)S(1)} %get-tuple-element.130) | copy-start | bytes 1540
  17.6 57.0 %copy-start.103 = (f32[128]{0:T(128)}, f32[128]{0:T(128)S(1)}, u32[]{:S(2)}) copy-start(f32[128]{0:T(128)S(1)} %fusion.71) | copy-start | bytes 1540
  17.6 255.2 %copy-start.89 = (f32[128]{0:T(128)}, f32[128]{0:T(128)S(1)}, u32[]{:S(2)}) copy-start(f32[128]{0:T(128)S(1)} %fusion.117) | copy-start | bytes 1540
  74.8 198.0 %copy-start.66 = (f32[2048]{0:T(1024)}, f32[2048]{0:T(1024)S(1)}, u32[]{:S(2)}) copy-start(f32[2048]{0:T(1024)S(1)} %reshape.605) | copy-start | bytes 24580
  79.6 62.1 %copy-start.105 = (f32[128]{0:T(128)}, f32[128]{0:T(128)S(1)}, u32[]{:S(2)}) copy-start(f32[128]{0:T(128)S(1)} %multiply_reduce_fusion.11) | copy-start | bytes 1540
  79.6 65.4 %copy-start.97 = (f32[128]{0:T(128)}, f32[128]{0:T(128)S(1)}, u32[]{:S(2)}) copy-start(f32[128]{0:T(128)S(1)} %fusion.118) | copy-start | bytes 1540
  80.2 200.7 %copy-start.74 = (f32[128,32]{0,1:T(8,128)}, f32[128,32]{0,1:T(8,128)S(1)}, u32[]{:S(2)}) copy-start(f32[128,32]{0,1:T(8,128)S(1)} %get-tuple-element.116) | copy-start | bytes 49156
  80.2 201.3 %copy-start.78 = (bf16[128,32]{0,1:T(8,128)(2,1)}, bf16[128,32]{0,1:T(8,128)(2,1)S(1)}, u32[]{:S(2)}) copy-start(bf16[128,32]{0,1:T(8,128)(2,1)S(1)} %get-tuple-element.118) | copy-start | bytes 24580
  80.2 201.3 %copy-start.80 = (bf16[128,32]{0,1:T(8,128)(2,1)}, bf16[128,32]{0,1:T(8,128)(2,1)S(1)}, u32[]{:S(2)}) copy-start(bf16[128,32]{0,1:T(8,128)(2,1)S(1)} %get-tuple-element.119) | copy-start | bytes 24580
  80.4 71.1 %copy-start.54 = (bf16[128,512]{0,1:T(8,128)(2,1)}, bf16[128,512]{0,1:T(8,128)(2,1)S(1)}, u32[]{:S(2)}) copy-start(bf16[128,512]{0,1:T(8,128)(2,1)S(1)} %multiply_convert_fusion.8) | copy-start | bytes 393220
  80.4 71.1 %copy-start.24 = (bf16[128,2048]{1,0:T(8,128)(2,1)S(1)}, bf16[128,2048]{1,0:T(8,128)(2,1)}, u32[]{:S(2)}) copy-start(bf16[128,2048]{1,0:T(8,128)(2,1)} %param.18) | copy-start | bytes 1572868
  141.8 18.5 %collective-permute-start = (bf16[128,4160]{0,1:T(8,128)(2,1)}, bf16[128,4160]{0,1:T(8,128)(2,1)}, u32[]{:S(2)}, u32[]{:S(2)}) collective-permute-start(bf16[128,4160]{0,1:T(8,128)(2,1)} %pad_maximum_fusion.6), channel_id=1, source_target_pairs={{0,1},{2,3},{4,5},{6,7},{8,9},{10,11},{12,13},{14,15},{16,17},{18,... | collective-permute-start | bytes 3194888 | tf_op jit(solution)/shard_map/ppermute | solution.py:24
  158.5 133.2 %copy-start.76 = (f32[2048]{0:T(1024)}, f32[2048]{0:T(1024)S(1)}, u32[]{:S(2)}) copy-start(f32[2048]{0:T(1024)S(1)} %reshape.607) | copy-start | bytes 24580
  160.2 122.7 %copy-start.9 = (bf16[128,16,256]{2,0,1:T(8,128)(2,1)}, bf16[128,16,256]{2,0,1:T(8,128)(2,1)S(1)}, u32[]{:S(2)}) copy-start(bf16[128,16,256]{2,0,1:T(8,128)(2,1)S(1)} %copy.143) | copy-start | bytes 3145732
  164.4 118.6 %copy-start.11 = (bf16[128,16,256]{2,0,1:T(8,128)(2,1)}, bf16[128,16,256]{2,0,1:T(8,128)(2,1)S(1)}, u32[]{:S(2)}) copy-start(bf16[128,16,256]{2,0,1:T(8,128)(2,1)S(1)} %copy.142) | copy-start | bytes 3145732
  165.1 116.4 %copy-start.72 = (bf16[128,64]{0,1:T(8,128)(2,1)}, bf16[128,64]{0,1:T(8,128)(2,1)S(1)}, u32[]{:S(2)}) copy-start(bf16[128,64]{0,1:T(8,128)(2,1)S(1)} %slice.260) | copy-start | bytes 49156
  292.3 376.1 %copy-start.7 = (bf16[128,2048]{1,0:T(8,128)(2,1)}, bf16[128,2048]{1,0:T(8,128)(2,1)S(1)}, u32[]{:S(2)}) copy-start(bf16[128,2048]{1,0:T(8,128)(2,1)S(1)} %multiply_convert_fusion.7) | copy-start | bytes 1572868
  298.7 10.7 copy-start.62
  328.8 415.7 %all-to-all-start = ((bf16[16,2,64,2048]{3,2,1,0:T(8,128)(2,1)}), bf16[16,2,64,2048]{3,2,1,0:T(8,128)(2,1)}, u32[]{:S(2)}, u32[]{:S(2)}) async-start(bf16[16,2,64,2048]{3,2,1,0:T(8,128)(2,1)} %pad_maximum_fusion.2), calls=%async_computation | async-start | bytes 16777216 | tf_op jit(solution)/shard_map/all_to_all | solution.py:257
  640.4 10.3 copy-start
  664.7 30.0 %copy-start.42 = (bf16[128,2816]{0,1:T(8,128)(2,1)}, bf16[128,2816]{0,1:T(8,128)(2,1)S(1)}, u32[]{:S(2)}) copy-start(bf16[128,2816]{0,1:T(8,128)(2,1)S(1)} %get-tuple-element.90) | copy-start | bytes 2162692
  683.4 11.1 copy-start.1
  694.5 32.3 %collective-permute-start.1 = (bf16[16,128,2816]{2,1,0:T(8,128)(2,1)}, bf16[16,128,2816]{2,1,0:T(8,128)(2,1)}, u32[]{:S(2)}, u32[]{:S(2)}) collective-permute-start(bf16[16,128,2816]{2,1,0:T(8,128)(2,1)} %dynamic-slice_bitcast_fusion), channel_id=1, source_target_pairs={{0,1},{1,0},{2,3},{3,2},{4,5},{5,4},{6,7},{7,6},{8,9},{9,8},{10,11... | collective-permute-start | bytes 34603016 | tf_op jit(solution)/shard_map/ppermute | solution.py:74
  704.2 16.5 collective-permute-start.2
  704.4 89.4 %collective-permute-start.4 = (bf16[704,2048]{1,0:T(8,128)(2,1)}, bf16[704,2048]{1,0:T(8,128)(2,1)}, u32[]{:S(2)}, u32[]{:S(2)}) collective-permute-start(bf16[704,2048]{1,0:T(8,128)(2,1)} %bitcast.41), channel_id=1, source_target_pairs={{0,1},{1,0},{2,3},{3,2},{4,5},{5,4},{6,7},{7,6},{8,9},{9,8},{10,11... | collective-permute-start | bytes 8650760 | tf_op jit(solution)/shard_map/ppermute | solution.py:74
  704.7 60.6 %collective-permute-start.3 = (bf16[2,2048,704]{1,2,0:T(8,128)(2,1)}, bf16[2,2048,704]{1,2,0:T(8,128)(2,1)}, u32[]{:S(2)}, u32[]{:S(2)}) collective-permute-start(bf16[2,2048,704]{1,2,0:T(8,128)(2,1)} %bitcast.396), channel_id=1, source_target_pairs={{0,1},{1,0},{2,3},{3,2},{4,5},{5,4},{6,7},{7,6},{8,9},{9,8},{10,11... | collective-permute-start | bytes 17301512 | tf_op jit(solution)/shard_map/ppermute | solution.py:74
  748.5 16.8 copy-start.37
  748.5 45.3 %copy-start.39 = (bf16[16,1,64,2048]{3,2,1,0:T(8,128)(2,1)}, bf16[16,1,64,2048]{3,2,1,0:T(8,128)(2,1)S(1)}, u32[]{:S(2)}) copy-start(bf16[16,1,64,2048]{3,2,1,0:T(8,128)(2,1)S(1)} %get-tuple-element.88) | copy-start | bytes 12582916
  765.3 21.5 %copy-start.109 = (f32[1024,1,704]{0,2,1:T(8,128)}, f32[1024,1,704]{0,2,1:T(8,128)S(1)}, u32[]{:S(2)}) copy-start(f32[1024,1,704]{0,2,1:T(8,128)S(1)} %get-tuple-element.83) | copy-start | bytes 8650756
  765.3 21.5 %copy-start.111 = (f32[1024,1,704]{0,2,1:T(8,128)}, f32[1024,1,704]{0,2,1:T(8,128)S(1)}, u32[]{:S(2)}) copy-start(f32[1024,1,704]{0,2,1:T(8,128)S(1)} %get-tuple-element.84) | copy-start | bytes 8650756
  777.4 9.4 slice-start
  786.8 15.3 slice-start.2
  802.2 9.5 copy-start.44
  802.2 9.5 copy-start.46
  827.3 167.4 %all-to-all-start.1 = ((bf16[16,2,64,2048]{3,2,1,0:T(8,128)(2,1)}), bf16[16,2,64,2048]{3,2,1,0:T(8,128)(2,1)}, u32[]{:S(2)}, u32[]{:S(2)}) async-start(bf16[16,2,64,2048]{3,2,1,0:T(8,128)(2,1)} %pad_maximum_fusion.3), calls=%async_computation.1 | async-start | bytes 16777216 | tf_op jit(solution)/shard_map/all_to_all | solution.py:334
  835.6 429.5 %reduce-scatter.7.cloned.1.call-start = ((), (), s32[]{:S(2)}) async-start(), calls=%async_computation.9 | async-start | bytes 2228224 | tf_op jit(solution)/shard_map/reduce_scatter | solution.py:87
  1045.6 8.6 copy-start.21
  1045.6 8.6 copy-start.28
  1045.6 9.7 copy-start.108
  1093.8 4.6 collective-permute-start.5
  1106.8 11.5 collective-permute-start.7
  1117.9 7.5 collective-permute-start.8
  1123.1 207.8 %reduce-scatter.9.cloned.1.call-start = ((), (), s32[]{:S(2)}) async-start(), calls=%async_computation.10 | async-start | bytes 4456448 | tf_op jit(solution)/shard_map/reduce_scatter | solution.py:87
  1133.7 469.2 %reduce-scatter.11.cloned.1.call-start = ((), (), s32[]{:S(2)}) async-start(), calls=%async_computation.11 | async-start | bytes 18382848 | tf_op jit(solution)/shard_map/reduce_scatter | solution.py:87
  1134.5 8.7 copy-start.32
  1134.5 8.7 copy-start.88
  1134.5 8.7 copy-start.98
  1134.5 630.1 %reduce-scatter.5.cloned.1.call-start = ((), (), s32[]{:S(2)}) async-start(), calls=%async_computation.8 | async-start | bytes 8355840 | tf_op jit(solution)/shard_map/reduce_scatter | solution.py:87
  1205.4 12.8 collective-permute-start.6
  1228.5 9.6 copy-start.40
  1237.6 13.6 copy-start.57
  1237.6 18.6 %collective-permute-start.9 = (bf16[2,2048,704]{1,2,0:T(8,128)(2,1)S(1)}, bf16[2,2048,704]{1,2,0:T(8,128)(2,1)S(1)}, u32[]{:S(2)}, u32[]{:S(2)}) collective-permute-start(bf16[2,2048,704]{1,2,0:T(8,128)(2,1)S(1)} %convert_bitcast_fusion), channel_id=1, source_target_pairs={{0,1},{1,0},{2,3},{3,2},{4,5},{5,4},{6,7},{7,6},{8,9},{9,8},{10,11... | collective-permute-start | bytes 17301512 | tf_op jit(solution)/shard_map/ppermute | solution.py:74
  1244.5 11.7 copy-start.38
  1244.5 11.7 copy-start.110
  1244.5 11.7 copy-start.112
  1244.5 6.7 collective-permute-start.10
  (74 other events, 329.9 us)
Sparse Core Ops, SparseCore 0:
  12.0 61.2 all-gather.13
  76.2 60.5 all-gather.7
  140.2 132.5 all-gather.9
  276.1 345.2 all-gather.11
  1123.2 113.6 reduce-scatter.6
  1239.0 91.7 reduce-scatter.8
  1336.8 266.1 reduce-scatter.10
  1608.3 156.2 reduce-scatter.4

commit v9 on v8

--- a/solution.py
+++ b/solution.py
@@ -291,8 +291,12 @@
         (experts_all, shard_count, -1, delta_shared_outer_t.shape[-1])
     )
     ffn_total = jnp.concatenate(
-        [pair_total(inner_grad_blocks), pair_total(outer_grad_blocks)], axis=1
-    )
+        [
+            inner_grad_blocks.reshape((devices, -1) + inner_grad_blocks.shape[3:]),
+            outer_grad_blocks.reshape((devices, -1) + outer_grad_blocks.shape[3:]),
+        ],
+        axis=1,
+    ).astype(jnp.bfloat16)
     incoming, ffn_total = lax.optimization_barrier((incoming, ffn_total))
     arrived = incoming[:, 0].reshape(-1, D)
     delta_arrived = incoming[:, 1].reshape(-1, D)
@@ -370,7 +374,10 @@
     _, second_back = jax.vjp(norm_rows, residual, gain_two_float)
     delta_residual_norm, delta_gain_two = second_back(delta_normed)
     delta_residual = delta_out + delta_residual_norm
-    ffn_local = reduce_over_expert(ffn_total)
+    ffn_local = lax.psum_scatter(
+        ffn_total.reshape((-1,) + ffn_total.shape[2:]), ALL, scatter_dimension=0, tiled=True
+    )
+    ffn_local = ffn_local.astype(jnp.float32)
     delta_shared_inner_local = ffn_local[:inner_rows].reshape(shared_inner.shape)
     delta_shared_outer_local = ffn_local[inner_rows:].T
 

time: 1790 us -> 1880 us (1.050)
  waiting for transfers between devices: 1180 us -> 1250 us
    reduce_scatter x0 -> x1, waiting for transfers between devices: none -> 326 us  [shards(): lax.psum_scatter(ffn_total.reshape((-1,) + ffn_total.shape[2:]), ALL, sca...]
    reduce_scatter x4 -> x3, waiting for transfers between devices: 492 us -> 260 us  [reduce_over_expert(): summed = lax.psum_scatter(rows, 'expert', scatter_dimension=0, tiled=True)]
    ppermute x9 -> x7, waiting for transfers between devices: 36.8 us -> 10.6 us  [swap_shard(): return lax.ppermute(value, 'shard', [(0, 1), (1, 0)])]
    convert_element_type x5 -> x3, other arithmetic: 38.5 us -> 24.5 us  [pair_total(): return (mine + arrived.astype(jnp.float32)).astype(jnp.bfloat16)]
    unnamed x246 -> x256, local copies, waits for them, and re-layouts: 48 us -> 40.5 us
  transfers between devices with their start and end apart: 21 -> 19, of which waited for: 13 -> 11; matrix products, arithmetic and copies ran while one was open for 22% -> 22% of each run, Pallas kernels for 0% -> 0%
where the time goes in v9:
time: 1880 us; the launch traced here: 1870 us
  waiting for transfers between devices  1250 us (66%)
  matrix products  236 us (13%)
  local copies, waits for them, and re-layouts  193 us (10%)
  other arithmetic  143 us (8%)
  starting transfers between devices  33.3 us (2%)
    reduce_scatter x1, waiting for transfers between devices, shards(): lax.psum_scatter(ffn_total.reshape((-1,) + ffn_total.shape[2:]), ALL, sca...  326 us
    all_gather x1, waiting for transfers between devices, shards(): lax.all_gather(jnp.concatenate([shared_inner.reshape(inner_rows, shared_i...  291 us
    reduce_scatter x3, waiting for transfers between devices, reduce_over_expert(): summed = lax.psum_scatter(rows, 'expert', scatter_dimension=0, tiled=True)  260 us
    all_to_all x1, waiting for transfers between devices, shards(): lax.all_to_all(going_back, 'expert', split_axis=0, concat_axis=0, tiled=T...  137 us
    all_gather x1, waiting for transfers between devices, shards(): lax.all_gather(jnp.concatenate([query_weight, output_weight.T], axis=1),...  108 us
    dot_general x10, matrix products, matmul(): return jnp.dot(left_side, right_side, preferred_element_type=jnp.float32)  65.8 us
    all_gather x1, waiting for transfers between devices, shards(): up_full = lax.all_gather(latent_up, ALL, axis=0, tiled=True)  56.4 us
    all_gather x1, waiting for transfers between devices, shards(): lax.all_gather(jnp.concatenate([latent_down, small_local], axis=0), ALL,...  55.7 us
  transfers between devices with their start and end apart: 19, of which 11 were waited for; matrix products, arithmetic and copies ran while one was open for 22% of the time, Pallas kernels for 0%

profile of v9, /device:TPU:0, one launch (start us, length us, event | category | flops | bytes accessed | tf_op | source)
XLA Modules:
  0.0 1867.5 jit_solution(9866638814265494802)
XLA Ops:
  17.6 55.7 %all-gather.14.cloned.1.call-done = bf16[32,67,576]{2,1,0:T(8,128)(2,1)} async-done(((bf16[1,67,576]{2,1,0:T(8,128)(2,1)}), bf16[32,67,576]{2,1,0:T(8,128)(2,1)}) %all-gather.14.cloned.1.call-update) | async-done | bytes 2469904 | tf_op jit(solution)/shard_map/all_gather | solution.py:150
  80.4 56.4 %all-gather.8.cloned.1.call-done = bf16[512,4096]{1,0:T(8,128)(2,1)} async-done(((bf16[16,4096]{1,0:T(8,128)(2,1)}), bf16[512,4096]{1,0:T(8,128)(2,1)}) %all-gather.8.cloned.1.call-update) | async-done | bytes 4194320 | tf_op jit(solution)/shard_map/all_gather | solution.py:169
  151.7 6.7 gather_fusion.1
  165.2 107.7 %all-gather.10.cloned.1.call-done = bf16[2048,5120]{1,0:T(8,128)(2,1)} async-done(((bf16[64,5120]{1,0:T(8,128)(2,1)}), bf16[2048,5120]{1,0:T(8,128)(2,1)}) %all-gather.10.cloned.1.call-update) | async-done | bytes 20971536 | tf_op jit(solution)/shard_map/all_gather | solution.py:164
  272.9 8.1 fusion.9
  283.8 7.5 multiply_reduce_fusion.8
  292.3 5.1 gather_fusion.3
  303.3 6.0 gather_fusion
  313.9 5.4 multiply_convert_fusion
  319.2 6.3 pad_maximum_fusion.2
  325.5 4.8 all-to-all-start
  330.8 290.5 %all-gather.12.cloned.1.call-done = bf16[6144,2816]{1,0:T(8,128)(2,1)} async-done(((bf16[192,2816]{1,0:T(8,128)(2,1)}), bf16[6144,2816]{1,0:T(8,128)(2,1)}) %all-gather.12.cloned.1.call-update) | async-done | bytes 34603024 | tf_op jit(solution)/shard_map/all_gather | solution.py:171
  621.4 18.9 %fusion.146 = (bf16[32,64,2816]{2,1,0:T(8,128)(2,1)}, bf16[32,64,2816]{2,1,0:T(8,128)(2,1)}, bf16[32,64,2816]{2,1,0:T(8,128)(2,1)S(1)}) fusion(bf16[32,192,2816]{2,1,0:T(8,128)(2,1)} %bitcast.338), kind=kLoop, calls=%fused_computation.297 | loop fusion | bytes 69206016 | tf_op jit(solution)/shard_map/slice | solution.py:185
  640.3 6.0 fusion.154
  646.8 8.9 convolution_bitcast_fusion
  655.8 7.2 fusion.49
  663.0 4.8 fusion.155
  667.7 5.9 fusion.156
  673.7 14.6 pad_maximum_fusion.1
  688.3 5.9 fusion.157
  694.2 23.3 %pad_maximum_fusion = bf16[32,192,2816]{2,1,0:T(8,128)(2,1)} fusion(bf16[32,64,2816]{2,1,0:T(8,128)(2,1)} %bitcast.329, bf16[32,128,2816]{2,1,0:T(8,128)(2,1)} %bitcast.326), kind=kLoop, calls=%fused_computation.9 | loop fusion | flops 69206016 | bytes 69206016 | tf_op jit(solution)/shard_map/concatenate | solution.py:293
  721.6 10.5 fusion.129
  732.2 7.6 fusion.30
  739.8 11.0 fusion.158
  751.8 8.8 fusion.54
  760.6 6.9 fusion.75
  767.5 7.6 multiply_bitcast_fusion
  775.2 12.7 add_convert_fusion
  787.9 9.3 fusion.12
  797.3 6.3 pad_maximum_fusion.3
  803.6 19.7 %all-to-all-start.1 = ((bf16[16,2,64,2048]{3,2,1,0:T(8,128)(2,1)}), bf16[16,2,64,2048]{3,2,1,0:T(8,128)(2,1)}, u32[]{:S(2)}, u32[]{:S(2)}) async-start(bf16[16,2,64,2048]{3,2,1,0:T(8,128)(2,1)} %pad_maximum_fusion.3), calls=%async_computation.1 | async-start | bytes 16777216 | tf_op jit(solution)/shard_map/all_to_all | solution.py:338
  827.7 8.3 mul.559
  836.1 9.2 fusion.159
  845.2 137.2 %all-to-all-done.1 = bf16[16,2,64,2048]{3,2,1,0:T(8,128)(2,1)} async-done(((bf16[16,2,64,2048]{3,2,1,0:T(8,128)(2,1)}), bf16[16,2,64,2048]{3,2,1,0:T(8,128)(2,1)}, u32[]{:S(2)}, u32[]{:S(2)}) %all-to-all-start.1) | async-done | bytes 8388640 | tf_op jit(solution)/shard_map/all_to_all | solution.py:338
  982.4 6.1 fusion.147
  988.6 9.8 gather_fusion.5
  998.4 9.1 gather_fusion.4
  1012.0 7.3 select_convert_fusion
  1019.2 8.2 reshape.597
  1027.4 6.1 reduce_sum.196
  1033.6 8.5 fusion.35
  1043.3 7.9 reshape.596
  1051.2 6.6 multiply_reduce_fusion
  1057.8 9.7 multiply_reduce_fusion.3
  1068.6 5.6 fusion.36
  1090.4 8.1 fusion.163
  1102.4 6.2 fusion.18
  1128.6 7.4 fusion.7
  1142.5 6.3 reshape.582
  1153.7 4.9 constant_dynamic-update-slice_fusion
  1166.5 6.2 dynamic-update-slice.6
  1172.7 9.1 copy.200
  1185.3 7.2 fusion.13
  1197.7 8.4 fusion.11
  1210.0 11.4 fusion.5
  1223.3 9.3 convert_bitcast_fusion
  1233.1 6.2 convolution_convert_fusion.1
  1239.6 6.7 collective-permute-done.8
  1246.3 5.0 add_bitcast_fusion
  1251.3 8.8 fusion.6
  1260.2 7.2 reduce-scatter.7.cloned.1.call-done
  1269.0 92.5 %reduce-scatter.9.cloned.1.call-done = bf16[64,2048]{1,0:T(8,128)(2,1)} async-done(((bf16[1024,2048]{1,0:T(8,128)(2,1)}), bf16[64,2048]{1,0:T(8,128)(2,1)}) %reduce-scatter.9.cloned.1.call-update) | async-done | bytes 262160 | tf_op jit(solution)/shard_map/reduce_scatter | solution.py:87
  1363.2 159.9 %reduce-scatter.5.cloned.1.call-done = bf16[80,3072]{1,0:T(8,128)(2,1)} async-done(((bf16[1280,3072]{1,0:T(8,128)(2,1)}), bf16[80,3072]{1,0:T(8,128)(2,1)}) %reduce-scatter.5.cloned.1.call-update) | async-done | bytes 491536 | tf_op jit(solution)/shard_map/reduce_scatter | solution.py:87
  1530.4 326.3 %reduce-scatter.11.cloned.1.call-done = bf16[192,2816]{1,0:T(8,128)(2,1)} async-done(((bf16[6144,2816]{1,0:T(8,128)(2,1)}), bf16[192,2816]{1,0:T(8,128)(2,1)}) %reduce-scatter.11.cloned.1.call-update) | async-done | bytes 1081360 | tf_op jit(solution)/shard_map/reduce_scatter | solution.py:377
  (434 shorter events, 158.5 us)
Async XLA Ops:
  7.2 9.9 copy-start.84
  7.2 10.2 copy-start.18
  7.2 66.2 %all-gather.14.cloned.1.call-start = ((), (), s32[]{:S(2)}) async-start(), calls=%async_computation.13 | async-start | bytes 3041280 | tf_op jit(solution)/shard_map/all_gather | solution.py:150
  11.9 124.9 %all-gather.8.cloned.1.call-start = ((), (), s32[]{:S(2)}) async-start(), calls=%async_computation.6 | async-start | bytes 4325376 | tf_op jit(solution)/shard_map/all_gather | solution.py:169
  12.7 260.2 %all-gather.10.cloned.1.call-start = ((), (), s32[]{:S(2)}) async-start(), calls=%async_computation.7 | async-start | bytes 21626880 | tf_op jit(solution)/shard_map/all_gather | solution.py:164
  14.7 606.7 %all-gather.12.cloned.1.call-start = ((), (), s32[]{:S(2)}) async-start(), calls=%async_computation.12 | async-start | bytes 35684352 | tf_op jit(solution)/shard_map/all_gather | solution.py:171
  17.2 127.8 %copy-start.65 = (s32[128,6]{1,0:T(8,128)}, s32[128,6]{1,0:T(8,128)S(1)}, u32[]{:S(2)}) copy-start(s32[128,6]{1,0:T(8,128)S(1)} %copy.149) | copy-start | bytes 9220
  17.3 62.3 %copy-start.101 = (f32[32]{0:T(128)}, f32[32]{0:T(128)S(1)}, u32[]{:S(2)}) copy-start(f32[32]{0:T(128)S(1)} %multiply_power_fusion) | copy-start | bytes 388
  17.4 62.3 %copy-start.103 = (f32[128]{0:T(128)}, f32[128]{0:T(128)S(1)}, u32[]{:S(2)}) copy-start(f32[128]{0:T(128)S(1)} %get-tuple-element.130) | copy-start | bytes 1540
  17.6 61.9 %copy-start.105 = (f32[128]{0:T(128)}, f32[128]{0:T(128)S(1)}, u32[]{:S(2)}) copy-start(f32[128]{0:T(128)S(1)} %fusion.69) | copy-start | bytes 1540
  17.6 255.3 %copy-start.91 = (f32[128]{0:T(128)}, f32[128]{0:T(128)S(1)}, u32[]{:S(2)}) copy-start(f32[128]{0:T(128)S(1)} %fusion.115) | copy-start | bytes 1540
  74.8 198.0 %copy-start.68 = (f32[2048]{0:T(1024)}, f32[2048]{0:T(1024)S(1)}, u32[]{:S(2)}) copy-start(f32[2048]{0:T(1024)S(1)} %reshape.593) | copy-start | bytes 24580
  79.6 62.1 %copy-start.107 = (f32[128]{0:T(128)}, f32[128]{0:T(128)S(1)}, u32[]{:S(2)}) copy-start(f32[128]{0:T(128)S(1)} %multiply_reduce_fusion.11) | copy-start | bytes 1540
  79.6 62.1 %copy-start.99 = (f32[128]{0:T(128)}, f32[128]{0:T(128)S(1)}, u32[]{:S(2)}) copy-start(f32[128]{0:T(128)S(1)} %fusion.116) | copy-start | bytes 1540
  80.2 200.7 %copy-start.76 = (f32[128,32]{0,1:T(8,128)}, f32[128,32]{0,1:T(8,128)S(1)}, u32[]{:S(2)}) copy-start(f32[128,32]{0,1:T(8,128)S(1)} %get-tuple-element.116) | copy-start | bytes 49156
  80.2 201.3 %copy-start.80 = (bf16[128,32]{0,1:T(8,128)(2,1)}, bf16[128,32]{0,1:T(8,128)(2,1)S(1)}, u32[]{:S(2)}) copy-start(bf16[128,32]{0,1:T(8,128)(2,1)S(1)} %get-tuple-element.118) | copy-start | bytes 24580
  80.2 201.4 %copy-start.82 = (bf16[128,32]{0,1:T(8,128)(2,1)}, bf16[128,32]{0,1:T(8,128)(2,1)S(1)}, u32[]{:S(2)}) copy-start(bf16[128,32]{0,1:T(8,128)(2,1)S(1)} %get-tuple-element.119) | copy-start | bytes 24580
  80.4 61.4 %copy-start.54 = (bf16[128,512]{0,1:T(8,128)(2,1)}, bf16[128,512]{0,1:T(8,128)(2,1)S(1)}, u32[]{:S(2)}) copy-start(bf16[128,512]{0,1:T(8,128)(2,1)S(1)} %multiply_convert_fusion.8) | copy-start | bytes 393220
  80.4 71.2 %copy-start.22 = (bf16[128,2048]{1,0:T(8,128)(2,1)S(1)}, bf16[128,2048]{1,0:T(8,128)(2,1)}, u32[]{:S(2)}) copy-start(bf16[128,2048]{1,0:T(8,128)(2,1)} %param.18) | copy-start | bytes 1572868
  141.8 18.5 collective-permute-start
  158.6 132.8 %copy-start.78 = (f32[2048]{0:T(1024)}, f32[2048]{0:T(1024)S(1)}, u32[]{:S(2)}) copy-start(f32[2048]{0:T(1024)S(1)} %reshape.595) | copy-start | bytes 24580
  160.3 122.7 %copy-start.7 = (bf16[128,16,256]{2,0,1:T(8,128)(2,1)}, bf16[128,16,256]{2,0,1:T(8,128)(2,1)S(1)}, u32[]{:S(2)}) copy-start(bf16[128,16,256]{2,0,1:T(8,128)(2,1)S(1)} %copy.141) | copy-start | bytes 3145732
  164.4 118.5 %copy-start.9 = (bf16[128,16,256]{2,0,1:T(8,128)(2,1)}, bf16[128,16,256]{2,0,1:T(8,128)(2,1)S(1)}, u32[]{:S(2)}) copy-start(bf16[128,16,256]{2,0,1:T(8,128)(2,1)S(1)} %copy.140) | copy-start | bytes 3145732
  165.2 116.4 %copy-start.74 = (bf16[128,64]{0,1:T(8,128)(2,1)}, bf16[128,64]{0,1:T(8,128)(2,1)S(1)}, u32[]{:S(2)}) copy-start(bf16[128,64]{0,1:T(8,128)(2,1)S(1)} %slice.260) | copy-start | bytes 49156
  291.9 375.8 %copy-start.5 = (bf16[128,2048]{1,0:T(8,128)(2,1)}, bf16[128,2048]{1,0:T(8,128)(2,1)S(1)}, u32[]{:S(2)}) copy-start(bf16[128,2048]{1,0:T(8,128)(2,1)S(1)} %multiply_convert_fusion.7) | copy-start | bytes 1572868
  325.5 392.1 %all-to-all-start = ((bf16[16,2,64,2048]{3,2,1,0:T(8,128)(2,1)}), bf16[16,2,64,2048]{3,2,1,0:T(8,128)(2,1)}, u32[]{:S(2)}, u32[]{:S(2)}) async-start(bf16[16,2,64,2048]{3,2,1,0:T(8,128)(2,1)} %pad_maximum_fusion.2), calls=%async_computation | async-start | bytes 16777216 | tf_op jit(solution)/shard_map/all_to_all | solution.py:257
  330.3 437.2 %collective-permute-start.2 = (bf16[704,2048]{1,0:T(8,128)(2,1)}, bf16[704,2048]{1,0:T(8,128)(2,1)}, u32[]{:S(2)}, u32[]{:S(2)}) collective-permute-start(bf16[704,2048]{1,0:T(8,128)(2,1)} %bitcast.35), channel_id=1, source_target_pairs={{0,1},{1,0},{2,3},{3,2},{4,5},{5,4},{6,7},{7,6},{8,9},{9,8},{10,11... | collective-permute-start | bytes 8650760 | tf_op jit(solution)/shard_map/ppermute | solution.py:74
  330.6 409.2 %collective-permute-start.1 = (bf16[2,2048,704]{1,2,0:T(8,128)(2,1)}, bf16[2,2048,704]{1,2,0:T(8,128)(2,1)}, u32[]{:S(2)}, u32[]{:S(2)}) collective-permute-start(bf16[2,2048,704]{1,2,0:T(8,128)(2,1)} %bitcast.384), channel_id=1, source_target_pairs={{0,1},{1,0},{2,3},{3,2},{4,5},{5,4},{6,7},{7,6},{8,9},{9,8},{10,11... | collective-permute-start | bytes 17301512 | tf_op jit(solution)/shard_map/ppermute | solution.py:74
  640.3 15.5 slice-start
  640.3 15.5 slice-start.1
  646.8 8.9 slice-start.2
  646.8 8.9 copy-start.56
  673.7 14.6 copy-start.23
  673.7 14.6 copy-start.42
  721.6 18.2 copy-start.37
  721.6 45.9 %copy-start.39 = (bf16[16,1,64,2048]{3,2,1,0:T(8,128)(2,1)}, bf16[16,1,64,2048]{3,2,1,0:T(8,128)(2,1)S(1)}, u32[]{:S(2)}) copy-start(bf16[16,1,64,2048]{3,2,1,0:T(8,128)(2,1)S(1)} %get-tuple-element.88) | copy-start | bytes 12582916
  739.8 20.8 %copy-start.111 = (f32[1024,1,704]{0,2,1:T(8,128)}, f32[1024,1,704]{0,2,1:T(8,128)S(1)}, u32[]{:S(2)}) copy-start(f32[1024,1,704]{0,2,1:T(8,128)S(1)} %get-tuple-element.83) | copy-start | bytes 8650756
  750.8 9.8 slice-start.3
  751.7 8.8 copy-start.57
  751.7 8.8 slice-start.4
  751.8 8.8 copy-start.113
  751.8 15.8 slice-start.5
  775.2 12.7 copy-start.45
  775.2 12.7 copy-start.47
  803.6 178.9 %all-to-all-start.1 = ((bf16[16,2,64,2048]{3,2,1,0:T(8,128)(2,1)}), bf16[16,2,64,2048]{3,2,1,0:T(8,128)(2,1)}, u32[]{:S(2)}, u32[]{:S(2)}) async-start(bf16[16,2,64,2048]{3,2,1,0:T(8,128)(2,1)} %pad_maximum_fusion.3), calls=%async_computation.1 | async-start | bytes 16777216 | tf_op jit(solution)/shard_map/all_to_all | solution.py:338
  823.3 444.1 %reduce-scatter.7.cloned.1.call-start = ((), (), s32[]{:S(2)}) async-start(), calls=%async_computation.9 | async-start | bytes 2228224 | tf_op jit(solution)/shard_map/reduce_scatter | solution.py:87
  1088.9 26.4 %collective-permute-start.3 = (bf16[128,4160]{0,1:T(8,128)(2,1)}, bf16[128,4160]{0,1:T(8,128)(2,1)}, u32[]{:S(2)}, u32[]{:S(2)}) collective-permute-start(bf16[128,4160]{0,1:T(8,128)(2,1)} %pad_maximum_fusion.7), channel_id=1, source_target_pairs={{1,0},{3,2},{5,4},{7,6},{9,8},{11,10},{13,12},{15,14},{17,16},{19,... | collective-permute-start | bytes 3194888 | tf_op jit(solution)/shard_map/ppermute | solution.py:24
  1102.4 10.3 copy-start.11
  1102.4 10.3 copy-start.13
  1108.6 89.1 %collective-permute-start.6 = (bf16[16,64,2048]{2,1,0:T(8,128)(2,1)}, bf16[16,64,2048]{2,1,0:T(8,128)(2,1)}, u32[]{:S(2)}, u32[]{:S(2)}) collective-permute-start(bf16[16,64,2048]{2,1,0:T(8,128)(2,1)} %fusion.18), channel_id=1, source_target_pairs={{0,1},{1,0},{2,3},{3,2},{4,5},{5,4},{6,7},{7,6},{8,9},{9,8},{10,11... | collective-permute-start | bytes 12582920 | tf_op jit(solution)/shard_map/ppermute | solution.py:74
  1128.2 20.6 %collective-permute-start.5 = (bf16[16,16,4096]{2,1,0:T(8,128)(2,1)}, bf16[16,16,4096]{2,1,0:T(8,128)(2,1)}, u32[]{:S(2)}, u32[]{:S(2)}) collective-permute-start(bf16[16,16,4096]{2,1,0:T(8,128)(2,1)} %fusion.39), channel_id=1, source_target_pairs={{0,1},{1,0},{2,3},{3,2},{4,5},{5,4},{6,7},{7,6},{8,9},{9,8},{10,11... | collective-permute-start | bytes 6291464 | tf_op jit(solution)/shard_map/ppermute | solution.py:74
  1153.6 9.5 copy-start.67
  1153.6 207.8 %reduce-scatter.9.cloned.1.call-start = ((), (), s32[]{:S(2)}) async-start(), calls=%async_computation.10 | async-start | bytes 4456448 | tf_op jit(solution)/shard_map/reduce_scatter | solution.py:87
  1185.2 11.9 copy-start
  1197.2 12.9 collective-permute-start.4
  1206.1 317.0 %reduce-scatter.5.cloned.1.call-start = ((), (), s32[]{:S(2)}) async-start(), calls=%async_computation.8 | async-start | bytes 8355840 | tf_op jit(solution)/shard_map/reduce_scatter | solution.py:87
  1221.4 635.3 %reduce-scatter.11.cloned.1.call-start = ((), (), s32[]{:S(2)}) async-start(), calls=%async_computation.11 | async-start | bytes 35684352 | tf_op jit(solution)/shard_map/reduce_scatter | solution.py:377
  1223.3 9.8 copy-start.40
  1232.6 13.7 copy-start.58
  1232.7 18.6 collective-permute-start.7
  1239.3 12.0 copy-start.38
  1239.3 12.0 copy-start.112
  1239.3 12.0 copy-start.114
  1239.3 7.0 collective-permute-start.8
  (77 other events, 327.8 us)
Sparse Core Ops, SparseCore 0:
  12.0 61.2 all-gather.13
  76.2 60.5 all-gather.7
  140.2 132.5 all-gather.9
  276.2 345.1 all-gather.11
  1153.7 113.5 reduce-scatter.6
  1269.5 91.8 reduce-scatter.8
  1366.8 156.2 reduce-scatter.4
  1529.5 327.1 reduce-scatter.10
